TPU v7x, 128 devices: a whole 4x4x4 slice. The times are simulated.
128 devices in a mesh: seq: 32 (over x, z, core), tp: 4 (over y).
Axes of the slice: x: 4, y: 4, z: 4, core: 2. Of those that a mesh axis runs over, the one named last changes fastest.
Arguments:
- hidden_in: bfloat16 [4, 64, 2048], replicated, may hold values from -8 to 8
- lengths: int32 [64], replicated, may hold values from 2 to 16384, as said below
- request_perm: int32 [64], replicated, may hold values from 0 to 63, each once
- k_cache: bfloat16 [64, 16384, 512], P(None, 'seq', 'tp'), may hold values from -2450 to 2450
- v_cache: bfloat16 [64, 16384, 512], P(None, 'seq', 'tp'), may hold values from -16 to 16
- attn_gain: bfloat16 [2048], replicated, may hold values from 0.5 to 1.5
- w_query: bfloat16 [2048, 2048], P(None, 'tp'), may hold values from -0.125 to 0.125
- w_key: bfloat16 [2048, 512], P(None, 'tp'), may hold values from -2 to 2
- w_value: bfloat16 [2048, 512], P(None, 'tp'), may hold values from -0.5 to 0.5
- w_out: bfloat16 [2048, 2048], P('tp'), may hold values from -0.125 to 0.125
- mlp_gain: bfloat16 [2048], replicated, may hold values from 0.099609375 to 1.8984375
- w_gate: bfloat16 [8192, 2048], P(('seq', 'tp')), may hold values from -0.125 to 0.125
- w_up: bfloat16 [8192, 2048], P(('seq', 'tp')), may hold values from -0.125 to 0.125
- w_down: bfloat16 [8192, 2048], P(('seq', 'tp')), may hold values from -1 to 1
Outputs:
- hidden_out: bfloat16 [4, 64, 2048], replicated
- key_new: bfloat16 [4, 64, 512], P(None, None, 'tp')
- value_new: bfloat16 [4, 64, 512], P(None, None, 'tp')
Inputs may be any that keep to these rules, and one draw needn't show every extreme that they name: `lengths`: some request has exactly 16384 cached positions.
All inputs are finite; a program needn't handle non-finite values.
Results may differ from a plain program's by a relative error of at most 0.014.
The roundings to bfloat16 on the way count: a program that leaves them out, or rounds other values in their place, can miss the bound.
Values may be sent and summed in bfloat16 or wider, within the bound.
No kernel may reach another device: no remote copies, remote signals or barrier semaphores. Data moves between devices by JAX's collectives and lax.ppermute only.
A program may use at most 192 MiB of HBM per device.

v0:
```python
import math

import jax
import jax.numpy as jnp
from jax import lax
from jax.experimental import pallas as pl
from jax.experimental.pallas import tpu as pltpu
from jax.sharding import PartitionSpec as P

H = 32
KVH = 8
HD = 64
S_CAP = 16384


norm_eps = 1e-05
rope_theta = 10000000.0
attn_scale = 0.015625
branch_scale = 0.5
neg_large = -1e30

CORE = ("seq", 1, 2)
ZAX = ("seq", 2, 4)
XAX = ("seq", 8, 4)
YAX = ("tp", 1, 4)
AXIS_SIZE = {"seq": 32, "tp": 4}


def coord(level):
    axis, stride, size = level
    return (lax.axis_index(axis) // stride) % size


def shift_perm(level, d):
    axis, stride, size = level
    pairs = []
    for i in range(AXIS_SIZE[axis]):
        c = (i // stride) % size
        pairs.append((i, i + ((c + d) % size - c) * stride))
    return pairs


def shifted(x, level, d):
    return lax.ppermute(x, level[0], shift_perm(level, d))


def take(x, index):
    return lax.dynamic_index_in_dim(x, index, axis=0, keepdims=False)


def softmax_scatter(level, packed):
    size = level[2]
    c = coord(level)
    parts = [take(packed, c)]
    for d in range(1, size):
        parts.append(shifted(take(packed, (c + d) % size), level, d))
    head_dim = packed.shape[-1] - 2
    top_all = parts[0][..., head_dim]
    for p in parts[1:]:
        top_all = jnp.maximum(top_all, p[..., head_dim])
    total_all = 0.0
    mixed_all = 0.0
    for p in parts:
        factor = jnp.exp(p[..., head_dim] - top_all)
        total_all = total_all + p[..., head_dim + 1] * factor
        mixed_all = mixed_all + p[..., :head_dim] * factor[..., None]
    return jnp.concatenate([mixed_all, top_all[..., None], total_all[..., None]], axis=-1)


def sum_scatter_abs(x, level):
    size = level[2]
    c = coord(level)
    acc = take(x, c)
    for d in range(1, size):
        acc = acc + shifted(take(x, (c + d) % size), level, d)
    return acc


def sum_all_ordered(x, level):
    size = level[2]
    c = coord(level)
    parts = [x] + [shifted(x, level, d) for d in range(1, size)]
    total = None
    for m in range(size):
        part = parts[0]
        for d in range(1, size):
            part = jnp.where((c - d) % size == m, parts[d], part)
        total = part if total is None else total + part
    return total


def gather_rel(x, level):
    size = level[2]
    parts = [x] + [shifted(x, level, d) for d in range(1, size)]
    return jnp.stack(parts, axis=0)


def sum_scatter_rel(x, level):
    size = level[2]
    acc = x[0]
    for d in range(1, size):
        acc = acc + shifted(x[size - d], level, d)
    return acc


def rms_norm(values, gain_vector):
    floats = values.astype(jnp.float32)
    square_mean = jnp.mean(floats * floats, axis=-1, keepdims=True)
    return (floats * lax.rsqrt(square_mean + norm_eps) * gain_vector.astype(jnp.float32)).astype(
        jnp.bfloat16
    )


def rotate(vectors, positions):
    half_size = vectors.shape[-1] // 2
    inverse = jnp.exp(
        jnp.arange(half_size, dtype=jnp.float32) * (-2.0 * math.log(rope_theta) / vectors.shape[-1])
    )
    angles = positions.astype(jnp.float32)[..., None] * inverse
    cosine = jnp.cos(angles)[..., None, :]
    sine = jnp.sin(angles)[..., None, :]
    first_half = vectors[..., :half_size]
    second_half = vectors[..., half_size:]
    return jnp.concatenate(
        [first_half * cosine - second_half * sine, second_half * cosine + first_half * sine],
        axis=-1,
    )


BLOCK_REQ = 8


def cache_kernel(start_ref, len_ref, q_ref, k_ref, v_ref, packed_ref):
    block = pl.program_id(0)
    rows = q_ref.shape[1]
    half = rows // 2
    head_dim = packed_ref.shape[2] - 2
    shard_len = k_ref.shape[1]
    slots = lax.broadcasted_iota(jnp.int32, (1, shard_len), 1)
    for i in range(q_ref.shape[0]):
        r = block * q_ref.shape[0] + i
        rel = slots + start_ref[r]
        rel = jnp.where(rel >= S_CAP, rel - S_CAP, rel)
        live = rel < len_ref[r]
        scores = lax.dot_general(q_ref[i], k_ref[i], (((1,), (1,)), ((), ())),
                                 preferred_element_type=jnp.float32) * attn_scale
        top = jnp.max(jnp.where(live, scores, neg_large), axis=-1, keepdims=True)
        weights = jnp.where(live, jnp.exp(scores - top), 0.0)
        packed_ref[i, :, head_dim:head_dim + 1] = top
        packed_ref[i, :, head_dim + 1:head_dim + 2] = jnp.sum(weights, axis=-1, keepdims=True)
        mixed = jnp.dot(weights.astype(jnp.bfloat16), v_ref[i], preferred_element_type=jnp.float32)
        packed_ref[i, 0:half, 0:head_dim] = mixed[0:half, 0:head_dim]
        packed_ref[i, half:rows, 0:head_dim] = mixed[half:rows, head_dim:2 * head_dim]


def cache_attention(start, lengths, spread, keys, values, head_dim):
    req, rows, width = spread.shape
    shard_len = keys.shape[1]
    grid = (req // BLOCK_REQ,)
    def blk(b, s, l):
        return (b, 0, 0)
    return pl.pallas_call(
        cache_kernel,
        out_shape=jax.ShapeDtypeStruct((req, rows, head_dim + 2), jnp.float32),
        grid_spec=pltpu.PrefetchScalarGridSpec(
            num_scalar_prefetch=2, grid=grid,
            in_specs=[pl.BlockSpec((BLOCK_REQ, rows, width), blk),
                      pl.BlockSpec((BLOCK_REQ, shard_len, width), blk),
                      pl.BlockSpec((BLOCK_REQ, shard_len, width), blk)],
            out_specs=pl.BlockSpec((BLOCK_REQ, rows, head_dim + 2), blk)),
    )(start, lengths, spread, keys, values)


def attend_shard(query_sel, keys_sel, values_sel, lengths_sel, offsets_sel, slot_base):
    step_count, request_count, local_kv, group_size, head_dim = query_sel.shape
    query_rows = jnp.transpose(query_sel, (1, 2, 0, 3, 4)).reshape(
        request_count, local_kv, step_count * group_size, head_dim
    )
    blank = jnp.zeros((request_count, step_count * group_size, head_dim), query_sel.dtype)
    spread = jnp.concatenate(
        [
            jnp.concatenate([query_rows[:, k] if j == k else blank for j in range(local_kv)], axis=-1)
            for k in range(local_kv)
        ],
        axis=1,
    )
    start = (slot_base - offsets_sel) % S_CAP
    return cache_attention(start, lengths_sel, spread, keys_sel, values_sel, head_dim)


def local(
    hidden_in,
    lengths,
    request_perm,
    k_cache,
    v_cache,
    attn_gain,
    w_query,
    w_key,
    w_value,
    w_out,
    mlp_gain,
    w_gate,
    w_up,
    w_down,
):
    step_count, request_count, model_width = hidden_in.shape
    row_total = step_count * request_count
    group_size = H // KVH
    local_kv = k_cache.shape[2] // HD
    local_heads = local_kv * group_size
    shard_len = k_cache.shape[1]
    flat_in = hidden_in.reshape(row_total, model_width)
    normed = rms_norm(flat_in, attn_gain)
    positions = lengths[None, :] + jnp.arange(step_count, dtype=jnp.int32)[:, None]
    query_raw = jnp.dot(normed, w_query, preferred_element_type=jnp.float32).reshape(
        step_count, request_count, local_heads, HD
    )
    key_raw = jnp.dot(normed, w_key, preferred_element_type=jnp.float32).reshape(
        step_count, request_count, local_kv, HD
    )
    value_new = (
        jnp.dot(normed, w_value, preferred_element_type=jnp.float32)
        .astype(jnp.bfloat16)
        .reshape(step_count, request_count, local_kv, HD)
    )
    queries = (
        rotate(query_raw, positions)
        .astype(jnp.bfloat16)
        .reshape(step_count, request_count, local_kv, group_size, HD)
    )
    key_new = rotate(key_raw, positions).astype(jnp.bfloat16)
    offsets = request_perm * S_CAP // request_count
    slot_base = lax.axis_index("seq") * shard_len
    packed = attend_shard(queries, k_cache, v_cache, lengths, offsets, slot_base)

    levels = (CORE, ZAX, XAX)
    packed = packed.reshape((2, 4, 4, -1) + packed.shape[1:])
    for level in levels:
        packed = softmax_scatter(level, packed)
    own_shape = (packed.shape[0], local_kv, step_count, group_size)
    top_s = packed[..., HD].reshape(own_shape)
    total_s = packed[..., HD + 1].reshape(own_shape)
    mixed_s = packed[..., :HD].reshape(own_shape + (HD,))
    own_count = top_s.shape[0]
    first_req = ((coord(CORE) * 4 + coord(ZAX)) * 4 + coord(XAX)) * own_count

    def own(x):
        return lax.dynamic_slice_in_dim(x, first_req, own_count, axis=1)

    queries_own = own(queries)
    key_own = own(key_new)
    value_own = own(value_new)
    causal = jnp.arange(step_count)[None, :] <= jnp.arange(step_count)[:, None]
    causal_full = causal[None, None, :, None, :]
    new_scores = (
        jnp.einsum("trkgd,urkd->rktgu", queries_own, key_own, preferred_element_type=jnp.float32)
        * attn_scale
    )
    top_new = jnp.max(jnp.where(causal_full, new_scores, neg_large), axis=-1)
    top_final = jnp.maximum(top_s, top_new)
    new_weights = jnp.where(causal_full, jnp.exp(new_scores - top_final[..., None]), 0.0)
    new_mixed = jnp.einsum(
        "rktgu,urkd->rktgd",
        new_weights.astype(jnp.bfloat16),
        value_own,
        preferred_element_type=jnp.float32,
    )
    weight_cache = jnp.exp(top_s - top_final)
    denominator = total_s * weight_cache + jnp.sum(new_weights, axis=-1)
    heads = (mixed_s * weight_cache[..., None] + new_mixed) / denominator[..., None]
    heads = (
        jnp.transpose(heads, (2, 0, 1, 3, 4))
        .reshape(step_count * own_count, local_heads * HD)
        .astype(jnp.bfloat16)
    )
    attended_part = jnp.dot(heads, w_out, preferred_element_type=jnp.float32).reshape(
        step_count, own_count, model_width
    )
    attended = sum_all_ordered(attended_part, YAX)
    hidden_own = lax.dynamic_slice_in_dim(hidden_in, first_req, own_count, axis=1)
    residual = (hidden_own.astype(jnp.float32) + branch_scale * attended).astype(jnp.bfloat16)
    normed_mlp = rms_norm(residual, mlp_gain)

    gather_levels = (XAX, ZAX)
    rows = normed_mlp
    for level in gather_levels:
        rows = gather_rel(rows, level)
    halves = (rows, shifted(rows, CORE, 1))
    block_shape = rows.shape[:-1]
    contract_rows = (((1,), (1,)), ((), ()))

    def feed(half_rows):
        flat = half_rows.reshape(-1, model_width)
        gate = lax.dot_general(flat, w_gate, contract_rows, preferred_element_type=jnp.float32)
        up_proj = lax.dot_general(flat, w_up, contract_rows, preferred_element_type=jnp.float32)
        hidden = (jax.nn.silu(gate) * up_proj).astype(jnp.bfloat16)
        return jnp.dot(hidden, w_down, preferred_element_type=jnp.float32).reshape(
            block_shape + (model_width,)
        )

    feed_forward = feed(halves[0]) + shifted(feed(halves[1]), CORE, 1)
    for level in reversed(gather_levels):
        feed_forward = sum_scatter_rel(feed_forward, level)
    feed_forward = sum_all_ordered(feed_forward, YAX)
    output = (residual.astype(jnp.float32) + branch_scale * feed_forward).astype(jnp.bfloat16)

    out_rows = output
    for level in gather_levels:
        out_rows = gather_rel(out_rows, level)
    out_halves = (out_rows, shifted(out_rows, CORE, 1))
    block_rows = out_rows.shape[3]
    half_blocks = [h.reshape(-1, block_rows * model_width) for h in out_halves]
    half_count = half_blocks[0].shape[0]
    dest = jnp.arange(2 * half_count, dtype=jnp.int32)
    member = {}
    for level in (XAX, ZAX, CORE):
        member[level] = dest % level[2]
        dest = dest // level[2]
    step_of = dest % step_count
    source = jnp.zeros_like(dest)
    for level in (CORE, ZAX, XAX):
        size = level[2]
        source = source * size + (coord(level) - member[level]) % size
    source = source * step_count + step_of
    merged = 0.0
    for kc, blocks in enumerate(half_blocks):
        cols = kc * half_count + jnp.arange(half_count, dtype=jnp.int32)
        one_hot = (source[:, None] == cols[None, :]).astype(blocks.dtype)
        merged = merged + jnp.dot(one_hot, blocks, preferred_element_type=jnp.float32)
    hidden_out = merged.astype(jnp.bfloat16).reshape(step_count, request_count, model_width)
    key_out = key_new.reshape(step_count, request_count, local_kv * HD)
    value_out = value_new.reshape(step_count, request_count, local_kv * HD)
    return (hidden_out, key_out, value_out)


def solution(mesh):
    placed = (
        P(),
        P(),
        P(),
        P(None, "seq", "tp"),
        P(None, "seq", "tp"),
        P(),
        P(None, "tp"),
        P(None, "tp"),
        P(None, "tp"),
        P("tp", None),
        P(),
        P(("seq", "tp"), None),
        P(("seq", "tp"), None),
        P(("seq", "tp"), None),
    )
    return jax.shard_map(
        local,
        mesh=mesh,
        in_specs=placed,
        out_specs=(P(), P(None, None, "tp"), P(None, None, "tp")),
        check_vma=False,
    )
```

profile of v0, /device:TPU:1, one launch (start us, length us, event | category | flops | bytes accessed | tf_op | source)
XLA Modules:
  0.0 174.5 jit_solution(5678242580885128129)
XLA Ops:
  3.7 4.0 %copy.91 = bf16[2048,512]{0,1:T(8,128)(2,1)} copy(bf16[2048,512]{1,0:T(8,128)(2,1)} %param.20) | data formatting | bytes 4194304 | tf_op args[6]
  8.1 2.9 %fusion.12 = f32[4,64,8,64]{1,3,2,0:T(8,128)S(1)} fusion(bf16[8,64,2048,1]{2,1,0,3:T(8,128)(2,1)} %bitcast.159, f32[2048]{0:T(1024)S(1)} %convert_element_type.86, f32[4,64]{1,0:T(4,128)S(1)} %add_rsqrt_fusion, bf16[4,64,2048]{2,1,0:T(8,128)(2,1)S(1)} %copy-done.5), kind=kOutput, calls=%fused_computation.21 | convolution fusion | flops 538968064 | bytes 3679232 | tf_op jit(solution)/shard_map/dot_general | solution.py:216
  16.9 20.3 %shard_map.157 = f32[64,32,66]{2,1,0:T(8,128)} custom-call(s32[64]{0:T(128)} %and_select_fusion.start_ref, s32[64]{0:T(128)} %len_ref.1, bf16[64,32,128]{2,1,0:T(8,128)(2,1)} %fusion.14.q_ref, bf16[64,512,128]{2,1,0:T(8,128)(2,1)} %k_ref.1, bf16[64,512,128]{2,1,0:T(8,128)(2,1)} %v_ref.1), custom_call_target="tpu_custom_call" | custom-call | tf_op jit(solution)/shard_map/pallas_call | solution.py:162
  42.8 2.2 %fusion.10 = f32[4,64,2,64]{1,3,2,0:T(8,128)S(1)} fusion(bf16[2,64,2048,1]{2,1,0,3:T(8,128)(2,1)} %bitcast.168, f32[2048]{0:T(1024)S(1)} %convert_element_type.86, f32[4,64]{1,0:T(4,128)S(1)} %add_rsqrt_fusion, bf16[4,64,2048]{2,1,0:T(8,128)(2,1)} %param.14), kind=kOutput, calls=%fused_computation.20 | convolution fusion | flops 136314880 | bytes 1713152 | tf_op jit(solution)/shard_map/dot_general | solution.py:219
  51.3 3.9 %collective-permute-start.3 = (f32[4,2,32,66]{3,2,1,0:T(8,128)S(1)}, f32[4,2,32,66]{3,2,1,0:T(8,128)S(1)}, u32[]{:S(2)}, u32[]{:S(2)}) collective-permute-start(f32[4,2,32,66]{3,2,1,0:T(8,128)S(1)} %get-tuple-element.48), channel_id=1, source_target_pairs={{0,24},{4,28},{8,0},{12,4},{16,8},{20,12},{24,16},{28,20},{32,56},... | collective-permute-start | bytes 202760 | tf_op jit(solution)/shard_map/ppermute | solution.py:44
  56.5 4.4 %collective-permute-done.3 = f32[4,2,32,66]{3,2,1,0:T(8,128)S(1)} collective-permute-done((f32[4,2,32,66]{3,2,1,0:T(8,128)S(1)}, f32[4,2,32,66]{3,2,1,0:T(8,128)S(1)}, u32[]{:S(2)}, u32[]{:S(2)}) %collective-permute-start.3) | collective-permute-done | bytes 67616 | tf_op jit(solution)/shard_map/ppermute | solution.py:44
  61.5 2.8 %collective-permute-done.1 = f32[4,2,32,66]{3,2,1,0:T(8,128)S(1)} collective-permute-done((f32[4,2,32,66]{3,2,1,0:T(8,128)S(1)}, f32[4,2,32,66]{3,2,1,0:T(8,128)S(1)}, u32[]{:S(2)}, u32[]{:S(2)}) %collective-permute-start.1) | collective-permute-done | bytes 67616 | tf_op jit(solution)/shard_map/ppermute | solution.py:44
  65.5 2.5 %collective-permute-start.6 = (f32[2,32,66]{2,1,0:T(8,128)S(1)}, f32[2,32,66]{2,1,0:T(8,128)S(1)}, u32[]{:S(2)}, u32[]{:S(2)}) collective-permute-start(f32[2,32,66]{2,1,0:T(8,128)S(1)} %get-tuple-element.59), channel_id=1, source_target_pairs={{0,96},{4,100},{8,104},{12,108},{16,112},{20,116},{24,120},{28,124... | collective-permute-start | bytes 50696 | tf_op jit(solution)/shard_map/ppermute | solution.py:44
  69.2 3.1 %collective-permute-done.5 = f32[2,32,66]{2,1,0:T(8,128)S(1)} collective-permute-done((f32[2,32,66]{2,1,0:T(8,128)S(1)}, f32[2,32,66]{2,1,0:T(8,128)S(1)}, u32[]{:S(2)}, u32[]{:S(2)}) %collective-permute-start.5) | collective-permute-done | bytes 16928 | tf_op jit(solution)/shard_map/ppermute | solution.py:44
  76.1 2.6 %collective-permute-start.8 = (f32[4,2,2048]{2,0,1:T(4,128)S(1)}, f32[4,2,2048]{2,0,1:T(4,128)S(1)}, u32[]{:S(2)}, u32[]{:S(2)}) collective-permute-start(f32[4,2,2048]{2,0,1:T(4,128)S(1)} %fusion.1), channel_id=1, source_target_pairs={{0,2},{1,3},{2,0},{3,1},{4,6},{5,7},{6,4},{7,5},{8,10},{9,11},{10,... | collective-permute-start | bytes 196616 | tf_op jit(solution)/shard_map/ppermute | solution.py:44
  83.6 2.7 %collective-permute-start.12 = (bf16[4,2,2048]{2,0,1:T(4,128)(2,1)S(1)}, bf16[4,2,2048]{2,0,1:T(4,128)(2,1)S(1)}, u32[]{:S(2)}, u32[]{:S(2)}) collective-permute-start(bf16[4,2,2048]{2,0,1:T(4,128)(2,1)S(1)} %fusion.30), channel_id=1, source_target_pairs={{0,96},{4,100},{8,104},{12,108},{16,112},{20,116},{24,120},{28,124... | collective-permute-start | bytes 98312 | tf_op jit(solution)/shard_map/ppermute | solution.py:44
  88.7 2.7 %collective-permute-start.15 = (bf16[4,4,2,2048]{3,1,2,0:T(4,128)(2,1)S(1)}, bf16[4,4,2,2048]{3,1,2,0:T(4,128)(2,1)S(1)}, u32[]{:S(2)}, u32[]{:S(2)}) collective-permute-start(bf16[4,4,2,2048]{3,1,2,0:T(4,128)(2,1)S(1)} %pad_maximum_fusion.4), channel_id=1, source_target_pairs={{0,24},{4,28},{8,0},{12,4},{16,8},{20,12},{24,16},{28,20},{32,56},... | collective-permute-start | bytes 393224 | tf_op jit(solution)/shard_map/ppermute | solution.py:44
  95.8 6.5 %collective-permute-start.16 = (bf16[4,4,4,2,2048]{4,2,3,1,0:T(4,128)(2,1)S(1)}, bf16[4,4,4,2,2048]{4,2,3,1,0:T(4,128)(2,1)S(1)}, u32[]{:S(2)}, u32[]{:S(2)}) collective-permute-start(bf16[4,4,4,2,2048]{4,2,3,1,0:T(4,128)(2,1)S(1)} %pad_maximum_fusion.1), channel_id=1, source_target_pairs={{0,4},{4,0},{8,12},{12,8},{16,20},{20,16},{24,28},{28,24},{32,36},... | collective-permute-start | bytes 1572872 | tf_op jit(solution)/shard_map/ppermute | solution.py:44
  104.9 2.8 %fusion.57 = f32[128,2048]{1,0:T(8,128)} fusion(bf16[64,2048]{1,0:T(8,128)(2,1)} %param.27, f32[128,64]{0,1:T(8,128)S(1)} %fusion.90, bf16[128,2048]{1,0:T(8,128)(2,1)S(1)} %reshape.396, bf16[64,2048]{1,0:T(8,128)(2,1)} %param.26), kind=kOutput, calls=%fused_computation.147 | convolution fusion | flops 67158016 | bytes 2129920 | tf_op jit(solution)/shard_map/dot_general | solution.py:298
  112.7 2.9 %fusion.6 = f32[128,2048]{1,0:T(8,128)} fusion(bf16[64,2048]{1,0:T(8,128)(2,1)} %param.27, bf16[128,2048]{1,0:T(8,128)(2,1)S(1)} %reshape.394, bf16[64,2048]{1,0:T(8,128)(2,1)} %param.26, f32[128,64]{0,1:T(8,128)S(1)} %fusion.89), kind=kOutput, calls=%fused_computation.13 | convolution fusion | flops 67158016 | bytes 2129920 | tf_op jit(solution)/shard_map/dot_general | solution.py:298
  120.0 2.4 %collective-permute-start.20 = (f32[4,4,2,2048]{3,1,2,0:T(4,128)S(1)}, f32[4,4,2,2048]{3,1,2,0:T(4,128)S(1)}, u32[]{:S(2)}, u32[]{:S(2)}) collective-permute-start(f32[4,4,2,2048]{3,1,2,0:T(4,128)S(1)} %get-tuple-element.43), channel_id=1, source_target_pairs={{0,24},{4,28},{8,0},{12,4},{16,8},{20,12},{24,16},{28,20},{32,56},... | collective-permute-start | bytes 786440 | tf_op jit(solution)/shard_map/ppermute | solution.py:44
  122.7 5.9 %collective-permute-done.18 = f32[4,4,2,2048]{3,1,2,0:T(4,128)S(1)} collective-permute-done((f32[4,4,2,2048]{3,1,2,0:T(4,128)S(1)}, f32[4,4,2,2048]{3,1,2,0:T(4,128)S(1)}, u32[]{:S(2)}, u32[]{:S(2)}) %collective-permute-start.18) | collective-permute-done | bytes 262176 | tf_op jit(solution)/shard_map/ppermute | solution.py:44
  128.7 5.9 %collective-permute-done.19 = f32[4,4,2,2048]{3,1,2,0:T(4,128)S(1)} collective-permute-done((f32[4,4,2,2048]{3,1,2,0:T(4,128)S(1)}, f32[4,4,2,2048]{3,1,2,0:T(4,128)S(1)}, u32[]{:S(2)}, u32[]{:S(2)}) %collective-permute-start.19) | collective-permute-done | bytes 262176 | tf_op jit(solution)/shard_map/ppermute | solution.py:44
  135.3 2.6 %collective-permute-start.23 = (f32[4,2,2048]{2,0,1:T(4,128)S(1)}, f32[4,2,2048]{2,0,1:T(4,128)S(1)}, u32[]{:S(2)}, u32[]{:S(2)}) collective-permute-start(f32[4,2,2048]{2,0,1:T(4,128)S(1)} %get-tuple-element.56), channel_id=1, source_target_pairs={{0,96},{4,100},{8,104},{12,108},{16,112},{20,116},{24,120},{28,124... | collective-permute-start | bytes 196616 | tf_op jit(solution)/shard_map/ppermute | solution.py:44
  139.4 3.3 %collective-permute-done.22 = f32[4,2,2048]{2,0,1:T(4,128)S(1)} collective-permute-done((f32[4,2,2048]{2,0,1:T(4,128)S(1)}, f32[4,2,2048]{2,0,1:T(4,128)S(1)}, u32[]{:S(2)}, u32[]{:S(2)}) %collective-permute-start.22) | collective-permute-done | bytes 65568 | tf_op jit(solution)/shard_map/ppermute | solution.py:44
  142.9 3.4 %collective-permute-start.25 = (f32[4,2,2048]{2,0,1:T(4,128)S(1)}, f32[4,2,2048]{2,0,1:T(4,128)S(1)}, u32[]{:S(2)}, u32[]{:S(2)}) collective-permute-start(f32[4,2,2048]{2,0,1:T(4,128)S(1)} %fusion.34), channel_id=1, source_target_pairs={{0,2},{1,3},{2,0},{3,1},{4,6},{5,7},{6,4},{7,5},{8,10},{9,11},{10,... | collective-permute-start | bytes 196616 | tf_op jit(solution)/shard_map/ppermute | solution.py:44
  155.9 2.4 %collective-permute-start.30 = (bf16[4,4,2,2048]{3,1,2,0:T(4,128)(2,1)S(1)}, bf16[4,4,2,2048]{3,1,2,0:T(4,128)(2,1)S(1)}, u32[]{:S(2)}, u32[]{:S(2)}) collective-permute-start(bf16[4,4,2,2048]{3,1,2,0:T(4,128)(2,1)S(1)} %pad_maximum_fusion.5), channel_id=1, source_target_pairs={{0,8},{4,12},{8,16},{12,20},{16,24},{20,28},{24,0},{28,4},{32,40},... | collective-permute-start | bytes 393224 | tf_op jit(solution)/shard_map/ppermute | solution.py:44
  158.7 2.4 %collective-permute-done.31 = bf16[4,4,2,2048]{3,1,2,0:T(4,128)(2,1)S(1)} collective-permute-done((bf16[4,4,2,2048]{3,1,2,0:T(4,128)(2,1)S(1)}, bf16[4,4,2,2048]{3,1,2,0:T(4,128)(2,1)S(1)}, u32[]{:S(2)}, u32[]{:S(2)}) %collective-permute-start.31) | collective-permute-done | bytes 131104 | tf_op jit(solution)/shard_map/ppermute | solution.py:44
  162.8 7.4 %collective-permute-start.33 = (bf16[4,4,4,2,2048]{4,2,3,1,0:T(4,128)(2,1)S(1)}, bf16[4,4,4,2,2048]{4,2,3,1,0:T(4,128)(2,1)S(1)}, u32[]{:S(2)}, u32[]{:S(2)}) collective-permute-start(bf16[4,4,4,2,2048]{4,2,3,1,0:T(4,128)(2,1)S(1)} %pad_maximum_fusion.2), channel_id=1, source_target_pairs={{0,4},{4,0},{8,12},{12,8},{16,20},{20,16},{24,28},{28,24},{32,36},... | collective-permute-start | bytes 1572872 | tf_op jit(solution)/shard_map/ppermute | solution.py:44
  (175 shorter events, 70.9 us)
Async XLA Ops:
  39.3 9.9 %collective-permute-start = (f32[4,4,2,32,66]{4,3,2,1,0:T(8,128)}, f32[4,4,2,32,66]{4,3,2,1,0:T(8,128)S(1)}, u32[]{:S(2)}, u32[]{:S(2)}) collective-permute-start(f32[4,4,2,32,66]{4,3,2,1,0:T(8,128)} %get-tuple-element.46), channel_id=1, source_target_pairs={{0,4},{4,0},{8,12},{12,8},{16,20},{20,16},{24,28},{28,24},{32,36},... | collective-permute-start | bytes 811016 | tf_op jit(solution)/shard_map/ppermute | solution.py:44
  51.3 9.6 %collective-permute-start.3 = (f32[4,2,32,66]{3,2,1,0:T(8,128)S(1)}, f32[4,2,32,66]{3,2,1,0:T(8,128)S(1)}, u32[]{:S(2)}, u32[]{:S(2)}) collective-permute-start(f32[4,2,32,66]{3,2,1,0:T(8,128)S(1)} %get-tuple-element.48), channel_id=1, source_target_pairs={{0,24},{4,28},{8,0},{12,4},{16,8},{20,12},{24,16},{28,20},{32,56},... | collective-permute-start | bytes 202760 | tf_op jit(solution)/shard_map/ppermute | solution.py:44
  55.2 6.3 %collective-permute-start.2 = (f32[4,2,32,66]{3,2,1,0:T(8,128)S(1)}, f32[4,2,32,66]{3,2,1,0:T(8,128)S(1)}, u32[]{:S(2)}, u32[]{:S(2)}) collective-permute-start(f32[4,2,32,66]{3,2,1,0:T(8,128)S(1)} %get-tuple-element.49), channel_id=1, source_target_pairs={{0,16},{4,20},{8,24},{12,28},{16,0},{20,4},{24,8},{28,12},{32,48},... | collective-permute-start | bytes 202760 | tf_op jit(solution)/shard_map/ppermute | solution.py:44
  55.2 9.1 %collective-permute-start.1 = (f32[4,2,32,66]{3,2,1,0:T(8,128)S(1)}, f32[4,2,32,66]{3,2,1,0:T(8,128)S(1)}, u32[]{:S(2)}, u32[]{:S(2)}) collective-permute-start(f32[4,2,32,66]{3,2,1,0:T(8,128)S(1)} %get-tuple-element.50), channel_id=1, source_target_pairs={{0,8},{4,12},{8,16},{12,20},{16,24},{20,28},{24,0},{28,4},{32,40},... | collective-permute-start | bytes 202760 | tf_op jit(solution)/shard_map/ppermute | solution.py:44
  68.1 4.3 %collective-permute-start.5 = (f32[2,32,66]{2,1,0:T(8,128)S(1)}, f32[2,32,66]{2,1,0:T(8,128)S(1)}, u32[]{:S(2)}, u32[]{:S(2)}) collective-permute-start(f32[2,32,66]{2,1,0:T(8,128)S(1)} %get-tuple-element.60), channel_id=1, source_target_pairs={{0,64},{4,68},{8,72},{12,76},{16,80},{20,84},{24,88},{28,92},{32,9... | collective-permute-start | bytes 50696 | tf_op jit(solution)/shard_map/ppermute | solution.py:44
  74.8 6.1 %collective-permute-start.9 = (f32[4,2,2048]{2,0,1:T(4,128)S(1)}, f32[4,2,2048]{2,0,1:T(4,128)S(1)}, u32[]{:S(2)}, u32[]{:S(2)}) collective-permute-start(f32[4,2,2048]{2,0,1:T(4,128)S(1)} %fusion.1), channel_id=1, source_target_pairs={{0,1},{1,2},{2,3},{3,0},{4,5},{5,6},{6,7},{7,4},{8,9},{9,10},{10,1... | collective-permute-start | bytes 196616 | tf_op jit(solution)/shard_map/ppermute | solution.py:44
  76.1 5.0 %collective-permute-start.8 = (f32[4,2,2048]{2,0,1:T(4,128)S(1)}, f32[4,2,2048]{2,0,1:T(4,128)S(1)}, u32[]{:S(2)}, u32[]{:S(2)}) collective-permute-start(f32[4,2,2048]{2,0,1:T(4,128)S(1)} %fusion.1), channel_id=1, source_target_pairs={{0,2},{1,3},{2,0},{3,1},{4,6},{5,7},{6,4},{7,5},{8,10},{9,11},{10,... | collective-permute-start | bytes 196616 | tf_op jit(solution)/shard_map/ppermute | solution.py:44
  82.4 4.3 %collective-permute-start.11 = (bf16[4,2,2048]{2,0,1:T(4,128)(2,1)S(1)}, bf16[4,2,2048]{2,0,1:T(4,128)(2,1)S(1)}, u32[]{:S(2)}, u32[]{:S(2)}) collective-permute-start(bf16[4,2,2048]{2,0,1:T(4,128)(2,1)S(1)} %fusion.30), channel_id=1, source_target_pairs={{0,64},{4,68},{8,72},{12,76},{16,80},{20,84},{24,88},{28,92},{32,9... | collective-permute-start | bytes 98312 | tf_op jit(solution)/shard_map/ppermute | solution.py:44
  87.7 5.5 %collective-permute-start.14 = (bf16[4,4,2,2048]{3,1,2,0:T(4,128)(2,1)S(1)}, bf16[4,4,2,2048]{3,1,2,0:T(4,128)(2,1)S(1)}, u32[]{:S(2)}, u32[]{:S(2)}) collective-permute-start(bf16[4,4,2,2048]{3,1,2,0:T(4,128)(2,1)S(1)} %pad_maximum_fusion.4), channel_id=1, source_target_pairs={{0,16},{4,20},{8,24},{12,28},{16,0},{20,4},{24,8},{28,12},{32,48},... | collective-permute-start | bytes 393224 | tf_op jit(solution)/shard_map/ppermute | solution.py:44
  88.6 5.9 %collective-permute-start.13 = (bf16[4,4,2,2048]{3,1,2,0:T(4,128)(2,1)S(1)}, bf16[4,4,2,2048]{3,1,2,0:T(4,128)(2,1)S(1)}, u32[]{:S(2)}, u32[]{:S(2)}) collective-permute-start(bf16[4,4,2,2048]{3,1,2,0:T(4,128)(2,1)S(1)} %pad_maximum_fusion.4), channel_id=1, source_target_pairs={{0,8},{4,12},{8,16},{12,20},{16,24},{20,28},{24,0},{28,4},{32,40},... | collective-permute-start | bytes 393224 | tf_op jit(solution)/shard_map/ppermute | solution.py:44
  88.7 5.9 %collective-permute-start.15 = (bf16[4,4,2,2048]{3,1,2,0:T(4,128)(2,1)S(1)}, bf16[4,4,2,2048]{3,1,2,0:T(4,128)(2,1)S(1)}, u32[]{:S(2)}, u32[]{:S(2)}) collective-permute-start(bf16[4,4,2,2048]{3,1,2,0:T(4,128)(2,1)S(1)} %pad_maximum_fusion.4), channel_id=1, source_target_pairs={{0,24},{4,28},{8,0},{12,4},{16,8},{20,12},{24,16},{28,20},{32,56},... | collective-permute-start | bytes 393224 | tf_op jit(solution)/shard_map/ppermute | solution.py:44
  95.8 8.0 %collective-permute-start.16 = (bf16[4,4,4,2,2048]{4,2,3,1,0:T(4,128)(2,1)S(1)}, bf16[4,4,4,2,2048]{4,2,3,1,0:T(4,128)(2,1)S(1)}, u32[]{:S(2)}, u32[]{:S(2)}) collective-permute-start(bf16[4,4,4,2,2048]{4,2,3,1,0:T(4,128)(2,1)S(1)} %pad_maximum_fusion.1), channel_id=1, source_target_pairs={{0,4},{4,0},{8,12},{12,8},{16,20},{20,16},{24,28},{28,24},{32,36},... | collective-permute-start | bytes 1572872 | tf_op jit(solution)/shard_map/ppermute | solution.py:44
  111.3 6.2 %collective-permute-start.17 = (f32[4,4,4,2,2048]{4,2,3,1,0:T(4,128)}, f32[4,4,4,2,2048]{4,2,3,1,0:T(4,128)}, u32[]{:S(2)}, u32[]{:S(2)}) collective-permute-start(f32[4,4,4,2,2048]{4,2,3,1,0:T(4,128)} %copy.103), channel_id=1, source_target_pairs={{0,4},{4,0},{8,12},{12,8},{16,20},{20,16},{24,28},{28,24},{32,36},... | collective-permute-start | bytes 3145736 | tf_op jit(solution)/shard_map/ppermute | solution.py:44
  119.7 9.0 %collective-permute-start.18 = (f32[4,4,2,2048]{3,1,2,0:T(4,128)S(1)}, f32[4,4,2,2048]{3,1,2,0:T(4,128)S(1)}, u32[]{:S(2)}, u32[]{:S(2)}) collective-permute-start(f32[4,4,2,2048]{3,1,2,0:T(4,128)S(1)} %get-tuple-element.42), channel_id=1, source_target_pairs={{0,8},{4,12},{8,16},{12,20},{16,24},{20,28},{24,0},{28,4},{32,40},... | collective-permute-start | bytes 786440 | tf_op jit(solution)/shard_map/ppermute | solution.py:44
  120.0 8.6 %collective-permute-start.20 = (f32[4,4,2,2048]{3,1,2,0:T(4,128)S(1)}, f32[4,4,2,2048]{3,1,2,0:T(4,128)S(1)}, u32[]{:S(2)}, u32[]{:S(2)}) collective-permute-start(f32[4,4,2,2048]{3,1,2,0:T(4,128)S(1)} %get-tuple-element.43), channel_id=1, source_target_pairs={{0,24},{4,28},{8,0},{12,4},{16,8},{20,12},{24,16},{28,20},{32,56},... | collective-permute-start | bytes 786440 | tf_op jit(solution)/shard_map/ppermute | solution.py:44
  122.4 12.2 %collective-permute-start.19 = (f32[4,4,2,2048]{3,1,2,0:T(4,128)S(1)}, f32[4,4,2,2048]{3,1,2,0:T(4,128)S(1)}, u32[]{:S(2)}, u32[]{:S(2)}) collective-permute-start(f32[4,4,2,2048]{3,1,2,0:T(4,128)S(1)} %get-tuple-element.44), channel_id=1, source_target_pairs={{0,16},{4,20},{8,24},{12,28},{16,0},{20,4},{24,8},{28,12},{32,48},... | collective-permute-start | bytes 786440 | tf_op jit(solution)/shard_map/ppermute | solution.py:44
  134.8 4.7 %collective-permute-start.21 = (f32[4,2,2048]{2,0,1:T(4,128)S(1)}, f32[4,2,2048]{2,0,1:T(4,128)S(1)}, u32[]{:S(2)}, u32[]{:S(2)}) collective-permute-start(f32[4,2,2048]{2,0,1:T(4,128)S(1)} %get-tuple-element.55), channel_id=1, source_target_pairs={{0,32},{4,36},{8,40},{12,44},{16,48},{20,52},{24,56},{28,60},{32,6... | collective-permute-start | bytes 196616 | tf_op jit(solution)/shard_map/ppermute | solution.py:44
  137.9 4.9 %collective-permute-start.22 = (f32[4,2,2048]{2,0,1:T(4,128)S(1)}, f32[4,2,2048]{2,0,1:T(4,128)S(1)}, u32[]{:S(2)}, u32[]{:S(2)}) collective-permute-start(f32[4,2,2048]{2,0,1:T(4,128)S(1)} %get-tuple-element.57), channel_id=1, source_target_pairs={{0,64},{4,68},{8,72},{12,76},{16,80},{20,84},{24,88},{28,92},{32,9... | collective-permute-start | bytes 196616 | tf_op jit(solution)/shard_map/ppermute | solution.py:44
  142.8 4.4 %collective-permute-start.26 = (f32[4,2,2048]{2,0,1:T(4,128)S(1)}, f32[4,2,2048]{2,0,1:T(4,128)S(1)}, u32[]{:S(2)}, u32[]{:S(2)}) collective-permute-start(f32[4,2,2048]{2,0,1:T(4,128)S(1)} %fusion.34), channel_id=1, source_target_pairs={{0,1},{1,2},{2,3},{3,0},{4,5},{5,6},{6,7},{7,4},{8,9},{9,10},{10,1... | collective-permute-start | bytes 196616 | tf_op jit(solution)/shard_map/ppermute | solution.py:44
  142.9 5.8 %collective-permute-start.25 = (f32[4,2,2048]{2,0,1:T(4,128)S(1)}, f32[4,2,2048]{2,0,1:T(4,128)S(1)}, u32[]{:S(2)}, u32[]{:S(2)}) collective-permute-start(f32[4,2,2048]{2,0,1:T(4,128)S(1)} %fusion.34), channel_id=1, source_target_pairs={{0,2},{1,3},{2,0},{3,1},{4,6},{5,7},{6,4},{7,5},{8,10},{9,11},{10,... | collective-permute-start | bytes 196616 | tf_op jit(solution)/shard_map/ppermute | solution.py:44
  150.8 4.3 %collective-permute-start.28 = (bf16[4,2,2048]{2,0,1:T(4,128)(2,1)S(1)}, bf16[4,2,2048]{2,0,1:T(4,128)(2,1)S(1)}, u32[]{:S(2)}, u32[]{:S(2)}) collective-permute-start(bf16[4,2,2048]{2,0,1:T(4,128)(2,1)S(1)} %fusion.31), channel_id=1, source_target_pairs={{0,64},{4,68},{8,72},{12,76},{16,80},{20,84},{24,88},{28,92},{32,9... | collective-permute-start | bytes 98312 | tf_op jit(solution)/shard_map/ppermute | solution.py:44
  155.6 5.5 %collective-permute-start.31 = (bf16[4,4,2,2048]{3,1,2,0:T(4,128)(2,1)S(1)}, bf16[4,4,2,2048]{3,1,2,0:T(4,128)(2,1)S(1)}, u32[]{:S(2)}, u32[]{:S(2)}) collective-permute-start(bf16[4,4,2,2048]{3,1,2,0:T(4,128)(2,1)S(1)} %pad_maximum_fusion.5), channel_id=1, source_target_pairs={{0,16},{4,20},{8,24},{12,28},{16,0},{20,4},{24,8},{28,12},{32,48},... | collective-permute-start | bytes 393224 | tf_op jit(solution)/shard_map/ppermute | solution.py:44
  155.9 6.4 %collective-permute-start.30 = (bf16[4,4,2,2048]{3,1,2,0:T(4,128)(2,1)S(1)}, bf16[4,4,2,2048]{3,1,2,0:T(4,128)(2,1)S(1)}, u32[]{:S(2)}, u32[]{:S(2)}) collective-permute-start(bf16[4,4,2,2048]{3,1,2,0:T(4,128)(2,1)S(1)} %pad_maximum_fusion.5), channel_id=1, source_target_pairs={{0,8},{4,12},{8,16},{12,20},{16,24},{20,28},{24,0},{28,4},{32,40},... | collective-permute-start | bytes 393224 | tf_op jit(solution)/shard_map/ppermute | solution.py:44
  162.8 9.3 %collective-permute-start.33 = (bf16[4,4,4,2,2048]{4,2,3,1,0:T(4,128)(2,1)S(1)}, bf16[4,4,4,2,2048]{4,2,3,1,0:T(4,128)(2,1)S(1)}, u32[]{:S(2)}, u32[]{:S(2)}) collective-permute-start(bf16[4,4,4,2,2048]{4,2,3,1,0:T(4,128)(2,1)S(1)} %pad_maximum_fusion.2), channel_id=1, source_target_pairs={{0,4},{4,0},{8,12},{12,8},{16,20},{20,16},{24,28},{28,24},{32,36},... | collective-permute-start | bytes 1572872 | tf_op jit(solution)/shard_map/ppermute | solution.py:44
  (27 other events, 233.1 us)
where the time goes:
time: 175 us
  starting transfers between devices  52 us (30%)
  waiting for transfers between devices  45.1 us (26%)
  local copies, waits for them, and re-layouts  24 us (14%)
  Pallas kernels  20.3 us (12%)
  other arithmetic  16.4 us (9%)
  matrix products  15.2 us (9%)
    ppermute x34, starting transfers between devices, shifted(): return lax.ppermute(x, level[0], shift_perm(level, d))  52 us
    ppermute x34, waiting for transfers between devices, shifted(): return lax.ppermute(x, level[0], shift_perm(level, d))  45.1 us
    pallas_call x1, Pallas kernels, cache_attention(): pl.pallas_call(cache_kernel, out_shape=jax.ShapeDtypeStruct((req, rows, h...  20.3 us
    unnamed x39, local copies, waits for them, and re-layouts  8.03 us
    dot_general x2, matrix products, feed(): jnp.dot(hidden, w_down, preferred_element_type=jnp.float32)  5.75 us
    reshape x3, local copies, waits for them, and re-layouts, feed(): jnp.dot(hidden, w_down, preferred_element_type=jnp.float32)  5.36 us
  transfers between devices with their start and end apart: 34, of which 24 were waited for; matrix products, arithmetic and copies ran while one was open for 10% of the time, Pallas kernels for 0%

commit v1 on v0

--- a/solution.py
+++ b/solution.py
@@ -95,11 +95,11 @@
     return jnp.stack(parts, axis=0)
 
 
-def sum_scatter_rel(x, level):
+def sum_scatter_rel(x, level, wire):
     size = level[2]
     acc = x[0]
     for d in range(1, size):
-        acc = acc + shifted(x[size - d], level, d)
+        acc = acc + shifted(x[size - d].astype(wire), level, d).astype(acc.dtype)
     return acc
 
 
@@ -277,8 +277,10 @@
     attended_part = jnp.dot(heads, w_out, preferred_element_type=jnp.float32).reshape(
         step_count, own_count, model_width
     )
-    attended = sum_all_ordered(attended_part, YAX)
-    hidden_own = lax.dynamic_slice_in_dim(hidden_in, first_req, own_count, axis=1)
+    attended = sum_all_ordered(attended_part.reshape(-1, model_width), YAX)
+    hidden_own = lax.dynamic_slice_in_dim(hidden_in, first_req, own_count, axis=1).reshape(
+        -1, model_width
+    )
     residual = (hidden_own.astype(jnp.float32) + branch_scale * attended).astype(jnp.bfloat16)
     normed_mlp = rms_norm(residual, mlp_gain)
 
@@ -301,7 +303,7 @@
 
     feed_forward = feed(halves[0]) + shifted(feed(halves[1]), CORE, 1)
     for level in reversed(gather_levels):
-        feed_forward = sum_scatter_rel(feed_forward, level)
+        feed_forward = sum_scatter_rel(feed_forward, level, jnp.bfloat16)
     feed_forward = sum_all_ordered(feed_forward, YAX)
     output = (residual.astype(jnp.float32) + branch_scale * feed_forward).astype(jnp.bfloat16)
 
@@ -309,10 +311,12 @@
     for level in gather_levels:
         out_rows = gather_rel(out_rows, level)
     out_halves = (out_rows, shifted(out_rows, CORE, 1))
-    block_rows = out_rows.shape[3]
-    half_blocks = [h.reshape(-1, block_rows * model_width) for h in out_halves]
-    half_count = half_blocks[0].shape[0]
+    own_rows = out_rows.shape[2]
+    half_flat = [h.reshape(-1, model_width) for h in out_halves]
+    half_count = half_flat[0].shape[0]
     dest = jnp.arange(2 * half_count, dtype=jnp.int32)
+    pair = dest % own_count
+    dest = dest // own_count
     member = {}
     for level in (XAX, ZAX, CORE):
         member[level] = dest % level[2]
@@ -322,12 +326,12 @@
     for level in (CORE, ZAX, XAX):
         size = level[2]
         source = source * size + (coord(level) - member[level]) % size
-    source = source * step_count + step_of
+    source = source * own_rows + step_of * own_count + pair
     merged = 0.0
-    for kc, blocks in enumerate(half_blocks):
+    for kc, flat in enumerate(half_flat):
         cols = kc * half_count + jnp.arange(half_count, dtype=jnp.int32)
-        one_hot = (source[:, None] == cols[None, :]).astype(blocks.dtype)
-        merged = merged + jnp.dot(one_hot, blocks, preferred_element_type=jnp.float32)
+        one_hot = (source[:, None] == cols[None, :]).astype(flat.dtype)
+        merged = merged + jnp.dot(one_hot, flat, preferred_element_type=jnp.float32)
     hidden_out = merged.astype(jnp.bfloat16).reshape(step_count, request_count, model_width)
     key_out = key_new.reshape(step_count, request_count, local_kv * HD)
     value_out = value_new.reshape(step_count, request_count, local_kv * HD)

time: 175 us -> 159 us (0.909)
  local copies, waits for them, and re-layouts: 24 us -> 12.8 us
  waiting for transfers between devices: 45.1 us -> 39.6 us
    reshape x6 -> x0, local copies, waits for them, and re-layouts: 6.93 us -> none  [the longest x3 5.36 us: feed(): jnp.dot(hidden, w_down, preferred_element_type=jnp.float32)]
    ppermute x34, waiting for transfers between devices: 45.1 us -> 39.6 us  [shifted(): return lax.ppermute(x, level[0], shift_perm(level, d))]
    add x4 -> x2, other arithmetic: 2.26 us -> 0.06 us  [the longest x1 0.04 us: local(): source = source * own_rows + step_of * own_count + pair]
    another operation x1 -> x3, other arithmetic: 0.15 us -> 1.9 us
    unnamed x39 -> x33, local copies, waits for them, and re-layouts: 8.03 us -> 6.88 us
  transfers between devices with their start and end apart: 34 -> 34, of which waited for: 24 -> 26; matrix products, arithmetic and copies ran while one was open for 10% -> 9% of each run, Pallas kernels for 0% -> 0%
where the time goes in v1:
time: 159 us
  starting transfers between devices  52.5 us (33%)
  waiting for transfers between devices  39.6 us (25%)
  Pallas kernels  20.3 us (13%)
  matrix products  16.7 us (11%)
  other arithmetic  15.6 us (10%)
  local copies, waits for them, and re-layouts  12.8 us (8%)
    ppermute x34, starting transfers between devices, shifted(): return lax.ppermute(x, level[0], shift_perm(level, d))  52.5 us
    ppermute x34, waiting for transfers between devices, shifted(): return lax.ppermute(x, level[0], shift_perm(level, d))  39.6 us
    pallas_call x1, Pallas kernels, cache_attention(): pl.pallas_call(cache_kernel, out_shape=jax.ShapeDtypeStruct((req, rows, h...  20.3 us
    unnamed x33, local copies, waits for them, and re-layouts  6.88 us
    dot_general x2, matrix products, feed(): jnp.dot(hidden, w_down, preferred_element_type=jnp.float32)  5.7 us
  transfers between devices with their start and end apart: 34, of which 26 were waited for; matrix products, arithmetic and copies ran while one was open for 9% of the time, Pallas kernels for 0%

profile of v1, /device:TPU:1, one launch (start us, length us, event | category | flops | bytes accessed | tf_op | source)
XLA Modules:
  0.0 158.9 jit_solution(15764797532163559927)
XLA Ops:
  3.7 4.0 %copy.65 = bf16[2048,512]{0,1:T(8,128)(2,1)} copy(bf16[2048,512]{1,0:T(8,128)(2,1)} %param.20) | data formatting | bytes 4194304 | tf_op args[6]
  8.1 2.9 %fusion.10 = f32[4,64,8,64]{1,3,2,0:T(8,128)S(1)} fusion(bf16[8,64,2048,1]{2,1,0,3:T(8,128)(2,1)} %bitcast.160, f32[2048]{0:T(1024)S(1)} %convert_element_type.131, f32[4,64]{1,0:T(4,128)S(1)} %add_rsqrt_fusion, bf16[4,64,2048]{2,1,0:T(8,128)(2,1)S(1)} %copy-done.5), kind=kOutput, calls=%fused_computation.18 | convolution fusion | flops 538968064 | bytes 3679232 | tf_op jit(solution)/shard_map/dot_general | solution.py:216
  16.8 20.3 %shard_map.157 = f32[64,32,66]{2,1,0:T(8,128)} custom-call(s32[64]{0:T(128)} %and_select_fusion.start_ref, s32[64]{0:T(128)} %len_ref.1, bf16[64,32,128]{2,1,0:T(8,128)(2,1)} %fusion.12.q_ref, bf16[64,512,128]{2,1,0:T(8,128)(2,1)} %k_ref.1, bf16[64,512,128]{2,1,0:T(8,128)(2,1)} %v_ref.1), custom_call_target="tpu_custom_call" | custom-call | tf_op jit(solution)/shard_map/pallas_call | solution.py:162
  37.2 2.1 %dynamic-slice_bitcast_fusion.1 = (f32[4,4,2,32,66]{4,3,2,1,0:T(8,128)S(1)}, f32[4,4,2,32,66]{4,3,2,1,0:T(8,128)}) fusion(f32[2,4,4,2,32,66]{5,4,3,2,1,0:T(8,128)} %bitcast.159, s32[]{:T(128)S(6)} %select_n.441, s32[]{:T(128)S(6)} %select_n.443), kind=kLoop, calls=%fused_computation.33 | loop fusion | bytes 1081352 | tf_op jit(solution)/shard_map/jit(dynamic_index_in_dim)/squeeze | solution.py:48
  42.8 2.2 %fusion.8 = f32[4,64,2,64]{1,3,2,0:T(8,128)S(1)} fusion(bf16[2,64,2048,1]{2,1,0,3:T(8,128)(2,1)} %bitcast.170, f32[2048]{0:T(1024)S(1)} %convert_element_type.131, f32[4,64]{1,0:T(4,128)S(1)} %add_rsqrt_fusion, bf16[4,64,2048]{2,1,0:T(8,128)(2,1)} %param.14), kind=kOutput, calls=%fused_computation.17 | convolution fusion | flops 136314880 | bytes 1713152 | tf_op jit(solution)/shard_map/dot_general | solution.py:219
  51.2 3.9 %collective-permute-start.3 = (f32[4,2,32,66]{3,2,1,0:T(8,128)S(1)}, f32[4,2,32,66]{3,2,1,0:T(8,128)S(1)}, u32[]{:S(2)}, u32[]{:S(2)}) collective-permute-start(f32[4,2,32,66]{3,2,1,0:T(8,128)S(1)} %get-tuple-element.52), channel_id=1, source_target_pairs={{0,24},{4,28},{8,0},{12,4},{16,8},{20,12},{24,16},{28,20},{32,56},... | collective-permute-start | bytes 202760 | tf_op jit(solution)/shard_map/ppermute | solution.py:44
  56.4 4.4 %collective-permute-done.3 = f32[4,2,32,66]{3,2,1,0:T(8,128)S(1)} collective-permute-done((f32[4,2,32,66]{3,2,1,0:T(8,128)S(1)}, f32[4,2,32,66]{3,2,1,0:T(8,128)S(1)}, u32[]{:S(2)}, u32[]{:S(2)}) %collective-permute-start.3) | collective-permute-done | bytes 67616 | tf_op jit(solution)/shard_map/ppermute | solution.py:44
  61.5 2.8 %collective-permute-done.1 = f32[4,2,32,66]{3,2,1,0:T(8,128)S(1)} collective-permute-done((f32[4,2,32,66]{3,2,1,0:T(8,128)S(1)}, f32[4,2,32,66]{3,2,1,0:T(8,128)S(1)}, u32[]{:S(2)}, u32[]{:S(2)}) %collective-permute-start.1) | collective-permute-done | bytes 67616 | tf_op jit(solution)/shard_map/ppermute | solution.py:44
  65.5 2.5 %collective-permute-start.6 = (f32[2,32,66]{2,1,0:T(8,128)S(1)}, f32[2,32,66]{2,1,0:T(8,128)S(1)}, u32[]{:S(2)}, u32[]{:S(2)}) collective-permute-start(f32[2,32,66]{2,1,0:T(8,128)S(1)} %get-tuple-element.67), channel_id=1, source_target_pairs={{0,96},{4,100},{8,104},{12,108},{16,112},{20,116},{24,120},{28,124... | collective-permute-start | bytes 50696 | tf_op jit(solution)/shard_map/ppermute | solution.py:44
  69.2 3.1 %collective-permute-done.5 = f32[2,32,66]{2,1,0:T(8,128)S(1)} collective-permute-done((f32[2,32,66]{2,1,0:T(8,128)S(1)}, f32[2,32,66]{2,1,0:T(8,128)S(1)}, u32[]{:S(2)}, u32[]{:S(2)}) %collective-permute-start.5) | collective-permute-done | bytes 16928 | tf_op jit(solution)/shard_map/ppermute | solution.py:44
  76.0 2.6 %collective-permute-start.8 = (f32[8,2048]{1,0:T(8,128)S(1)}, f32[8,2048]{1,0:T(8,128)S(1)}, u32[]{:S(2)}, u32[]{:S(2)}) collective-permute-start(f32[8,2048]{1,0:T(8,128)S(1)} %fusion.95), channel_id=1, source_target_pairs={{0,2},{1,3},{2,0},{3,1},{4,6},{5,7},{6,4},{7,5},{8,10},{9,11},{10,... | collective-permute-start | bytes 196616 | tf_op jit(solution)/shard_map/ppermute | solution.py:44
  83.5 2.7 %collective-permute-start.12 = (bf16[8,2048]{1,0:T(8,128)(2,1)S(1)}, bf16[8,2048]{1,0:T(8,128)(2,1)S(1)}, u32[]{:S(2)}, u32[]{:S(2)}) collective-permute-start(bf16[8,2048]{1,0:T(8,128)(2,1)S(1)} %fusion.30), channel_id=1, source_target_pairs={{0,96},{4,100},{8,104},{12,108},{16,112},{20,116},{24,120},{28,124... | collective-permute-start | bytes 98312 | tf_op jit(solution)/shard_map/ppermute | solution.py:44
  88.4 2.7 %collective-permute-start.15 = (bf16[4,8,2048]{2,1,0:T(8,128)(2,1)S(1)}, bf16[4,8,2048]{2,1,0:T(8,128)(2,1)S(1)}, u32[]{:S(2)}, u32[]{:S(2)}) collective-permute-start(bf16[4,8,2048]{2,1,0:T(8,128)(2,1)S(1)} %get-tuple-element.65), channel_id=1, source_target_pairs={{0,24},{4,28},{8,0},{12,4},{16,8},{20,12},{24,16},{28,20},{32,56},... | collective-permute-start | bytes 393224 | tf_op jit(solution)/shard_map/ppermute | solution.py:44
  94.4 6.6 %collective-permute-start.16 = (bf16[4,4,8,2048]{3,2,1,0:T(8,128)(2,1)S(1)}, bf16[4,4,8,2048]{3,2,1,0:T(8,128)(2,1)S(1)}, u32[]{:S(2)}, u32[]{:S(2)}) collective-permute-start(bf16[4,4,8,2048]{3,2,1,0:T(8,128)(2,1)S(1)} %pad_maximum_fusion.1), channel_id=1, source_target_pairs={{0,4},{4,0},{8,12},{12,8},{16,20},{20,16},{24,28},{28,24},{32,36},... | collective-permute-start | bytes 1572872 | tf_op jit(solution)/shard_map/ppermute | solution.py:44
  103.4 2.9 %fusion.55 = f32[128,2048]{1,0:T(8,128)} fusion(bf16[64,2048]{1,0:T(8,128)(2,1)} %param.27, f32[128,64]{0,1:T(8,128)} %fusion.97, bf16[128,2048]{1,0:T(8,128)(2,1)S(1)} %bitcast.164, bf16[64,2048]{1,0:T(8,128)(2,1)} %param.26), kind=kOutput, calls=%fused_computation.145 | convolution fusion | flops 67158016 | bytes 2129920 | tf_op jit(solution)/shard_map/dot_general | solution.py:300
  106.9 2.8 %fusion.4 = f32[128,2048]{1,0:T(8,128)} fusion(bf16[64,2048]{1,0:T(8,128)(2,1)} %param.27, bf16[128,2048]{1,0:T(8,128)(2,1)S(1)} %bitcast.157, bf16[64,2048]{1,0:T(8,128)(2,1)} %param.26, f32[128,64]{0,1:T(8,128)S(1)} %fusion.96), kind=kOutput, calls=%fused_computation.11 | convolution fusion | flops 67158016 | bytes 2129920 | tf_op jit(solution)/shard_map/dot_general | solution.py:300
  111.9 2.4 %collective-permute-start.20 = (bf16[4,8,2048]{2,1,0:T(8,128)(2,1)S(1)}, bf16[4,8,2048]{2,1,0:T(8,128)(2,1)S(1)}, u32[]{:S(2)}, u32[]{:S(2)}) collective-permute-start(bf16[4,8,2048]{2,1,0:T(8,128)(2,1)S(1)} %get-tuple-element.49), channel_id=1, source_target_pairs={{0,24},{4,28},{8,0},{12,4},{16,8},{20,12},{24,16},{28,20},{32,56},... | collective-permute-start | bytes 393224 | tf_op jit(solution)/shard_map/ppermute | solution.py:44
  114.6 3.1 %collective-permute-done.18 = bf16[4,8,2048]{2,1,0:T(8,128)(2,1)S(1)} collective-permute-done((bf16[4,8,2048]{2,1,0:T(8,128)(2,1)S(1)}, bf16[4,8,2048]{2,1,0:T(8,128)(2,1)S(1)}, u32[]{:S(2)}, u32[]{:S(2)}) %collective-permute-start.18) | collective-permute-done | bytes 131104 | tf_op jit(solution)/shard_map/ppermute | solution.py:44
  117.7 2.7 %collective-permute-done.19 = bf16[4,8,2048]{2,1,0:T(8,128)(2,1)S(1)} collective-permute-done((bf16[4,8,2048]{2,1,0:T(8,128)(2,1)S(1)}, bf16[4,8,2048]{2,1,0:T(8,128)(2,1)S(1)}, u32[]{:S(2)}, u32[]{:S(2)}) %collective-permute-start.19) | collective-permute-done | bytes 131104 | tf_op jit(solution)/shard_map/ppermute | solution.py:44
  121.1 2.6 %collective-permute-start.23 = (bf16[8,2048]{1,0:T(8,128)(2,1)S(1)}, bf16[8,2048]{1,0:T(8,128)(2,1)S(1)}, u32[]{:S(2)}, u32[]{:S(2)}) collective-permute-start(bf16[8,2048]{1,0:T(8,128)(2,1)S(1)} %get-tuple-element.62), channel_id=1, source_target_pairs={{0,96},{4,100},{8,104},{12,108},{16,112},{20,116},{24,120},{28,124... | collective-permute-start | bytes 98312 | tf_op jit(solution)/shard_map/ppermute | solution.py:44
  124.9 3.4 %collective-permute-done.22 = bf16[8,2048]{1,0:T(8,128)(2,1)S(1)} collective-permute-done((bf16[8,2048]{1,0:T(8,128)(2,1)S(1)}, bf16[8,2048]{1,0:T(8,128)(2,1)S(1)}, u32[]{:S(2)}, u32[]{:S(2)}) %collective-permute-start.22) | collective-permute-done | bytes 32800 | tf_op jit(solution)/shard_map/ppermute | solution.py:44
  128.4 3.4 %collective-permute-start.25 = (f32[8,2048]{1,0:T(8,128)S(1)}, f32[8,2048]{1,0:T(8,128)S(1)}, u32[]{:S(2)}, u32[]{:S(2)}) collective-permute-start(f32[8,2048]{1,0:T(8,128)S(1)} %fusion.34), channel_id=1, source_target_pairs={{0,2},{1,3},{2,0},{3,1},{4,6},{5,7},{6,4},{7,5},{8,10},{9,11},{10,... | collective-permute-start | bytes 196616 | tf_op jit(solution)/shard_map/ppermute | solution.py:44
  141.2 2.7 %collective-permute-start.30 = (bf16[4,8,2048]{2,1,0:T(8,128)(2,1)S(1)}, bf16[4,8,2048]{2,1,0:T(8,128)(2,1)S(1)}, u32[]{:S(2)}, u32[]{:S(2)}) collective-permute-start(bf16[4,8,2048]{2,1,0:T(8,128)(2,1)S(1)} %get-tuple-element.60), channel_id=1, source_target_pairs={{0,8},{4,12},{8,16},{12,20},{16,24},{20,28},{24,0},{28,4},{32,40},... | collective-permute-start | bytes 393224 | tf_op jit(solution)/shard_map/ppermute | solution.py:44
  147.8 7.6 %collective-permute-start.33 = (bf16[4,4,8,2048]{3,2,1,0:T(8,128)(2,1)S(1)}, bf16[4,4,8,2048]{3,2,1,0:T(8,128)(2,1)S(1)}, u32[]{:S(2)}, u32[]{:S(2)}) collective-permute-start(bf16[4,4,8,2048]{3,2,1,0:T(8,128)(2,1)S(1)} %pad_maximum_fusion.2), channel_id=1, source_target_pairs={{0,4},{4,0},{8,12},{12,8},{16,20},{20,16},{24,28},{28,24},{32,36},... | collective-permute-start | bytes 1572872 | tf_op jit(solution)/shard_map/ppermute | solution.py:44
  (158 shorter events, 61.0 us)
Async XLA Ops:
  39.3 9.9 %collective-permute-start = (f32[4,4,2,32,66]{4,3,2,1,0:T(8,128)}, f32[4,4,2,32,66]{4,3,2,1,0:T(8,128)S(1)}, u32[]{:S(2)}, u32[]{:S(2)}) collective-permute-start(f32[4,4,2,32,66]{4,3,2,1,0:T(8,128)} %get-tuple-element.47), channel_id=1, source_target_pairs={{0,4},{4,0},{8,12},{12,8},{16,20},{20,16},{24,28},{28,24},{32,36},... | collective-permute-start | bytes 811016 | tf_op jit(solution)/shard_map/ppermute | solution.py:44
  51.2 9.6 %collective-permute-start.3 = (f32[4,2,32,66]{3,2,1,0:T(8,128)S(1)}, f32[4,2,32,66]{3,2,1,0:T(8,128)S(1)}, u32[]{:S(2)}, u32[]{:S(2)}) collective-permute-start(f32[4,2,32,66]{3,2,1,0:T(8,128)S(1)} %get-tuple-element.52), channel_id=1, source_target_pairs={{0,24},{4,28},{8,0},{12,4},{16,8},{20,12},{24,16},{28,20},{32,56},... | collective-permute-start | bytes 202760 | tf_op jit(solution)/shard_map/ppermute | solution.py:44
  55.2 6.3 %collective-permute-start.2 = (f32[4,2,32,66]{3,2,1,0:T(8,128)S(1)}, f32[4,2,32,66]{3,2,1,0:T(8,128)S(1)}, u32[]{:S(2)}, u32[]{:S(2)}) collective-permute-start(f32[4,2,32,66]{3,2,1,0:T(8,128)S(1)} %get-tuple-element.53), channel_id=1, source_target_pairs={{0,16},{4,20},{8,24},{12,28},{16,0},{20,4},{24,8},{28,12},{32,48},... | collective-permute-start | bytes 202760 | tf_op jit(solution)/shard_map/ppermute | solution.py:44
  55.2 9.1 %collective-permute-start.1 = (f32[4,2,32,66]{3,2,1,0:T(8,128)S(1)}, f32[4,2,32,66]{3,2,1,0:T(8,128)S(1)}, u32[]{:S(2)}, u32[]{:S(2)}) collective-permute-start(f32[4,2,32,66]{3,2,1,0:T(8,128)S(1)} %get-tuple-element.54), channel_id=1, source_target_pairs={{0,8},{4,12},{8,16},{12,20},{16,24},{20,28},{24,0},{28,4},{32,40},... | collective-permute-start | bytes 202760 | tf_op jit(solution)/shard_map/ppermute | solution.py:44
  68.0 4.3 %collective-permute-start.5 = (f32[2,32,66]{2,1,0:T(8,128)S(1)}, f32[2,32,66]{2,1,0:T(8,128)S(1)}, u32[]{:S(2)}, u32[]{:S(2)}) collective-permute-start(f32[2,32,66]{2,1,0:T(8,128)S(1)} %get-tuple-element.68), channel_id=1, source_target_pairs={{0,64},{4,68},{8,72},{12,76},{16,80},{20,84},{24,88},{28,92},{32,9... | collective-permute-start | bytes 50696 | tf_op jit(solution)/shard_map/ppermute | solution.py:44
  74.7 6.1 %collective-permute-start.9 = (f32[8,2048]{1,0:T(8,128)S(1)}, f32[8,2048]{1,0:T(8,128)S(1)}, u32[]{:S(2)}, u32[]{:S(2)}) collective-permute-start(f32[8,2048]{1,0:T(8,128)S(1)} %fusion.95), channel_id=1, source_target_pairs={{0,1},{1,2},{2,3},{3,0},{4,5},{5,6},{6,7},{7,4},{8,9},{9,10},{10,1... | collective-permute-start | bytes 196616 | tf_op jit(solution)/shard_map/ppermute | solution.py:44
  76.0 5.0 %collective-permute-start.8 = (f32[8,2048]{1,0:T(8,128)S(1)}, f32[8,2048]{1,0:T(8,128)S(1)}, u32[]{:S(2)}, u32[]{:S(2)}) collective-permute-start(f32[8,2048]{1,0:T(8,128)S(1)} %fusion.95), channel_id=1, source_target_pairs={{0,2},{1,3},{2,0},{3,1},{4,6},{5,7},{6,4},{7,5},{8,10},{9,11},{10,... | collective-permute-start | bytes 196616 | tf_op jit(solution)/shard_map/ppermute | solution.py:44
  82.3 4.3 %collective-permute-start.11 = (bf16[8,2048]{1,0:T(8,128)(2,1)S(1)}, bf16[8,2048]{1,0:T(8,128)(2,1)S(1)}, u32[]{:S(2)}, u32[]{:S(2)}) collective-permute-start(bf16[8,2048]{1,0:T(8,128)(2,1)S(1)} %fusion.30), channel_id=1, source_target_pairs={{0,64},{4,68},{8,72},{12,76},{16,80},{20,84},{24,88},{28,92},{32,9... | collective-permute-start | bytes 98312 | tf_op jit(solution)/shard_map/ppermute | solution.py:44
  87.5 5.5 %collective-permute-start.14 = (bf16[4,8,2048]{2,1,0:T(8,128)(2,1)S(1)}, bf16[4,8,2048]{2,1,0:T(8,128)(2,1)S(1)}, u32[]{:S(2)}, u32[]{:S(2)}) collective-permute-start(bf16[4,8,2048]{2,1,0:T(8,128)(2,1)S(1)} %get-tuple-element.65), channel_id=1, source_target_pairs={{0,16},{4,20},{8,24},{12,28},{16,0},{20,4},{24,8},{28,12},{32,48},... | collective-permute-start | bytes 393224 | tf_op jit(solution)/shard_map/ppermute | solution.py:44
  88.4 5.9 %collective-permute-start.13 = (bf16[4,8,2048]{2,1,0:T(8,128)(2,1)S(1)}, bf16[4,8,2048]{2,1,0:T(8,128)(2,1)S(1)}, u32[]{:S(2)}, u32[]{:S(2)}) collective-permute-start(bf16[4,8,2048]{2,1,0:T(8,128)(2,1)S(1)} %get-tuple-element.65), channel_id=1, source_target_pairs={{0,8},{4,12},{8,16},{12,20},{16,24},{20,28},{24,0},{28,4},{32,40},... | collective-permute-start | bytes 393224 | tf_op jit(solution)/shard_map/ppermute | solution.py:44
  88.4 5.9 %collective-permute-start.15 = (bf16[4,8,2048]{2,1,0:T(8,128)(2,1)S(1)}, bf16[4,8,2048]{2,1,0:T(8,128)(2,1)S(1)}, u32[]{:S(2)}, u32[]{:S(2)}) collective-permute-start(bf16[4,8,2048]{2,1,0:T(8,128)(2,1)S(1)} %get-tuple-element.65), channel_id=1, source_target_pairs={{0,24},{4,28},{8,0},{12,4},{16,8},{20,12},{24,16},{28,20},{32,56},... | collective-permute-start | bytes 393224 | tf_op jit(solution)/shard_map/ppermute | solution.py:44
  94.4 8.1 %collective-permute-start.16 = (bf16[4,4,8,2048]{3,2,1,0:T(8,128)(2,1)S(1)}, bf16[4,4,8,2048]{3,2,1,0:T(8,128)(2,1)S(1)}, u32[]{:S(2)}, u32[]{:S(2)}) collective-permute-start(bf16[4,4,8,2048]{3,2,1,0:T(8,128)(2,1)S(1)} %pad_maximum_fusion.1), channel_id=1, source_target_pairs={{0,4},{4,0},{8,12},{12,8},{16,20},{20,16},{24,28},{28,24},{32,36},... | collective-permute-start | bytes 1572872 | tf_op jit(solution)/shard_map/ppermute | solution.py:44
  111.5 6.2 %collective-permute-start.18 = (bf16[4,8,2048]{2,1,0:T(8,128)(2,1)S(1)}, bf16[4,8,2048]{2,1,0:T(8,128)(2,1)S(1)}, u32[]{:S(2)}, u32[]{:S(2)}) collective-permute-start(bf16[4,8,2048]{2,1,0:T(8,128)(2,1)S(1)} %get-tuple-element.48), channel_id=1, source_target_pairs={{0,8},{4,12},{8,16},{12,20},{16,24},{20,28},{24,0},{28,4},{32,40},... | collective-permute-start | bytes 393224 | tf_op jit(solution)/shard_map/ppermute | solution.py:44
  111.9 5.8 %collective-permute-start.20 = (bf16[4,8,2048]{2,1,0:T(8,128)(2,1)S(1)}, bf16[4,8,2048]{2,1,0:T(8,128)(2,1)S(1)}, u32[]{:S(2)}, u32[]{:S(2)}) collective-permute-start(bf16[4,8,2048]{2,1,0:T(8,128)(2,1)S(1)} %get-tuple-element.49), channel_id=1, source_target_pairs={{0,24},{4,28},{8,0},{12,4},{16,8},{20,12},{24,16},{28,20},{32,56},... | collective-permute-start | bytes 393224 | tf_op jit(solution)/shard_map/ppermute | solution.py:44
  114.3 6.2 %collective-permute-start.19 = (bf16[4,8,2048]{2,1,0:T(8,128)(2,1)S(1)}, bf16[4,8,2048]{2,1,0:T(8,128)(2,1)S(1)}, u32[]{:S(2)}, u32[]{:S(2)}) collective-permute-start(bf16[4,8,2048]{2,1,0:T(8,128)(2,1)S(1)} %get-tuple-element.50), channel_id=1, source_target_pairs={{0,16},{4,20},{8,24},{12,28},{16,0},{20,4},{24,8},{28,12},{32,48},... | collective-permute-start | bytes 393224 | tf_op jit(solution)/shard_map/ppermute | solution.py:44
  120.6 4.3 %collective-permute-start.21 = (bf16[8,2048]{1,0:T(8,128)(2,1)S(1)}, bf16[8,2048]{1,0:T(8,128)(2,1)S(1)}, u32[]{:S(2)}, u32[]{:S(2)}) collective-permute-start(bf16[8,2048]{1,0:T(8,128)(2,1)S(1)} %get-tuple-element.61), channel_id=1, source_target_pairs={{0,32},{4,36},{8,40},{12,44},{16,48},{20,52},{24,56},{28,60},{32,6... | collective-permute-start | bytes 98312 | tf_op jit(solution)/shard_map/ppermute | solution.py:44
  123.7 4.6 %collective-permute-start.22 = (bf16[8,2048]{1,0:T(8,128)(2,1)S(1)}, bf16[8,2048]{1,0:T(8,128)(2,1)S(1)}, u32[]{:S(2)}, u32[]{:S(2)}) collective-permute-start(bf16[8,2048]{1,0:T(8,128)(2,1)S(1)} %get-tuple-element.63), channel_id=1, source_target_pairs={{0,64},{4,68},{8,72},{12,76},{16,80},{20,84},{24,88},{28,92},{32,9... | collective-permute-start | bytes 98312 | tf_op jit(solution)/shard_map/ppermute | solution.py:44
  128.3 4.4 %collective-permute-start.26 = (f32[8,2048]{1,0:T(8,128)S(1)}, f32[8,2048]{1,0:T(8,128)S(1)}, u32[]{:S(2)}, u32[]{:S(2)}) collective-permute-start(f32[8,2048]{1,0:T(8,128)S(1)} %fusion.34), channel_id=1, source_target_pairs={{0,1},{1,2},{2,3},{3,0},{4,5},{5,6},{6,7},{7,4},{8,9},{9,10},{10,1... | collective-permute-start | bytes 196616 | tf_op jit(solution)/shard_map/ppermute | solution.py:44
  128.4 5.8 %collective-permute-start.25 = (f32[8,2048]{1,0:T(8,128)S(1)}, f32[8,2048]{1,0:T(8,128)S(1)}, u32[]{:S(2)}, u32[]{:S(2)}) collective-permute-start(f32[8,2048]{1,0:T(8,128)S(1)} %fusion.34), channel_id=1, source_target_pairs={{0,2},{1,3},{2,0},{3,1},{4,6},{5,7},{6,4},{7,5},{8,10},{9,11},{10,... | collective-permute-start | bytes 196616 | tf_op jit(solution)/shard_map/ppermute | solution.py:44
  136.1 4.3 %collective-permute-start.28 = (bf16[8,2048]{1,0:T(8,128)(2,1)S(1)}, bf16[8,2048]{1,0:T(8,128)(2,1)S(1)}, u32[]{:S(2)}, u32[]{:S(2)}) collective-permute-start(bf16[8,2048]{1,0:T(8,128)(2,1)S(1)} %fusion.31), channel_id=1, source_target_pairs={{0,64},{4,68},{8,72},{12,76},{16,80},{20,84},{24,88},{28,92},{32,9... | collective-permute-start | bytes 98312 | tf_op jit(solution)/shard_map/ppermute | solution.py:44
  136.1 4.6 %collective-permute-start.27 = (bf16[8,2048]{1,0:T(8,128)(2,1)S(1)}, bf16[8,2048]{1,0:T(8,128)(2,1)S(1)}, u32[]{:S(2)}, u32[]{:S(2)}) collective-permute-start(bf16[8,2048]{1,0:T(8,128)(2,1)S(1)} %fusion.31), channel_id=1, source_target_pairs={{0,32},{4,36},{8,40},{12,44},{16,48},{20,52},{24,56},{28,60},{32,6... | collective-permute-start | bytes 98312 | tf_op jit(solution)/shard_map/ppermute | solution.py:44
  140.8 5.5 %collective-permute-start.31 = (bf16[4,8,2048]{2,1,0:T(8,128)(2,1)S(1)}, bf16[4,8,2048]{2,1,0:T(8,128)(2,1)S(1)}, u32[]{:S(2)}, u32[]{:S(2)}) collective-permute-start(bf16[4,8,2048]{2,1,0:T(8,128)(2,1)S(1)} %get-tuple-element.60), channel_id=1, source_target_pairs={{0,16},{4,20},{8,24},{12,28},{16,0},{20,4},{24,8},{28,12},{32,48},... | collective-permute-start | bytes 393224 | tf_op jit(solution)/shard_map/ppermute | solution.py:44
  141.2 6.4 %collective-permute-start.30 = (bf16[4,8,2048]{2,1,0:T(8,128)(2,1)S(1)}, bf16[4,8,2048]{2,1,0:T(8,128)(2,1)S(1)}, u32[]{:S(2)}, u32[]{:S(2)}) collective-permute-start(bf16[4,8,2048]{2,1,0:T(8,128)(2,1)S(1)} %get-tuple-element.60), channel_id=1, source_target_pairs={{0,8},{4,12},{8,16},{12,20},{16,24},{20,28},{24,0},{28,4},{32,40},... | collective-permute-start | bytes 393224 | tf_op jit(solution)/shard_map/ppermute | solution.py:44
  147.8 9.1 %collective-permute-start.33 = (bf16[4,4,8,2048]{3,2,1,0:T(8,128)(2,1)S(1)}, bf16[4,4,8,2048]{3,2,1,0:T(8,128)(2,1)S(1)}, u32[]{:S(2)}, u32[]{:S(2)}) collective-permute-start(bf16[4,4,8,2048]{3,2,1,0:T(8,128)(2,1)S(1)} %pad_maximum_fusion.2), channel_id=1, source_target_pairs={{0,4},{4,0},{8,12},{12,8},{16,20},{20,16},{24,28},{28,24},{32,36},... | collective-permute-start | bytes 1572872 | tf_op jit(solution)/shard_map/ppermute | solution.py:44
  (25 other events, 228.3 us)

commit v2 on v1

--- a/solution.py
+++ b/solution.py
@@ -127,7 +127,7 @@
     )
 
 
-BLOCK_REQ = 8
+BLOCK_REQ = 16
 
 
 def cache_kernel(start_ref, len_ref, q_ref, k_ref, v_ref, packed_ref):

time: 159 us -> 159 us (level)
  no operation moved by 1% of the time
where the time goes in v2:
time: 159 us
  starting transfers between devices  52.5 us (33%)
  waiting for transfers between devices  39.6 us (25%)
  Pallas kernels  20.3 us (13%)
  matrix products  16.7 us (11%)
  other arithmetic  15.6 us (10%)
  local copies, waits for them, and re-layouts  12.8 us (8%)
    ppermute x34, starting transfers between devices, shifted(): return lax.ppermute(x, level[0], shift_perm(level, d))  52.5 us
    ppermute x34, waiting for transfers between devices, shifted(): return lax.ppermute(x, level[0], shift_perm(level, d))  39.6 us
    pallas_call x1, Pallas kernels, cache_attention(): pl.pallas_call(cache_kernel, out_shape=jax.ShapeDtypeStruct((req, rows, h...  20.3 us
    unnamed x33, local copies, waits for them, and re-layouts  6.88 us
    dot_general x2, matrix products, feed(): jnp.dot(hidden, w_down, preferred_element_type=jnp.float32)  5.7 us
  transfers between devices with their start and end apart: 34, of which 26 were waited for; matrix products, arithmetic and copies ran while one was open for 9% of the time, Pallas kernels for 0%

profile of v2, /device:TPU:1, one launch (start us, length us, event | category | flops | bytes accessed | tf_op | source)
XLA Modules:
  0.0 158.8 jit_solution(16102676016827341551)
XLA Ops:
  3.7 4.0 %copy.65 = bf16[2048,512]{0,1:T(8,128)(2,1)} copy(bf16[2048,512]{1,0:T(8,128)(2,1)} %param.20) | data formatting | bytes 4194304 | tf_op args[6]
  8.1 2.9 %fusion.10 = f32[4,64,8,64]{1,3,2,0:T(8,128)S(1)} fusion(bf16[8,64,2048,1]{2,1,0,3:T(8,128)(2,1)} %bitcast.160, f32[2048]{0:T(1024)S(1)} %convert_element_type.131, f32[4,64]{1,0:T(4,128)S(1)} %add_rsqrt_fusion, bf16[4,64,2048]{2,1,0:T(8,128)(2,1)S(1)} %copy-done.5), kind=kOutput, calls=%fused_computation.18 | convolution fusion | flops 538968064 | bytes 3679232 | tf_op jit(solution)/shard_map/dot_general | solution.py:216
  16.8 20.3 %shard_map.157 = f32[64,32,66]{2,1,0:T(8,128)} custom-call(s32[64]{0:T(128)} %and_select_fusion.start_ref, s32[64]{0:T(128)} %len_ref.1, bf16[64,32,128]{2,1,0:T(8,128)(2,1)} %fusion.12.q_ref, bf16[64,512,128]{2,1,0:T(8,128)(2,1)} %k_ref.1, bf16[64,512,128]{2,1,0:T(8,128)(2,1)} %v_ref.1), custom_call_target="tpu_custom_call" | custom-call | tf_op jit(solution)/shard_map/pallas_call | solution.py:162
  37.2 2.1 %dynamic-slice_bitcast_fusion.1 = (f32[4,4,2,32,66]{4,3,2,1,0:T(8,128)S(1)}, f32[4,4,2,32,66]{4,3,2,1,0:T(8,128)}) fusion(f32[2,4,4,2,32,66]{5,4,3,2,1,0:T(8,128)} %bitcast.159, s32[]{:T(128)S(6)} %select_n.441, s32[]{:T(128)S(6)} %select_n.443), kind=kLoop, calls=%fused_computation.33 | loop fusion | bytes 1081352 | tf_op jit(solution)/shard_map/jit(dynamic_index_in_dim)/squeeze | solution.py:48
  42.8 2.2 %fusion.8 = f32[4,64,2,64]{1,3,2,0:T(8,128)S(1)} fusion(bf16[2,64,2048,1]{2,1,0,3:T(8,128)(2,1)} %bitcast.170, f32[2048]{0:T(1024)S(1)} %convert_element_type.131, f32[4,64]{1,0:T(4,128)S(1)} %add_rsqrt_fusion, bf16[4,64,2048]{2,1,0:T(8,128)(2,1)} %param.14), kind=kOutput, calls=%fused_computation.17 | convolution fusion | flops 136314880 | bytes 1713152 | tf_op jit(solution)/shard_map/dot_general | solution.py:219
  51.2 3.9 %collective-permute-start.3 = (f32[4,2,32,66]{3,2,1,0:T(8,128)S(1)}, f32[4,2,32,66]{3,2,1,0:T(8,128)S(1)}, u32[]{:S(2)}, u32[]{:S(2)}) collective-permute-start(f32[4,2,32,66]{3,2,1,0:T(8,128)S(1)} %get-tuple-element.52), channel_id=1, source_target_pairs={{0,24},{4,28},{8,0},{12,4},{16,8},{20,12},{24,16},{28,20},{32,56},... | collective-permute-start | bytes 202760 | tf_op jit(solution)/shard_map/ppermute | solution.py:44
  56.4 4.4 %collective-permute-done.3 = f32[4,2,32,66]{3,2,1,0:T(8,128)S(1)} collective-permute-done((f32[4,2,32,66]{3,2,1,0:T(8,128)S(1)}, f32[4,2,32,66]{3,2,1,0:T(8,128)S(1)}, u32[]{:S(2)}, u32[]{:S(2)}) %collective-permute-start.3) | collective-permute-done | bytes 67616 | tf_op jit(solution)/shard_map/ppermute | solution.py:44
  61.5 2.8 %collective-permute-done.1 = f32[4,2,32,66]{3,2,1,0:T(8,128)S(1)} collective-permute-done((f32[4,2,32,66]{3,2,1,0:T(8,128)S(1)}, f32[4,2,32,66]{3,2,1,0:T(8,128)S(1)}, u32[]{:S(2)}, u32[]{:S(2)}) %collective-permute-start.1) | collective-permute-done | bytes 67616 | tf_op jit(solution)/shard_map/ppermute | solution.py:44
  65.5 2.5 %collective-permute-start.6 = (f32[2,32,66]{2,1,0:T(8,128)S(1)}, f32[2,32,66]{2,1,0:T(8,128)S(1)}, u32[]{:S(2)}, u32[]{:S(2)}) collective-permute-start(f32[2,32,66]{2,1,0:T(8,128)S(1)} %get-tuple-element.67), channel_id=1, source_target_pairs={{0,96},{4,100},{8,104},{12,108},{16,112},{20,116},{24,120},{28,124... | collective-permute-start | bytes 50696 | tf_op jit(solution)/shard_map/ppermute | solution.py:44
  69.2 3.1 %collective-permute-done.5 = f32[2,32,66]{2,1,0:T(8,128)S(1)} collective-permute-done((f32[2,32,66]{2,1,0:T(8,128)S(1)}, f32[2,32,66]{2,1,0:T(8,128)S(1)}, u32[]{:S(2)}, u32[]{:S(2)}) %collective-permute-start.5) | collective-permute-done | bytes 16928 | tf_op jit(solution)/shard_map/ppermute | solution.py:44
  76.0 2.6 %collective-permute-start.8 = (f32[8,2048]{1,0:T(8,128)S(1)}, f32[8,2048]{1,0:T(8,128)S(1)}, u32[]{:S(2)}, u32[]{:S(2)}) collective-permute-start(f32[8,2048]{1,0:T(8,128)S(1)} %fusion.95), channel_id=1, source_target_pairs={{0,2},{1,3},{2,0},{3,1},{4,6},{5,7},{6,4},{7,5},{8,10},{9,11},{10,... | collective-permute-start | bytes 196616 | tf_op jit(solution)/shard_map/ppermute | solution.py:44
  83.5 2.7 %collective-permute-start.12 = (bf16[8,2048]{1,0:T(8,128)(2,1)S(1)}, bf16[8,2048]{1,0:T(8,128)(2,1)S(1)}, u32[]{:S(2)}, u32[]{:S(2)}) collective-permute-start(bf16[8,2048]{1,0:T(8,128)(2,1)S(1)} %fusion.30), channel_id=1, source_target_pairs={{0,96},{4,100},{8,104},{12,108},{16,112},{20,116},{24,120},{28,124... | collective-permute-start | bytes 98312 | tf_op jit(solution)/shard_map/ppermute | solution.py:44
  88.4 2.7 %collective-permute-start.15 = (bf16[4,8,2048]{2,1,0:T(8,128)(2,1)S(1)}, bf16[4,8,2048]{2,1,0:T(8,128)(2,1)S(1)}, u32[]{:S(2)}, u32[]{:S(2)}) collective-permute-start(bf16[4,8,2048]{2,1,0:T(8,128)(2,1)S(1)} %get-tuple-element.65), channel_id=1, source_target_pairs={{0,24},{4,28},{8,0},{12,4},{16,8},{20,12},{24,16},{28,20},{32,56},... | collective-permute-start | bytes 393224 | tf_op jit(solution)/shard_map/ppermute | solution.py:44
  94.4 6.6 %collective-permute-start.16 = (bf16[4,4,8,2048]{3,2,1,0:T(8,128)(2,1)S(1)}, bf16[4,4,8,2048]{3,2,1,0:T(8,128)(2,1)S(1)}, u32[]{:S(2)}, u32[]{:S(2)}) collective-permute-start(bf16[4,4,8,2048]{3,2,1,0:T(8,128)(2,1)S(1)} %pad_maximum_fusion.1), channel_id=1, source_target_pairs={{0,4},{4,0},{8,12},{12,8},{16,20},{20,16},{24,28},{28,24},{32,36},... | collective-permute-start | bytes 1572872 | tf_op jit(solution)/shard_map/ppermute | solution.py:44
  103.4 2.9 %fusion.55 = f32[128,2048]{1,0:T(8,128)} fusion(bf16[64,2048]{1,0:T(8,128)(2,1)} %param.27, f32[128,64]{0,1:T(8,128)} %fusion.97, bf16[128,2048]{1,0:T(8,128)(2,1)S(1)} %bitcast.164, bf16[64,2048]{1,0:T(8,128)(2,1)} %param.26), kind=kOutput, calls=%fused_computation.145 | convolution fusion | flops 67158016 | bytes 2129920 | tf_op jit(solution)/shard_map/dot_general | solution.py:300
  106.9 2.8 %fusion.4 = f32[128,2048]{1,0:T(8,128)} fusion(bf16[64,2048]{1,0:T(8,128)(2,1)} %param.27, bf16[128,2048]{1,0:T(8,128)(2,1)S(1)} %bitcast.157, bf16[64,2048]{1,0:T(8,128)(2,1)} %param.26, f32[128,64]{0,1:T(8,128)S(1)} %fusion.96), kind=kOutput, calls=%fused_computation.11 | convolution fusion | flops 67158016 | bytes 2129920 | tf_op jit(solution)/shard_map/dot_general | solution.py:300
  111.9 2.4 %collective-permute-start.20 = (bf16[4,8,2048]{2,1,0:T(8,128)(2,1)S(1)}, bf16[4,8,2048]{2,1,0:T(8,128)(2,1)S(1)}, u32[]{:S(2)}, u32[]{:S(2)}) collective-permute-start(bf16[4,8,2048]{2,1,0:T(8,128)(2,1)S(1)} %get-tuple-element.49), channel_id=1, source_target_pairs={{0,24},{4,28},{8,0},{12,4},{16,8},{20,12},{24,16},{28,20},{32,56},... | collective-permute-start | bytes 393224 | tf_op jit(solution)/shard_map/ppermute | solution.py:44
  114.6 3.1 %collective-permute-done.18 = bf16[4,8,2048]{2,1,0:T(8,128)(2,1)S(1)} collective-permute-done((bf16[4,8,2048]{2,1,0:T(8,128)(2,1)S(1)}, bf16[4,8,2048]{2,1,0:T(8,128)(2,1)S(1)}, u32[]{:S(2)}, u32[]{:S(2)}) %collective-permute-start.18) | collective-permute-done | bytes 131104 | tf_op jit(solution)/shard_map/ppermute | solution.py:44
  117.7 2.7 %collective-permute-done.19 = bf16[4,8,2048]{2,1,0:T(8,128)(2,1)S(1)} collective-permute-done((bf16[4,8,2048]{2,1,0:T(8,128)(2,1)S(1)}, bf16[4,8,2048]{2,1,0:T(8,128)(2,1)S(1)}, u32[]{:S(2)}, u32[]{:S(2)}) %collective-permute-start.19) | collective-permute-done | bytes 131104 | tf_op jit(solution)/shard_map/ppermute | solution.py:44
  121.1 2.6 %collective-permute-start.23 = (bf16[8,2048]{1,0:T(8,128)(2,1)S(1)}, bf16[8,2048]{1,0:T(8,128)(2,1)S(1)}, u32[]{:S(2)}, u32[]{:S(2)}) collective-permute-start(bf16[8,2048]{1,0:T(8,128)(2,1)S(1)} %get-tuple-element.62), channel_id=1, source_target_pairs={{0,96},{4,100},{8,104},{12,108},{16,112},{20,116},{24,120},{28,124... | collective-permute-start | bytes 98312 | tf_op jit(solution)/shard_map/ppermute | solution.py:44
  124.9 3.4 %collective-permute-done.22 = bf16[8,2048]{1,0:T(8,128)(2,1)S(1)} collective-permute-done((bf16[8,2048]{1,0:T(8,128)(2,1)S(1)}, bf16[8,2048]{1,0:T(8,128)(2,1)S(1)}, u32[]{:S(2)}, u32[]{:S(2)}) %collective-permute-start.22) | collective-permute-done | bytes 32800 | tf_op jit(solution)/shard_map/ppermute | solution.py:44
  128.4 3.4 %collective-permute-start.25 = (f32[8,2048]{1,0:T(8,128)S(1)}, f32[8,2048]{1,0:T(8,128)S(1)}, u32[]{:S(2)}, u32[]{:S(2)}) collective-permute-start(f32[8,2048]{1,0:T(8,128)S(1)} %fusion.34), channel_id=1, source_target_pairs={{0,2},{1,3},{2,0},{3,1},{4,6},{5,7},{6,4},{7,5},{8,10},{9,11},{10,... | collective-permute-start | bytes 196616 | tf_op jit(solution)/shard_map/ppermute | solution.py:44
  141.2 2.7 %collective-permute-start.30 = (bf16[4,8,2048]{2,1,0:T(8,128)(2,1)S(1)}, bf16[4,8,2048]{2,1,0:T(8,128)(2,1)S(1)}, u32[]{:S(2)}, u32[]{:S(2)}) collective-permute-start(bf16[4,8,2048]{2,1,0:T(8,128)(2,1)S(1)} %get-tuple-element.60), channel_id=1, source_target_pairs={{0,8},{4,12},{8,16},{12,20},{16,24},{20,28},{24,0},{28,4},{32,40},... | collective-permute-start | bytes 393224 | tf_op jit(solution)/shard_map/ppermute | solution.py:44
  147.8 7.6 %collective-permute-start.33 = (bf16[4,4,8,2048]{3,2,1,0:T(8,128)(2,1)S(1)}, bf16[4,4,8,2048]{3,2,1,0:T(8,128)(2,1)S(1)}, u32[]{:S(2)}, u32[]{:S(2)}) collective-permute-start(bf16[4,4,8,2048]{3,2,1,0:T(8,128)(2,1)S(1)} %pad_maximum_fusion.2), channel_id=1, source_target_pairs={{0,4},{4,0},{8,12},{12,8},{16,20},{20,16},{24,28},{28,24},{32,36},... | collective-permute-start | bytes 1572872 | tf_op jit(solution)/shard_map/ppermute | solution.py:44
  (158 shorter events, 60.9 us)
Async XLA Ops:
  39.3 9.9 %collective-permute-start = (f32[4,4,2,32,66]{4,3,2,1,0:T(8,128)}, f32[4,4,2,32,66]{4,3,2,1,0:T(8,128)S(1)}, u32[]{:S(2)}, u32[]{:S(2)}) collective-permute-start(f32[4,4,2,32,66]{4,3,2,1,0:T(8,128)} %get-tuple-element.47), channel_id=1, source_target_pairs={{0,4},{4,0},{8,12},{12,8},{16,20},{20,16},{24,28},{28,24},{32,36},... | collective-permute-start | bytes 811016 | tf_op jit(solution)/shard_map/ppermute | solution.py:44
  51.2 9.6 %collective-permute-start.3 = (f32[4,2,32,66]{3,2,1,0:T(8,128)S(1)}, f32[4,2,32,66]{3,2,1,0:T(8,128)S(1)}, u32[]{:S(2)}, u32[]{:S(2)}) collective-permute-start(f32[4,2,32,66]{3,2,1,0:T(8,128)S(1)} %get-tuple-element.52), channel_id=1, source_target_pairs={{0,24},{4,28},{8,0},{12,4},{16,8},{20,12},{24,16},{28,20},{32,56},... | collective-permute-start | bytes 202760 | tf_op jit(solution)/shard_map/ppermute | solution.py:44
  55.1 6.3 %collective-permute-start.2 = (f32[4,2,32,66]{3,2,1,0:T(8,128)S(1)}, f32[4,2,32,66]{3,2,1,0:T(8,128)S(1)}, u32[]{:S(2)}, u32[]{:S(2)}) collective-permute-start(f32[4,2,32,66]{3,2,1,0:T(8,128)S(1)} %get-tuple-element.53), channel_id=1, source_target_pairs={{0,16},{4,20},{8,24},{12,28},{16,0},{20,4},{24,8},{28,12},{32,48},... | collective-permute-start | bytes 202760 | tf_op jit(solution)/shard_map/ppermute | solution.py:44
  55.2 9.1 %collective-permute-start.1 = (f32[4,2,32,66]{3,2,1,0:T(8,128)S(1)}, f32[4,2,32,66]{3,2,1,0:T(8,128)S(1)}, u32[]{:S(2)}, u32[]{:S(2)}) collective-permute-start(f32[4,2,32,66]{3,2,1,0:T(8,128)S(1)} %get-tuple-element.54), channel_id=1, source_target_pairs={{0,8},{4,12},{8,16},{12,20},{16,24},{20,28},{24,0},{28,4},{32,40},... | collective-permute-start | bytes 202760 | tf_op jit(solution)/shard_map/ppermute | solution.py:44
  68.0 4.3 %collective-permute-start.5 = (f32[2,32,66]{2,1,0:T(8,128)S(1)}, f32[2,32,66]{2,1,0:T(8,128)S(1)}, u32[]{:S(2)}, u32[]{:S(2)}) collective-permute-start(f32[2,32,66]{2,1,0:T(8,128)S(1)} %get-tuple-element.68), channel_id=1, source_target_pairs={{0,64},{4,68},{8,72},{12,76},{16,80},{20,84},{24,88},{28,92},{32,9... | collective-permute-start | bytes 50696 | tf_op jit(solution)/shard_map/ppermute | solution.py:44
  74.7 6.1 %collective-permute-start.9 = (f32[8,2048]{1,0:T(8,128)S(1)}, f32[8,2048]{1,0:T(8,128)S(1)}, u32[]{:S(2)}, u32[]{:S(2)}) collective-permute-start(f32[8,2048]{1,0:T(8,128)S(1)} %fusion.95), channel_id=1, source_target_pairs={{0,1},{1,2},{2,3},{3,0},{4,5},{5,6},{6,7},{7,4},{8,9},{9,10},{10,1... | collective-permute-start | bytes 196616 | tf_op jit(solution)/shard_map/ppermute | solution.py:44
  76.0 5.0 %collective-permute-start.8 = (f32[8,2048]{1,0:T(8,128)S(1)}, f32[8,2048]{1,0:T(8,128)S(1)}, u32[]{:S(2)}, u32[]{:S(2)}) collective-permute-start(f32[8,2048]{1,0:T(8,128)S(1)} %fusion.95), channel_id=1, source_target_pairs={{0,2},{1,3},{2,0},{3,1},{4,6},{5,7},{6,4},{7,5},{8,10},{9,11},{10,... | collective-permute-start | bytes 196616 | tf_op jit(solution)/shard_map/ppermute | solution.py:44
  82.3 4.3 %collective-permute-start.11 = (bf16[8,2048]{1,0:T(8,128)(2,1)S(1)}, bf16[8,2048]{1,0:T(8,128)(2,1)S(1)}, u32[]{:S(2)}, u32[]{:S(2)}) collective-permute-start(bf16[8,2048]{1,0:T(8,128)(2,1)S(1)} %fusion.30), channel_id=1, source_target_pairs={{0,64},{4,68},{8,72},{12,76},{16,80},{20,84},{24,88},{28,92},{32,9... | collective-permute-start | bytes 98312 | tf_op jit(solution)/shard_map/ppermute | solution.py:44
  87.5 5.5 %collective-permute-start.14 = (bf16[4,8,2048]{2,1,0:T(8,128)(2,1)S(1)}, bf16[4,8,2048]{2,1,0:T(8,128)(2,1)S(1)}, u32[]{:S(2)}, u32[]{:S(2)}) collective-permute-start(bf16[4,8,2048]{2,1,0:T(8,128)(2,1)S(1)} %get-tuple-element.65), channel_id=1, source_target_pairs={{0,16},{4,20},{8,24},{12,28},{16,0},{20,4},{24,8},{28,12},{32,48},... | collective-permute-start | bytes 393224 | tf_op jit(solution)/shard_map/ppermute | solution.py:44
  88.4 5.9 %collective-permute-start.13 = (bf16[4,8,2048]{2,1,0:T(8,128)(2,1)S(1)}, bf16[4,8,2048]{2,1,0:T(8,128)(2,1)S(1)}, u32[]{:S(2)}, u32[]{:S(2)}) collective-permute-start(bf16[4,8,2048]{2,1,0:T(8,128)(2,1)S(1)} %get-tuple-element.65), channel_id=1, source_target_pairs={{0,8},{4,12},{8,16},{12,20},{16,24},{20,28},{24,0},{28,4},{32,40},... | collective-permute-start | bytes 393224 | tf_op jit(solution)/shard_map/ppermute | solution.py:44
  88.4 5.9 %collective-permute-start.15 = (bf16[4,8,2048]{2,1,0:T(8,128)(2,1)S(1)}, bf16[4,8,2048]{2,1,0:T(8,128)(2,1)S(1)}, u32[]{:S(2)}, u32[]{:S(2)}) collective-permute-start(bf16[4,8,2048]{2,1,0:T(8,128)(2,1)S(1)} %get-tuple-element.65), channel_id=1, source_target_pairs={{0,24},{4,28},{8,0},{12,4},{16,8},{20,12},{24,16},{28,20},{32,56},... | collective-permute-start | bytes 393224 | tf_op jit(solution)/shard_map/ppermute | solution.py:44
  94.4 8.1 %collective-permute-start.16 = (bf16[4,4,8,2048]{3,2,1,0:T(8,128)(2,1)S(1)}, bf16[4,4,8,2048]{3,2,1,0:T(8,128)(2,1)S(1)}, u32[]{:S(2)}, u32[]{:S(2)}) collective-permute-start(bf16[4,4,8,2048]{3,2,1,0:T(8,128)(2,1)S(1)} %pad_maximum_fusion.1), channel_id=1, source_target_pairs={{0,4},{4,0},{8,12},{12,8},{16,20},{20,16},{24,28},{28,24},{32,36},... | collective-permute-start | bytes 1572872 | tf_op jit(solution)/shard_map/ppermute | solution.py:44
  111.5 6.2 %collective-permute-start.18 = (bf16[4,8,2048]{2,1,0:T(8,128)(2,1)S(1)}, bf16[4,8,2048]{2,1,0:T(8,128)(2,1)S(1)}, u32[]{:S(2)}, u32[]{:S(2)}) collective-permute-start(bf16[4,8,2048]{2,1,0:T(8,128)(2,1)S(1)} %get-tuple-element.48), channel_id=1, source_target_pairs={{0,8},{4,12},{8,16},{12,20},{16,24},{20,28},{24,0},{28,4},{32,40},... | collective-permute-start | bytes 393224 | tf_op jit(solution)/shard_map/ppermute | solution.py:44
  111.9 5.8 %collective-permute-start.20 = (bf16[4,8,2048]{2,1,0:T(8,128)(2,1)S(1)}, bf16[4,8,2048]{2,1,0:T(8,128)(2,1)S(1)}, u32[]{:S(2)}, u32[]{:S(2)}) collective-permute-start(bf16[4,8,2048]{2,1,0:T(8,128)(2,1)S(1)} %get-tuple-element.49), channel_id=1, source_target_pairs={{0,24},{4,28},{8,0},{12,4},{16,8},{20,12},{24,16},{28,20},{32,56},... | collective-permute-start | bytes 393224 | tf_op jit(solution)/shard_map/ppermute | solution.py:44
  114.3 6.2 %collective-permute-start.19 = (bf16[4,8,2048]{2,1,0:T(8,128)(2,1)S(1)}, bf16[4,8,2048]{2,1,0:T(8,128)(2,1)S(1)}, u32[]{:S(2)}, u32[]{:S(2)}) collective-permute-start(bf16[4,8,2048]{2,1,0:T(8,128)(2,1)S(1)} %get-tuple-element.50), channel_id=1, source_target_pairs={{0,16},{4,20},{8,24},{12,28},{16,0},{20,4},{24,8},{28,12},{32,48},... | collective-permute-start | bytes 393224 | tf_op jit(solution)/shard_map/ppermute | solution.py:44
  120.6 4.3 %collective-permute-start.21 = (bf16[8,2048]{1,0:T(8,128)(2,1)S(1)}, bf16[8,2048]{1,0:T(8,128)(2,1)S(1)}, u32[]{:S(2)}, u32[]{:S(2)}) collective-permute-start(bf16[8,2048]{1,0:T(8,128)(2,1)S(1)} %get-tuple-element.61), channel_id=1, source_target_pairs={{0,32},{4,36},{8,40},{12,44},{16,48},{20,52},{24,56},{28,60},{32,6... | collective-permute-start | bytes 98312 | tf_op jit(solution)/shard_map/ppermute | solution.py:44
  123.7 4.6 %collective-permute-start.22 = (bf16[8,2048]{1,0:T(8,128)(2,1)S(1)}, bf16[8,2048]{1,0:T(8,128)(2,1)S(1)}, u32[]{:S(2)}, u32[]{:S(2)}) collective-permute-start(bf16[8,2048]{1,0:T(8,128)(2,1)S(1)} %get-tuple-element.63), channel_id=1, source_target_pairs={{0,64},{4,68},{8,72},{12,76},{16,80},{20,84},{24,88},{28,92},{32,9... | collective-permute-start | bytes 98312 | tf_op jit(solution)/shard_map/ppermute | solution.py:44
  128.3 4.4 %collective-permute-start.26 = (f32[8,2048]{1,0:T(8,128)S(1)}, f32[8,2048]{1,0:T(8,128)S(1)}, u32[]{:S(2)}, u32[]{:S(2)}) collective-permute-start(f32[8,2048]{1,0:T(8,128)S(1)} %fusion.34), channel_id=1, source_target_pairs={{0,1},{1,2},{2,3},{3,0},{4,5},{5,6},{6,7},{7,4},{8,9},{9,10},{10,1... | collective-permute-start | bytes 196616 | tf_op jit(solution)/shard_map/ppermute | solution.py:44
  128.4 5.8 %collective-permute-start.25 = (f32[8,2048]{1,0:T(8,128)S(1)}, f32[8,2048]{1,0:T(8,128)S(1)}, u32[]{:S(2)}, u32[]{:S(2)}) collective-permute-start(f32[8,2048]{1,0:T(8,128)S(1)} %fusion.34), channel_id=1, source_target_pairs={{0,2},{1,3},{2,0},{3,1},{4,6},{5,7},{6,4},{7,5},{8,10},{9,11},{10,... | collective-permute-start | bytes 196616 | tf_op jit(solution)/shard_map/ppermute | solution.py:44
  136.1 4.3 %collective-permute-start.28 = (bf16[8,2048]{1,0:T(8,128)(2,1)S(1)}, bf16[8,2048]{1,0:T(8,128)(2,1)S(1)}, u32[]{:S(2)}, u32[]{:S(2)}) collective-permute-start(bf16[8,2048]{1,0:T(8,128)(2,1)S(1)} %fusion.31), channel_id=1, source_target_pairs={{0,64},{4,68},{8,72},{12,76},{16,80},{20,84},{24,88},{28,92},{32,9... | collective-permute-start | bytes 98312 | tf_op jit(solution)/shard_map/ppermute | solution.py:44
  136.1 4.6 %collective-permute-start.27 = (bf16[8,2048]{1,0:T(8,128)(2,1)S(1)}, bf16[8,2048]{1,0:T(8,128)(2,1)S(1)}, u32[]{:S(2)}, u32[]{:S(2)}) collective-permute-start(bf16[8,2048]{1,0:T(8,128)(2,1)S(1)} %fusion.31), channel_id=1, source_target_pairs={{0,32},{4,36},{8,40},{12,44},{16,48},{20,52},{24,56},{28,60},{32,6... | collective-permute-start | bytes 98312 | tf_op jit(solution)/shard_map/ppermute | solution.py:44
  140.8 5.5 %collective-permute-start.31 = (bf16[4,8,2048]{2,1,0:T(8,128)(2,1)S(1)}, bf16[4,8,2048]{2,1,0:T(8,128)(2,1)S(1)}, u32[]{:S(2)}, u32[]{:S(2)}) collective-permute-start(bf16[4,8,2048]{2,1,0:T(8,128)(2,1)S(1)} %get-tuple-element.60), channel_id=1, source_target_pairs={{0,16},{4,20},{8,24},{12,28},{16,0},{20,4},{24,8},{28,12},{32,48},... | collective-permute-start | bytes 393224 | tf_op jit(solution)/shard_map/ppermute | solution.py:44
  141.2 6.4 %collective-permute-start.30 = (bf16[4,8,2048]{2,1,0:T(8,128)(2,1)S(1)}, bf16[4,8,2048]{2,1,0:T(8,128)(2,1)S(1)}, u32[]{:S(2)}, u32[]{:S(2)}) collective-permute-start(bf16[4,8,2048]{2,1,0:T(8,128)(2,1)S(1)} %get-tuple-element.60), channel_id=1, source_target_pairs={{0,8},{4,12},{8,16},{12,20},{16,24},{20,28},{24,0},{28,4},{32,40},... | collective-permute-start | bytes 393224 | tf_op jit(solution)/shard_map/ppermute | solution.py:44
  147.8 9.1 %collective-permute-start.33 = (bf16[4,4,8,2048]{3,2,1,0:T(8,128)(2,1)S(1)}, bf16[4,4,8,2048]{3,2,1,0:T(8,128)(2,1)S(1)}, u32[]{:S(2)}, u32[]{:S(2)}) collective-permute-start(bf16[4,4,8,2048]{3,2,1,0:T(8,128)(2,1)S(1)} %pad_maximum_fusion.2), channel_id=1, source_target_pairs={{0,4},{4,0},{8,12},{12,8},{16,20},{20,16},{24,28},{28,24},{32,36},... | collective-permute-start | bytes 1572872 | tf_op jit(solution)/shard_map/ppermute | solution.py:44
  (25 other events, 228.3 us)

commit v3 on v2

--- a/solution.py
+++ b/solution.py
@@ -65,15 +65,6 @@
         total_all = total_all + p[..., head_dim + 1] * factor
         mixed_all = mixed_all + p[..., :head_dim] * factor[..., None]
     return jnp.concatenate([mixed_all, top_all[..., None], total_all[..., None]], axis=-1)
-
-
-def sum_scatter_abs(x, level):
-    size = level[2]
-    c = coord(level)
-    acc = take(x, c)
-    for d in range(1, size):
-        acc = acc + shifted(take(x, (c + d) % size), level, d)
-    return acc
 
 
 def sum_all_ordered(x, level):
@@ -157,8 +148,10 @@
     req, rows, width = spread.shape
     shard_len = keys.shape[1]
     grid = (req // BLOCK_REQ,)
+
     def blk(b, s, l):
         return (b, 0, 0)
+
     return pl.pallas_call(
         cache_kernel,
         out_shape=jax.ShapeDtypeStruct((req, rows, head_dim + 2), jnp.float32),
@@ -188,7 +181,7 @@
     return cache_attention(start, lengths_sel, spread, keys_sel, values_sel, head_dim)
 
 
-def local(
+def local_body(
     hidden_in,
     lengths,
     request_perm,
@@ -216,6 +209,21 @@
     query_raw = jnp.dot(normed, w_query, preferred_element_type=jnp.float32).reshape(
         step_count, request_count, local_heads, HD
     )
+    queries = (
+        rotate(query_raw, positions)
+        .astype(jnp.bfloat16)
+        .reshape(step_count, request_count, local_kv, group_size, HD)
+    )
+    offsets = request_perm * S_CAP // request_count
+    slot_base = lax.axis_index("seq") * shard_len
+    packed = attend_shard(queries, k_cache, v_cache, lengths, offsets, slot_base)
+
+    own_count = request_count // (2 * 4 * 4)
+    first_req = ((coord(CORE) * 4 + coord(ZAX)) * 4 + coord(XAX)) * own_count
+
+    def own(x):
+        return lax.dynamic_slice_in_dim(x, first_req, own_count, axis=1)
+
     key_raw = jnp.dot(normed, w_key, preferred_element_type=jnp.float32).reshape(
         step_count, request_count, local_kv, HD
     )
@@ -224,15 +232,17 @@
         .astype(jnp.bfloat16)
         .reshape(step_count, request_count, local_kv, HD)
     )
-    queries = (
-        rotate(query_raw, positions)
-        .astype(jnp.bfloat16)
-        .reshape(step_count, request_count, local_kv, group_size, HD)
-    )
     key_new = rotate(key_raw, positions).astype(jnp.bfloat16)
-    offsets = request_perm * S_CAP // request_count
-    slot_base = lax.axis_index("seq") * shard_len
-    packed = attend_shard(queries, k_cache, v_cache, lengths, offsets, slot_base)
+    queries_own = own(queries)
+    key_own = own(key_new)
+    value_own = own(value_new)
+    causal = jnp.arange(step_count)[None, :] <= jnp.arange(step_count)[:, None]
+    causal_full = causal[None, None, :, None, :]
+    new_scores = (
+        jnp.einsum("trkgd,urkd->rktgu", queries_own, key_own, preferred_element_type=jnp.float32)
+        * attn_scale
+    )
+    top_new = jnp.max(jnp.where(causal_full, new_scores, neg_large), axis=-1)
 
     levels = (CORE, ZAX, XAX)
     packed = packed.reshape((2, 4, 4, -1) + packed.shape[1:])
@@ -242,22 +252,6 @@
     top_s = packed[..., HD].reshape(own_shape)
     total_s = packed[..., HD + 1].reshape(own_shape)
     mixed_s = packed[..., :HD].reshape(own_shape + (HD,))
-    own_count = top_s.shape[0]
-    first_req = ((coord(CORE) * 4 + coord(ZAX)) * 4 + coord(XAX)) * own_count
-
-    def own(x):
-        return lax.dynamic_slice_in_dim(x, first_req, own_count, axis=1)
-
-    queries_own = own(queries)
-    key_own = own(key_new)
-    value_own = own(value_new)
-    causal = jnp.arange(step_count)[None, :] <= jnp.arange(step_count)[:, None]
-    causal_full = causal[None, None, :, None, :]
-    new_scores = (
-        jnp.einsum("trkgd,urkd->rktgu", queries_own, key_own, preferred_element_type=jnp.float32)
-        * attn_scale
-    )
-    top_new = jnp.max(jnp.where(causal_full, new_scores, neg_large), axis=-1)
     top_final = jnp.maximum(top_s, top_new)
     new_weights = jnp.where(causal_full, jnp.exp(new_scores - top_final[..., None]), 0.0)
     new_mixed = jnp.einsum(
@@ -356,7 +350,7 @@
         P(("seq", "tp"), None),
     )
     return jax.shard_map(
-        local,
+        local_body,
         mesh=mesh,
         in_specs=placed,
         out_specs=(P(), P(None, None, "tp"), P(None, None, "tp")),

time: 159 us -> 159 us (level)
  no operation moved by 1% of the time
where the time goes in v3:
time: 159 us
  starting transfers between devices  52.5 us (33%)
  waiting for transfers between devices  39.6 us (25%)
  Pallas kernels  20.3 us (13%)
  matrix products  16.7 us (11%)
  other arithmetic  15.6 us (10%)
  local copies, waits for them, and re-layouts  12.8 us (8%)
    ppermute x34, starting transfers between devices, shifted(): return lax.ppermute(x, level[0], shift_perm(level, d))  52.5 us
    ppermute x34, waiting for transfers between devices, shifted(): return lax.ppermute(x, level[0], shift_perm(level, d))  39.6 us
    pallas_call x1, Pallas kernels, cache_attention(): pl.pallas_call(cache_kernel, out_shape=jax.ShapeDtypeStruct((req, rows, h...  20.3 us
    unnamed x33, local copies, waits for them, and re-layouts  6.88 us
    dot_general x2, matrix products, feed(): jnp.dot(hidden, w_down, preferred_element_type=jnp.float32)  5.7 us
  transfers between devices with their start and end apart: 34, of which 26 were waited for; matrix products, arithmetic and copies ran while one was open for 9% of the time, Pallas kernels for 0%

profile of v3, /device:TPU:1, one launch (start us, length us, event | category | flops | bytes accessed | tf_op | source)
XLA Modules:
  0.0 158.8 jit_solution(16102676016827341551)
XLA Ops:
  3.7 4.0 %copy.65 = bf16[2048,512]{0,1:T(8,128)(2,1)} copy(bf16[2048,512]{1,0:T(8,128)(2,1)} %param.20) | data formatting | bytes 4194304 | tf_op args[6]
  8.1 2.9 %fusion.10 = f32[4,64,8,64]{1,3,2,0:T(8,128)S(1)} fusion(bf16[8,64,2048,1]{2,1,0,3:T(8,128)(2,1)} %bitcast.160, f32[2048]{0:T(1024)S(1)} %convert_element_type.131, f32[4,64]{1,0:T(4,128)S(1)} %add_rsqrt_fusion, bf16[4,64,2048]{2,1,0:T(8,128)(2,1)S(1)} %copy-done.5), kind=kOutput, calls=%fused_computation.18 | convolution fusion | flops 538968064 | bytes 3679232 | tf_op jit(solution)/shard_map/dot_general | solution.py:209
  16.8 20.3 %shard_map.157 = f32[64,32,66]{2,1,0:T(8,128)} custom-call(s32[64]{0:T(128)} %and_select_fusion.start_ref, s32[64]{0:T(128)} %len_ref.1, bf16[64,32,128]{2,1,0:T(8,128)(2,1)} %fusion.12.q_ref, bf16[64,512,128]{2,1,0:T(8,128)(2,1)} %k_ref.1, bf16[64,512,128]{2,1,0:T(8,128)(2,1)} %v_ref.1), custom_call_target="tpu_custom_call" | custom-call | tf_op jit(solution)/shard_map/pallas_call | solution.py:155
  37.2 2.1 %dynamic-slice_bitcast_fusion.1 = (f32[4,4,2,32,66]{4,3,2,1,0:T(8,128)S(1)}, f32[4,4,2,32,66]{4,3,2,1,0:T(8,128)}) fusion(f32[2,4,4,2,32,66]{5,4,3,2,1,0:T(8,128)} %bitcast.159, s32[]{:T(128)S(6)} %select_n.441, s32[]{:T(128)S(6)} %select_n.443), kind=kLoop, calls=%fused_computation.33 | loop fusion | bytes 1081352 | tf_op jit(solution)/shard_map/jit(dynamic_index_in_dim)/squeeze | solution.py:48
  42.8 2.2 %fusion.8 = f32[4,64,2,64]{1,3,2,0:T(8,128)S(1)} fusion(bf16[2,64,2048,1]{2,1,0,3:T(8,128)(2,1)} %bitcast.170, f32[2048]{0:T(1024)S(1)} %convert_element_type.131, f32[4,64]{1,0:T(4,128)S(1)} %add_rsqrt_fusion, bf16[4,64,2048]{2,1,0:T(8,128)(2,1)} %param.14), kind=kOutput, calls=%fused_computation.17 | convolution fusion | flops 136314880 | bytes 1713152 | tf_op jit(solution)/shard_map/dot_general | solution.py:227
  51.2 3.9 %collective-permute-start.3 = (f32[4,2,32,66]{3,2,1,0:T(8,128)S(1)}, f32[4,2,32,66]{3,2,1,0:T(8,128)S(1)}, u32[]{:S(2)}, u32[]{:S(2)}) collective-permute-start(f32[4,2,32,66]{3,2,1,0:T(8,128)S(1)} %get-tuple-element.52), channel_id=1, source_target_pairs={{0,24},{4,28},{8,0},{12,4},{16,8},{20,12},{24,16},{28,20},{32,56},... | collective-permute-start | bytes 202760 | tf_op jit(solution)/shard_map/ppermute | solution.py:44
  56.4 4.4 %collective-permute-done.3 = f32[4,2,32,66]{3,2,1,0:T(8,128)S(1)} collective-permute-done((f32[4,2,32,66]{3,2,1,0:T(8,128)S(1)}, f32[4,2,32,66]{3,2,1,0:T(8,128)S(1)}, u32[]{:S(2)}, u32[]{:S(2)}) %collective-permute-start.3) | collective-permute-done | bytes 67616 | tf_op jit(solution)/shard_map/ppermute | solution.py:44
  61.5 2.8 %collective-permute-done.1 = f32[4,2,32,66]{3,2,1,0:T(8,128)S(1)} collective-permute-done((f32[4,2,32,66]{3,2,1,0:T(8,128)S(1)}, f32[4,2,32,66]{3,2,1,0:T(8,128)S(1)}, u32[]{:S(2)}, u32[]{:S(2)}) %collective-permute-start.1) | collective-permute-done | bytes 67616 | tf_op jit(solution)/shard_map/ppermute | solution.py:44
  65.5 2.5 %collective-permute-start.6 = (f32[2,32,66]{2,1,0:T(8,128)S(1)}, f32[2,32,66]{2,1,0:T(8,128)S(1)}, u32[]{:S(2)}, u32[]{:S(2)}) collective-permute-start(f32[2,32,66]{2,1,0:T(8,128)S(1)} %get-tuple-element.67), channel_id=1, source_target_pairs={{0,96},{4,100},{8,104},{12,108},{16,112},{20,116},{24,120},{28,124... | collective-permute-start | bytes 50696 | tf_op jit(solution)/shard_map/ppermute | solution.py:44
  69.2 3.1 %collective-permute-done.5 = f32[2,32,66]{2,1,0:T(8,128)S(1)} collective-permute-done((f32[2,32,66]{2,1,0:T(8,128)S(1)}, f32[2,32,66]{2,1,0:T(8,128)S(1)}, u32[]{:S(2)}, u32[]{:S(2)}) %collective-permute-start.5) | collective-permute-done | bytes 16928 | tf_op jit(solution)/shard_map/ppermute | solution.py:44
  76.0 2.6 %collective-permute-start.8 = (f32[8,2048]{1,0:T(8,128)S(1)}, f32[8,2048]{1,0:T(8,128)S(1)}, u32[]{:S(2)}, u32[]{:S(2)}) collective-permute-start(f32[8,2048]{1,0:T(8,128)S(1)} %fusion.95), channel_id=1, source_target_pairs={{0,2},{1,3},{2,0},{3,1},{4,6},{5,7},{6,4},{7,5},{8,10},{9,11},{10,... | collective-permute-start | bytes 196616 | tf_op jit(solution)/shard_map/ppermute | solution.py:44
  83.5 2.7 %collective-permute-start.12 = (bf16[8,2048]{1,0:T(8,128)(2,1)S(1)}, bf16[8,2048]{1,0:T(8,128)(2,1)S(1)}, u32[]{:S(2)}, u32[]{:S(2)}) collective-permute-start(bf16[8,2048]{1,0:T(8,128)(2,1)S(1)} %fusion.30), channel_id=1, source_target_pairs={{0,96},{4,100},{8,104},{12,108},{16,112},{20,116},{24,120},{28,124... | collective-permute-start | bytes 98312 | tf_op jit(solution)/shard_map/ppermute | solution.py:44
  88.4 2.7 %collective-permute-start.15 = (bf16[4,8,2048]{2,1,0:T(8,128)(2,1)S(1)}, bf16[4,8,2048]{2,1,0:T(8,128)(2,1)S(1)}, u32[]{:S(2)}, u32[]{:S(2)}) collective-permute-start(bf16[4,8,2048]{2,1,0:T(8,128)(2,1)S(1)} %get-tuple-element.65), channel_id=1, source_target_pairs={{0,24},{4,28},{8,0},{12,4},{16,8},{20,12},{24,16},{28,20},{32,56},... | collective-permute-start | bytes 393224 | tf_op jit(solution)/shard_map/ppermute | solution.py:44
  94.4 6.6 %collective-permute-start.16 = (bf16[4,4,8,2048]{3,2,1,0:T(8,128)(2,1)S(1)}, bf16[4,4,8,2048]{3,2,1,0:T(8,128)(2,1)S(1)}, u32[]{:S(2)}, u32[]{:S(2)}) collective-permute-start(bf16[4,4,8,2048]{3,2,1,0:T(8,128)(2,1)S(1)} %pad_maximum_fusion.1), channel_id=1, source_target_pairs={{0,4},{4,0},{8,12},{12,8},{16,20},{20,16},{24,28},{28,24},{32,36},... | collective-permute-start | bytes 1572872 | tf_op jit(solution)/shard_map/ppermute | solution.py:44
  103.4 2.9 %fusion.55 = f32[128,2048]{1,0:T(8,128)} fusion(bf16[64,2048]{1,0:T(8,128)(2,1)} %param.27, f32[128,64]{0,1:T(8,128)} %fusion.97, bf16[128,2048]{1,0:T(8,128)(2,1)S(1)} %bitcast.164, bf16[64,2048]{1,0:T(8,128)(2,1)} %param.26), kind=kOutput, calls=%fused_computation.145 | convolution fusion | flops 67158016 | bytes 2129920 | tf_op jit(solution)/shard_map/dot_general | solution.py:294
  106.9 2.8 %fusion.4 = f32[128,2048]{1,0:T(8,128)} fusion(bf16[64,2048]{1,0:T(8,128)(2,1)} %param.27, bf16[128,2048]{1,0:T(8,128)(2,1)S(1)} %bitcast.157, bf16[64,2048]{1,0:T(8,128)(2,1)} %param.26, f32[128,64]{0,1:T(8,128)S(1)} %fusion.96), kind=kOutput, calls=%fused_computation.11 | convolution fusion | flops 67158016 | bytes 2129920 | tf_op jit(solution)/shard_map/dot_general | solution.py:294
  111.9 2.4 %collective-permute-start.20 = (bf16[4,8,2048]{2,1,0:T(8,128)(2,1)S(1)}, bf16[4,8,2048]{2,1,0:T(8,128)(2,1)S(1)}, u32[]{:S(2)}, u32[]{:S(2)}) collective-permute-start(bf16[4,8,2048]{2,1,0:T(8,128)(2,1)S(1)} %get-tuple-element.49), channel_id=1, source_target_pairs={{0,24},{4,28},{8,0},{12,4},{16,8},{20,12},{24,16},{28,20},{32,56},... | collective-permute-start | bytes 393224 | tf_op jit(solution)/shard_map/ppermute | solution.py:44
  114.6 3.1 %collective-permute-done.18 = bf16[4,8,2048]{2,1,0:T(8,128)(2,1)S(1)} collective-permute-done((bf16[4,8,2048]{2,1,0:T(8,128)(2,1)S(1)}, bf16[4,8,2048]{2,1,0:T(8,128)(2,1)S(1)}, u32[]{:S(2)}, u32[]{:S(2)}) %collective-permute-start.18) | collective-permute-done | bytes 131104 | tf_op jit(solution)/shard_map/ppermute | solution.py:44
  117.7 2.7 %collective-permute-done.19 = bf16[4,8,2048]{2,1,0:T(8,128)(2,1)S(1)} collective-permute-done((bf16[4,8,2048]{2,1,0:T(8,128)(2,1)S(1)}, bf16[4,8,2048]{2,1,0:T(8,128)(2,1)S(1)}, u32[]{:S(2)}, u32[]{:S(2)}) %collective-permute-start.19) | collective-permute-done | bytes 131104 | tf_op jit(solution)/shard_map/ppermute | solution.py:44
  121.1 2.6 %collective-permute-start.23 = (bf16[8,2048]{1,0:T(8,128)(2,1)S(1)}, bf16[8,2048]{1,0:T(8,128)(2,1)S(1)}, u32[]{:S(2)}, u32[]{:S(2)}) collective-permute-start(bf16[8,2048]{1,0:T(8,128)(2,1)S(1)} %get-tuple-element.62), channel_id=1, source_target_pairs={{0,96},{4,100},{8,104},{12,108},{16,112},{20,116},{24,120},{28,124... | collective-permute-start | bytes 98312 | tf_op jit(solution)/shard_map/ppermute | solution.py:44
  124.9 3.4 %collective-permute-done.22 = bf16[8,2048]{1,0:T(8,128)(2,1)S(1)} collective-permute-done((bf16[8,2048]{1,0:T(8,128)(2,1)S(1)}, bf16[8,2048]{1,0:T(8,128)(2,1)S(1)}, u32[]{:S(2)}, u32[]{:S(2)}) %collective-permute-start.22) | collective-permute-done | bytes 32800 | tf_op jit(solution)/shard_map/ppermute | solution.py:44
  128.4 3.4 %collective-permute-start.25 = (f32[8,2048]{1,0:T(8,128)S(1)}, f32[8,2048]{1,0:T(8,128)S(1)}, u32[]{:S(2)}, u32[]{:S(2)}) collective-permute-start(f32[8,2048]{1,0:T(8,128)S(1)} %fusion.34), channel_id=1, source_target_pairs={{0,2},{1,3},{2,0},{3,1},{4,6},{5,7},{6,4},{7,5},{8,10},{9,11},{10,... | collective-permute-start | bytes 196616 | tf_op jit(solution)/shard_map/ppermute | solution.py:44
  141.2 2.7 %collective-permute-start.30 = (bf16[4,8,2048]{2,1,0:T(8,128)(2,1)S(1)}, bf16[4,8,2048]{2,1,0:T(8,128)(2,1)S(1)}, u32[]{:S(2)}, u32[]{:S(2)}) collective-permute-start(bf16[4,8,2048]{2,1,0:T(8,128)(2,1)S(1)} %get-tuple-element.60), channel_id=1, source_target_pairs={{0,8},{4,12},{8,16},{12,20},{16,24},{20,28},{24,0},{28,4},{32,40},... | collective-permute-start | bytes 393224 | tf_op jit(solution)/shard_map/ppermute | solution.py:44
  147.8 7.6 %collective-permute-start.33 = (bf16[4,4,8,2048]{3,2,1,0:T(8,128)(2,1)S(1)}, bf16[4,4,8,2048]{3,2,1,0:T(8,128)(2,1)S(1)}, u32[]{:S(2)}, u32[]{:S(2)}) collective-permute-start(bf16[4,4,8,2048]{3,2,1,0:T(8,128)(2,1)S(1)} %pad_maximum_fusion.2), channel_id=1, source_target_pairs={{0,4},{4,0},{8,12},{12,8},{16,20},{20,16},{24,28},{28,24},{32,36},... | collective-permute-start | bytes 1572872 | tf_op jit(solution)/shard_map/ppermute | solution.py:44
  (158 shorter events, 60.9 us)
Async XLA Ops:
  39.3 9.9 %collective-permute-start = (f32[4,4,2,32,66]{4,3,2,1,0:T(8,128)}, f32[4,4,2,32,66]{4,3,2,1,0:T(8,128)S(1)}, u32[]{:S(2)}, u32[]{:S(2)}) collective-permute-start(f32[4,4,2,32,66]{4,3,2,1,0:T(8,128)} %get-tuple-element.47), channel_id=1, source_target_pairs={{0,4},{4,0},{8,12},{12,8},{16,20},{20,16},{24,28},{28,24},{32,36},... | collective-permute-start | bytes 811016 | tf_op jit(solution)/shard_map/ppermute | solution.py:44
  51.2 9.6 %collective-permute-start.3 = (f32[4,2,32,66]{3,2,1,0:T(8,128)S(1)}, f32[4,2,32,66]{3,2,1,0:T(8,128)S(1)}, u32[]{:S(2)}, u32[]{:S(2)}) collective-permute-start(f32[4,2,32,66]{3,2,1,0:T(8,128)S(1)} %get-tuple-element.52), channel_id=1, source_target_pairs={{0,24},{4,28},{8,0},{12,4},{16,8},{20,12},{24,16},{28,20},{32,56},... | collective-permute-start | bytes 202760 | tf_op jit(solution)/shard_map/ppermute | solution.py:44
  55.1 6.3 %collective-permute-start.2 = (f32[4,2,32,66]{3,2,1,0:T(8,128)S(1)}, f32[4,2,32,66]{3,2,1,0:T(8,128)S(1)}, u32[]{:S(2)}, u32[]{:S(2)}) collective-permute-start(f32[4,2,32,66]{3,2,1,0:T(8,128)S(1)} %get-tuple-element.53), channel_id=1, source_target_pairs={{0,16},{4,20},{8,24},{12,28},{16,0},{20,4},{24,8},{28,12},{32,48},... | collective-permute-start | bytes 202760 | tf_op jit(solution)/shard_map/ppermute | solution.py:44
  55.2 9.1 %collective-permute-start.1 = (f32[4,2,32,66]{3,2,1,0:T(8,128)S(1)}, f32[4,2,32,66]{3,2,1,0:T(8,128)S(1)}, u32[]{:S(2)}, u32[]{:S(2)}) collective-permute-start(f32[4,2,32,66]{3,2,1,0:T(8,128)S(1)} %get-tuple-element.54), channel_id=1, source_target_pairs={{0,8},{4,12},{8,16},{12,20},{16,24},{20,28},{24,0},{28,4},{32,40},... | collective-permute-start | bytes 202760 | tf_op jit(solution)/shard_map/ppermute | solution.py:44
  68.0 4.3 %collective-permute-start.5 = (f32[2,32,66]{2,1,0:T(8,128)S(1)}, f32[2,32,66]{2,1,0:T(8,128)S(1)}, u32[]{:S(2)}, u32[]{:S(2)}) collective-permute-start(f32[2,32,66]{2,1,0:T(8,128)S(1)} %get-tuple-element.68), channel_id=1, source_target_pairs={{0,64},{4,68},{8,72},{12,76},{16,80},{20,84},{24,88},{28,92},{32,9... | collective-permute-start | bytes 50696 | tf_op jit(solution)/shard_map/ppermute | solution.py:44
  74.7 6.1 %collective-permute-start.9 = (f32[8,2048]{1,0:T(8,128)S(1)}, f32[8,2048]{1,0:T(8,128)S(1)}, u32[]{:S(2)}, u32[]{:S(2)}) collective-permute-start(f32[8,2048]{1,0:T(8,128)S(1)} %fusion.95), channel_id=1, source_target_pairs={{0,1},{1,2},{2,3},{3,0},{4,5},{5,6},{6,7},{7,4},{8,9},{9,10},{10,1... | collective-permute-start | bytes 196616 | tf_op jit(solution)/shard_map/ppermute | solution.py:44
  76.0 5.0 %collective-permute-start.8 = (f32[8,2048]{1,0:T(8,128)S(1)}, f32[8,2048]{1,0:T(8,128)S(1)}, u32[]{:S(2)}, u32[]{:S(2)}) collective-permute-start(f32[8,2048]{1,0:T(8,128)S(1)} %fusion.95), channel_id=1, source_target_pairs={{0,2},{1,3},{2,0},{3,1},{4,6},{5,7},{6,4},{7,5},{8,10},{9,11},{10,... | collective-permute-start | bytes 196616 | tf_op jit(solution)/shard_map/ppermute | solution.py:44
  82.3 4.3 %collective-permute-start.11 = (bf16[8,2048]{1,0:T(8,128)(2,1)S(1)}, bf16[8,2048]{1,0:T(8,128)(2,1)S(1)}, u32[]{:S(2)}, u32[]{:S(2)}) collective-permute-start(bf16[8,2048]{1,0:T(8,128)(2,1)S(1)} %fusion.30), channel_id=1, source_target_pairs={{0,64},{4,68},{8,72},{12,76},{16,80},{20,84},{24,88},{28,92},{32,9... | collective-permute-start | bytes 98312 | tf_op jit(solution)/shard_map/ppermute | solution.py:44
  87.5 5.5 %collective-permute-start.14 = (bf16[4,8,2048]{2,1,0:T(8,128)(2,1)S(1)}, bf16[4,8,2048]{2,1,0:T(8,128)(2,1)S(1)}, u32[]{:S(2)}, u32[]{:S(2)}) collective-permute-start(bf16[4,8,2048]{2,1,0:T(8,128)(2,1)S(1)} %get-tuple-element.65), channel_id=1, source_target_pairs={{0,16},{4,20},{8,24},{12,28},{16,0},{20,4},{24,8},{28,12},{32,48},... | collective-permute-start | bytes 393224 | tf_op jit(solution)/shard_map/ppermute | solution.py:44
  88.4 5.9 %collective-permute-start.13 = (bf16[4,8,2048]{2,1,0:T(8,128)(2,1)S(1)}, bf16[4,8,2048]{2,1,0:T(8,128)(2,1)S(1)}, u32[]{:S(2)}, u32[]{:S(2)}) collective-permute-start(bf16[4,8,2048]{2,1,0:T(8,128)(2,1)S(1)} %get-tuple-element.65), channel_id=1, source_target_pairs={{0,8},{4,12},{8,16},{12,20},{16,24},{20,28},{24,0},{28,4},{32,40},... | collective-permute-start | bytes 393224 | tf_op jit(solution)/shard_map/ppermute | solution.py:44
  88.4 5.9 %collective-permute-start.15 = (bf16[4,8,2048]{2,1,0:T(8,128)(2,1)S(1)}, bf16[4,8,2048]{2,1,0:T(8,128)(2,1)S(1)}, u32[]{:S(2)}, u32[]{:S(2)}) collective-permute-start(bf16[4,8,2048]{2,1,0:T(8,128)(2,1)S(1)} %get-tuple-element.65), channel_id=1, source_target_pairs={{0,24},{4,28},{8,0},{12,4},{16,8},{20,12},{24,16},{28,20},{32,56},... | collective-permute-start | bytes 393224 | tf_op jit(solution)/shard_map/ppermute | solution.py:44
  94.4 8.1 %collective-permute-start.16 = (bf16[4,4,8,2048]{3,2,1,0:T(8,128)(2,1)S(1)}, bf16[4,4,8,2048]{3,2,1,0:T(8,128)(2,1)S(1)}, u32[]{:S(2)}, u32[]{:S(2)}) collective-permute-start(bf16[4,4,8,2048]{3,2,1,0:T(8,128)(2,1)S(1)} %pad_maximum_fusion.1), channel_id=1, source_target_pairs={{0,4},{4,0},{8,12},{12,8},{16,20},{20,16},{24,28},{28,24},{32,36},... | collective-permute-start | bytes 1572872 | tf_op jit(solution)/shard_map/ppermute | solution.py:44
  111.5 6.2 %collective-permute-start.18 = (bf16[4,8,2048]{2,1,0:T(8,128)(2,1)S(1)}, bf16[4,8,2048]{2,1,0:T(8,128)(2,1)S(1)}, u32[]{:S(2)}, u32[]{:S(2)}) collective-permute-start(bf16[4,8,2048]{2,1,0:T(8,128)(2,1)S(1)} %get-tuple-element.48), channel_id=1, source_target_pairs={{0,8},{4,12},{8,16},{12,20},{16,24},{20,28},{24,0},{28,4},{32,40},... | collective-permute-start | bytes 393224 | tf_op jit(solution)/shard_map/ppermute | solution.py:44
  111.9 5.8 %collective-permute-start.20 = (bf16[4,8,2048]{2,1,0:T(8,128)(2,1)S(1)}, bf16[4,8,2048]{2,1,0:T(8,128)(2,1)S(1)}, u32[]{:S(2)}, u32[]{:S(2)}) collective-permute-start(bf16[4,8,2048]{2,1,0:T(8,128)(2,1)S(1)} %get-tuple-element.49), channel_id=1, source_target_pairs={{0,24},{4,28},{8,0},{12,4},{16,8},{20,12},{24,16},{28,20},{32,56},... | collective-permute-start | bytes 393224 | tf_op jit(solution)/shard_map/ppermute | solution.py:44
  114.3 6.2 %collective-permute-start.19 = (bf16[4,8,2048]{2,1,0:T(8,128)(2,1)S(1)}, bf16[4,8,2048]{2,1,0:T(8,128)(2,1)S(1)}, u32[]{:S(2)}, u32[]{:S(2)}) collective-permute-start(bf16[4,8,2048]{2,1,0:T(8,128)(2,1)S(1)} %get-tuple-element.50), channel_id=1, source_target_pairs={{0,16},{4,20},{8,24},{12,28},{16,0},{20,4},{24,8},{28,12},{32,48},... | collective-permute-start | bytes 393224 | tf_op jit(solution)/shard_map/ppermute | solution.py:44
  120.6 4.3 %collective-permute-start.21 = (bf16[8,2048]{1,0:T(8,128)(2,1)S(1)}, bf16[8,2048]{1,0:T(8,128)(2,1)S(1)}, u32[]{:S(2)}, u32[]{:S(2)}) collective-permute-start(bf16[8,2048]{1,0:T(8,128)(2,1)S(1)} %get-tuple-element.61), channel_id=1, source_target_pairs={{0,32},{4,36},{8,40},{12,44},{16,48},{20,52},{24,56},{28,60},{32,6... | collective-permute-start | bytes 98312 | tf_op jit(solution)/shard_map/ppermute | solution.py:44
  123.7 4.6 %collective-permute-start.22 = (bf16[8,2048]{1,0:T(8,128)(2,1)S(1)}, bf16[8,2048]{1,0:T(8,128)(2,1)S(1)}, u32[]{:S(2)}, u32[]{:S(2)}) collective-permute-start(bf16[8,2048]{1,0:T(8,128)(2,1)S(1)} %get-tuple-element.63), channel_id=1, source_target_pairs={{0,64},{4,68},{8,72},{12,76},{16,80},{20,84},{24,88},{28,92},{32,9... | collective-permute-start | bytes 98312 | tf_op jit(solution)/shard_map/ppermute | solution.py:44
  128.3 4.4 %collective-permute-start.26 = (f32[8,2048]{1,0:T(8,128)S(1)}, f32[8,2048]{1,0:T(8,128)S(1)}, u32[]{:S(2)}, u32[]{:S(2)}) collective-permute-start(f32[8,2048]{1,0:T(8,128)S(1)} %fusion.34), channel_id=1, source_target_pairs={{0,1},{1,2},{2,3},{3,0},{4,5},{5,6},{6,7},{7,4},{8,9},{9,10},{10,1... | collective-permute-start | bytes 196616 | tf_op jit(solution)/shard_map/ppermute | solution.py:44
  128.4 5.8 %collective-permute-start.25 = (f32[8,2048]{1,0:T(8,128)S(1)}, f32[8,2048]{1,0:T(8,128)S(1)}, u32[]{:S(2)}, u32[]{:S(2)}) collective-permute-start(f32[8,2048]{1,0:T(8,128)S(1)} %fusion.34), channel_id=1, source_target_pairs={{0,2},{1,3},{2,0},{3,1},{4,6},{5,7},{6,4},{7,5},{8,10},{9,11},{10,... | collective-permute-start | bytes 196616 | tf_op jit(solution)/shard_map/ppermute | solution.py:44
  136.1 4.3 %collective-permute-start.28 = (bf16[8,2048]{1,0:T(8,128)(2,1)S(1)}, bf16[8,2048]{1,0:T(8,128)(2,1)S(1)}, u32[]{:S(2)}, u32[]{:S(2)}) collective-permute-start(bf16[8,2048]{1,0:T(8,128)(2,1)S(1)} %fusion.31), channel_id=1, source_target_pairs={{0,64},{4,68},{8,72},{12,76},{16,80},{20,84},{24,88},{28,92},{32,9... | collective-permute-start | bytes 98312 | tf_op jit(solution)/shard_map/ppermute | solution.py:44
  136.1 4.6 %collective-permute-start.27 = (bf16[8,2048]{1,0:T(8,128)(2,1)S(1)}, bf16[8,2048]{1,0:T(8,128)(2,1)S(1)}, u32[]{:S(2)}, u32[]{:S(2)}) collective-permute-start(bf16[8,2048]{1,0:T(8,128)(2,1)S(1)} %fusion.31), channel_id=1, source_target_pairs={{0,32},{4,36},{8,40},{12,44},{16,48},{20,52},{24,56},{28,60},{32,6... | collective-permute-start | bytes 98312 | tf_op jit(solution)/shard_map/ppermute | solution.py:44
  140.8 5.5 %collective-permute-start.31 = (bf16[4,8,2048]{2,1,0:T(8,128)(2,1)S(1)}, bf16[4,8,2048]{2,1,0:T(8,128)(2,1)S(1)}, u32[]{:S(2)}, u32[]{:S(2)}) collective-permute-start(bf16[4,8,2048]{2,1,0:T(8,128)(2,1)S(1)} %get-tuple-element.60), channel_id=1, source_target_pairs={{0,16},{4,20},{8,24},{12,28},{16,0},{20,4},{24,8},{28,12},{32,48},... | collective-permute-start | bytes 393224 | tf_op jit(solution)/shard_map/ppermute | solution.py:44
  141.2 6.4 %collective-permute-start.30 = (bf16[4,8,2048]{2,1,0:T(8,128)(2,1)S(1)}, bf16[4,8,2048]{2,1,0:T(8,128)(2,1)S(1)}, u32[]{:S(2)}, u32[]{:S(2)}) collective-permute-start(bf16[4,8,2048]{2,1,0:T(8,128)(2,1)S(1)} %get-tuple-element.60), channel_id=1, source_target_pairs={{0,8},{4,12},{8,16},{12,20},{16,24},{20,28},{24,0},{28,4},{32,40},... | collective-permute-start | bytes 393224 | tf_op jit(solution)/shard_map/ppermute | solution.py:44
  147.8 9.1 %collective-permute-start.33 = (bf16[4,4,8,2048]{3,2,1,0:T(8,128)(2,1)S(1)}, bf16[4,4,8,2048]{3,2,1,0:T(8,128)(2,1)S(1)}, u32[]{:S(2)}, u32[]{:S(2)}) collective-permute-start(bf16[4,4,8,2048]{3,2,1,0:T(8,128)(2,1)S(1)} %pad_maximum_fusion.2), channel_id=1, source_target_pairs={{0,4},{4,0},{8,12},{12,8},{16,20},{20,16},{24,28},{28,24},{32,36},... | collective-permute-start | bytes 1572872 | tf_op jit(solution)/shard_map/ppermute | solution.py:44
  (25 other events, 228.3 us)

commit v4 on v2

--- a/solution.py
+++ b/solution.py
@@ -76,10 +76,13 @@
     return acc
 
 
-def sum_all_ordered(x, level):
+def sum_all_ordered(x, level, wire):
     size = level[2]
     c = coord(level)
-    parts = [x] + [shifted(x, level, d) for d in range(1, size)]
+    sent = x.astype(wire)
+    parts = [sent.astype(x.dtype)] + [
+        shifted(sent, level, d).astype(x.dtype) for d in range(1, size)
+    ]
     total = None
     for m in range(size):
         part = parts[0]
@@ -277,7 +280,7 @@
     attended_part = jnp.dot(heads, w_out, preferred_element_type=jnp.float32).reshape(
         step_count, own_count, model_width
     )
-    attended = sum_all_ordered(attended_part.reshape(-1, model_width), YAX)
+    attended = sum_all_ordered(attended_part.reshape(-1, model_width), YAX, jnp.float32)
     hidden_own = lax.dynamic_slice_in_dim(hidden_in, first_req, own_count, axis=1).reshape(
         -1, model_width
     )
@@ -301,10 +304,12 @@
             block_shape + (model_width,)
         )
 
-    feed_forward = feed(halves[0]) + shifted(feed(halves[1]), CORE, 1)
+    feed_forward = feed(halves[0]) + shifted(
+        feed(halves[1]).astype(jnp.bfloat16), CORE, 1
+    ).astype(jnp.float32)
     for level in reversed(gather_levels):
         feed_forward = sum_scatter_rel(feed_forward, level, jnp.bfloat16)
-    feed_forward = sum_all_ordered(feed_forward, YAX)
+    feed_forward = sum_all_ordered(feed_forward, YAX, jnp.bfloat16)
     output = (residual.astype(jnp.float32) + branch_scale * feed_forward).astype(jnp.bfloat16)
 
     out_rows = output

time: 159 us -> 159 us (level)
  no operation moved by 1% of the time
where the time goes in v4:
time: 159 us
  starting transfers between devices  52.9 us (33%)
  waiting for transfers between devices  38.7 us (24%)
  Pallas kernels  20.3 us (13%)
  matrix products  17.2 us (11%)
  other arithmetic  15.3 us (10%)
  local copies, waits for them, and re-layouts  12.8 us (8%)
    ppermute x34, starting transfers between devices, shifted(): return lax.ppermute(x, level[0], shift_perm(level, d))  52.9 us
    ppermute x34, waiting for transfers between devices, shifted(): return lax.ppermute(x, level[0], shift_perm(level, d))  38.7 us
    pallas_call x1, Pallas kernels, cache_attention(): pl.pallas_call(cache_kernel, out_shape=jax.ShapeDtypeStruct((req, rows, h...  20.3 us
    unnamed x33, local copies, waits for them, and re-layouts  6.88 us
    dot_general x2, matrix products, feed(): jnp.dot(hidden, w_down, preferred_element_type=jnp.float32)  5.54 us
  transfers between devices with their start and end apart: 34, of which 26 were waited for; matrix products, arithmetic and copies ran while one was open for 9% of the time, Pallas kernels for 0%

profile of v4, /device:TPU:1, one launch (start us, length us, event | category | flops | bytes accessed | tf_op | source)
XLA Modules:
  0.0 158.7 jit_solution(2185591690469425045)
XLA Ops:
  3.7 4.0 %copy.65 = bf16[2048,512]{0,1:T(8,128)(2,1)} copy(bf16[2048,512]{1,0:T(8,128)(2,1)} %param.20) | data formatting | bytes 4194304 | tf_op args[6]
  8.1 2.9 %fusion.10 = f32[4,64,8,64]{1,3,2,0:T(8,128)S(1)} fusion(bf16[8,64,2048,1]{2,1,0,3:T(8,128)(2,1)} %bitcast.164, f32[2048]{0:T(1024)S(1)} %convert_element_type.155, f32[4,64]{1,0:T(4,128)S(1)} %add_rsqrt_fusion, bf16[4,64,2048]{2,1,0:T(8,128)(2,1)S(1)} %copy-done.5), kind=kOutput, calls=%fused_computation.20 | convolution fusion | flops 538968064 | bytes 3679232 | tf_op jit(solution)/shard_map/dot_general | solution.py:219
  16.8 20.3 %shard_map.157 = f32[64,32,66]{2,1,0:T(8,128)} custom-call(s32[64]{0:T(128)} %and_select_fusion.start_ref, s32[64]{0:T(128)} %len_ref.1, bf16[64,32,128]{2,1,0:T(8,128)(2,1)} %fusion.12.q_ref, bf16[64,512,128]{2,1,0:T(8,128)(2,1)} %k_ref.1, bf16[64,512,128]{2,1,0:T(8,128)(2,1)} %v_ref.1), custom_call_target="tpu_custom_call" | custom-call | tf_op jit(solution)/shard_map/pallas_call | solution.py:165
  51.2 3.9 %collective-permute-start.3 = (f32[4,2,32,66]{3,2,1,0:T(8,128)S(1)}, f32[4,2,32,66]{3,2,1,0:T(8,128)S(1)}, u32[]{:S(2)}, u32[]{:S(2)}) collective-permute-start(f32[4,2,32,66]{3,2,1,0:T(8,128)S(1)} %get-tuple-element.52), channel_id=1, source_target_pairs={{0,24},{4,28},{8,0},{12,4},{16,8},{20,12},{24,16},{28,20},{32,56},... | collective-permute-start | bytes 202760 | tf_op jit(solution)/shard_map/ppermute | solution.py:44
  56.4 4.4 %collective-permute-done.3 = f32[4,2,32,66]{3,2,1,0:T(8,128)S(1)} collective-permute-done((f32[4,2,32,66]{3,2,1,0:T(8,128)S(1)}, f32[4,2,32,66]{3,2,1,0:T(8,128)S(1)}, u32[]{:S(2)}, u32[]{:S(2)}) %collective-permute-start.3) | collective-permute-done | bytes 67616 | tf_op jit(solution)/shard_map/ppermute | solution.py:44
  61.5 2.8 %collective-permute-done.1 = f32[4,2,32,66]{3,2,1,0:T(8,128)S(1)} collective-permute-done((f32[4,2,32,66]{3,2,1,0:T(8,128)S(1)}, f32[4,2,32,66]{3,2,1,0:T(8,128)S(1)}, u32[]{:S(2)}, u32[]{:S(2)}) %collective-permute-start.1) | collective-permute-done | bytes 67616 | tf_op jit(solution)/shard_map/ppermute | solution.py:44
  65.5 2.5 %collective-permute-start.6 = (f32[2,32,66]{2,1,0:T(8,128)S(1)}, f32[2,32,66]{2,1,0:T(8,128)S(1)}, u32[]{:S(2)}, u32[]{:S(2)}) collective-permute-start(f32[2,32,66]{2,1,0:T(8,128)S(1)} %get-tuple-element.67), channel_id=1, source_target_pairs={{0,96},{4,100},{8,104},{12,108},{16,112},{20,116},{24,120},{28,124... | collective-permute-start | bytes 50696 | tf_op jit(solution)/shard_map/ppermute | solution.py:44
  69.2 3.1 %collective-permute-done.5 = f32[2,32,66]{2,1,0:T(8,128)S(1)} collective-permute-done((f32[2,32,66]{2,1,0:T(8,128)S(1)}, f32[2,32,66]{2,1,0:T(8,128)S(1)}, u32[]{:S(2)}, u32[]{:S(2)}) %collective-permute-start.5) | collective-permute-done | bytes 16928 | tf_op jit(solution)/shard_map/ppermute | solution.py:44
  76.0 2.6 %collective-permute-start.8 = (f32[8,2048]{1,0:T(8,128)S(1)}, f32[8,2048]{1,0:T(8,128)S(1)}, u32[]{:S(2)}, u32[]{:S(2)}) collective-permute-start(f32[8,2048]{1,0:T(8,128)S(1)} %fusion.99), channel_id=1, source_target_pairs={{0,2},{1,3},{2,0},{3,1},{4,6},{5,7},{6,4},{7,5},{8,10},{9,11},{10,... | collective-permute-start | bytes 196616 | tf_op jit(solution)/shard_map/ppermute | solution.py:44
  83.5 2.7 %collective-permute-start.12 = (bf16[8,2048]{1,0:T(8,128)(2,1)S(1)}, bf16[8,2048]{1,0:T(8,128)(2,1)S(1)}, u32[]{:S(2)}, u32[]{:S(2)}) collective-permute-start(bf16[8,2048]{1,0:T(8,128)(2,1)S(1)} %fusion.30), channel_id=1, source_target_pairs={{0,96},{4,100},{8,104},{12,108},{16,112},{20,116},{24,120},{28,124... | collective-permute-start | bytes 98312 | tf_op jit(solution)/shard_map/ppermute | solution.py:44
  88.4 2.7 %collective-permute-start.15 = (bf16[4,8,2048]{2,1,0:T(8,128)(2,1)S(1)}, bf16[4,8,2048]{2,1,0:T(8,128)(2,1)S(1)}, u32[]{:S(2)}, u32[]{:S(2)}) collective-permute-start(bf16[4,8,2048]{2,1,0:T(8,128)(2,1)S(1)} %get-tuple-element.65), channel_id=1, source_target_pairs={{0,24},{4,28},{8,0},{12,4},{16,8},{20,12},{24,16},{28,20},{32,56},... | collective-permute-start | bytes 393224 | tf_op jit(solution)/shard_map/ppermute | solution.py:44
  94.4 6.6 %collective-permute-start.16 = (bf16[4,4,8,2048]{3,2,1,0:T(8,128)(2,1)S(1)}, bf16[4,4,8,2048]{3,2,1,0:T(8,128)(2,1)S(1)}, u32[]{:S(2)}, u32[]{:S(2)}) collective-permute-start(bf16[4,4,8,2048]{3,2,1,0:T(8,128)(2,1)S(1)} %pad_maximum_fusion.1), channel_id=1, source_target_pairs={{0,4},{4,0},{8,12},{12,8},{16,20},{20,16},{24,28},{28,24},{32,36},... | collective-permute-start | bytes 1572872 | tf_op jit(solution)/shard_map/ppermute | solution.py:44
  103.4 2.7 %convolution_convert_fusion = bf16[128,2048]{1,0:T(8,128)(2,1)} fusion(bf16[64,2048]{1,0:T(8,128)(2,1)} %param.27, f32[128,64]{0,1:T(8,128)} %fusion.101, bf16[128,2048]{1,0:T(8,128)(2,1)S(1)} %bitcast.163, bf16[64,2048]{1,0:T(8,128)(2,1)} %param.26), kind=kOutput, calls=%fused_computation.2 | convolution fusion | flops 67420160 | bytes 1605632 | tf_op jit(solution)/shard_map/dot_general | solution.py:303
  107.4 2.9 %fusion.4 = f32[128,2048]{1,0:T(8,128)} fusion(bf16[64,2048]{1,0:T(8,128)(2,1)} %param.27, bf16[128,2048]{1,0:T(8,128)(2,1)S(1)} %bitcast.159, bf16[64,2048]{1,0:T(8,128)(2,1)} %param.26, f32[128,64]{0,1:T(8,128)} %fusion.100), kind=kOutput, calls=%fused_computation.12 | convolution fusion | flops 67158016 | bytes 2129920 | tf_op jit(solution)/shard_map/dot_general | solution.py:303
  112.0 2.4 %collective-permute-start.20 = (bf16[4,8,2048]{2,1,0:T(8,128)(2,1)S(1)}, bf16[4,8,2048]{2,1,0:T(8,128)(2,1)S(1)}, u32[]{:S(2)}, u32[]{:S(2)}) collective-permute-start(bf16[4,8,2048]{2,1,0:T(8,128)(2,1)S(1)} %get-tuple-element.49), channel_id=1, source_target_pairs={{0,24},{4,28},{8,0},{12,4},{16,8},{20,12},{24,16},{28,20},{32,56},... | collective-permute-start | bytes 393224 | tf_op jit(solution)/shard_map/ppermute | solution.py:44
  114.7 3.1 %collective-permute-done.18 = bf16[4,8,2048]{2,1,0:T(8,128)(2,1)S(1)} collective-permute-done((bf16[4,8,2048]{2,1,0:T(8,128)(2,1)S(1)}, bf16[4,8,2048]{2,1,0:T(8,128)(2,1)S(1)}, u32[]{:S(2)}, u32[]{:S(2)}) %collective-permute-start.18) | collective-permute-done | bytes 131104 | tf_op jit(solution)/shard_map/ppermute | solution.py:44
  117.9 2.7 %collective-permute-done.19 = bf16[4,8,2048]{2,1,0:T(8,128)(2,1)S(1)} collective-permute-done((bf16[4,8,2048]{2,1,0:T(8,128)(2,1)S(1)}, bf16[4,8,2048]{2,1,0:T(8,128)(2,1)S(1)}, u32[]{:S(2)}, u32[]{:S(2)}) %collective-permute-start.19) | collective-permute-done | bytes 131104 | tf_op jit(solution)/shard_map/ppermute | solution.py:44
  121.2 2.6 %collective-permute-start.23 = (bf16[8,2048]{1,0:T(8,128)(2,1)S(1)}, bf16[8,2048]{1,0:T(8,128)(2,1)S(1)}, u32[]{:S(2)}, u32[]{:S(2)}) collective-permute-start(bf16[8,2048]{1,0:T(8,128)(2,1)S(1)} %get-tuple-element.62), channel_id=1, source_target_pairs={{0,96},{4,100},{8,104},{12,108},{16,112},{20,116},{24,120},{28,124... | collective-permute-start | bytes 98312 | tf_op jit(solution)/shard_map/ppermute | solution.py:44
  125.0 3.4 %collective-permute-done.22 = bf16[8,2048]{1,0:T(8,128)(2,1)S(1)} collective-permute-done((bf16[8,2048]{1,0:T(8,128)(2,1)S(1)}, bf16[8,2048]{1,0:T(8,128)(2,1)S(1)}, u32[]{:S(2)}, u32[]{:S(2)}) %collective-permute-start.22) | collective-permute-done | bytes 32800 | tf_op jit(solution)/shard_map/ppermute | solution.py:44
  128.5 3.4 %collective-permute-start.25 = (bf16[8,2048]{1,0:T(8,128)(2,1)S(1)}, bf16[8,2048]{1,0:T(8,128)(2,1)S(1)}, u32[]{:S(2)}, u32[]{:S(2)}) collective-permute-start(bf16[8,2048]{1,0:T(8,128)(2,1)S(1)} %fusion.39), channel_id=1, source_target_pairs={{0,2},{1,3},{2,0},{3,1},{4,6},{5,7},{6,4},{7,5},{8,10},{9,11},{10,... | collective-permute-start | bytes 98312 | tf_op jit(solution)/shard_map/ppermute | solution.py:44
  137.6 2.7 %collective-permute-done.28 = bf16[8,2048]{1,0:T(8,128)(2,1)S(1)} collective-permute-done((bf16[8,2048]{1,0:T(8,128)(2,1)S(1)}, bf16[8,2048]{1,0:T(8,128)(2,1)S(1)}, u32[]{:S(2)}, u32[]{:S(2)}) %collective-permute-start.28) | collective-permute-done | bytes 32800 | tf_op jit(solution)/shard_map/ppermute | solution.py:44
  140.9 2.5 %collective-permute-start.30 = (bf16[4,8,2048]{2,1,0:T(8,128)(2,1)S(1)}, bf16[4,8,2048]{2,1,0:T(8,128)(2,1)S(1)}, u32[]{:S(2)}, u32[]{:S(2)}) collective-permute-start(bf16[4,8,2048]{2,1,0:T(8,128)(2,1)S(1)} %get-tuple-element.60), channel_id=1, source_target_pairs={{0,8},{4,12},{8,16},{12,20},{16,24},{20,28},{24,0},{28,4},{32,40},... | collective-permute-start | bytes 393224 | tf_op jit(solution)/shard_map/ppermute | solution.py:44
  143.8 2.3 %collective-permute-done.31 = bf16[4,8,2048]{2,1,0:T(8,128)(2,1)S(1)} collective-permute-done((bf16[4,8,2048]{2,1,0:T(8,128)(2,1)S(1)}, bf16[4,8,2048]{2,1,0:T(8,128)(2,1)S(1)}, u32[]{:S(2)}, u32[]{:S(2)}) %collective-permute-start.31) | collective-permute-done | bytes 131104 | tf_op jit(solution)/shard_map/ppermute | solution.py:44
  147.3 7.9 %collective-permute-start.33 = (bf16[4,4,8,2048]{3,2,1,0:T(8,128)(2,1)S(1)}, bf16[4,4,8,2048]{3,2,1,0:T(8,128)(2,1)S(1)}, u32[]{:S(2)}, u32[]{:S(2)}) collective-permute-start(bf16[4,4,8,2048]{3,2,1,0:T(8,128)(2,1)S(1)} %pad_maximum_fusion.2), channel_id=1, source_target_pairs={{0,4},{4,0},{8,12},{12,8},{16,20},{20,16},{24,28},{28,24},{32,36},... | collective-permute-start | bytes 1572872 | tf_op jit(solution)/shard_map/ppermute | solution.py:44
  (158 shorter events, 60.2 us)
Async XLA Ops:
  39.3 9.9 %collective-permute-start = (f32[4,4,2,32,66]{4,3,2,1,0:T(8,128)}, f32[4,4,2,32,66]{4,3,2,1,0:T(8,128)S(1)}, u32[]{:S(2)}, u32[]{:S(2)}) collective-permute-start(f32[4,4,2,32,66]{4,3,2,1,0:T(8,128)} %get-tuple-element.47), channel_id=1, source_target_pairs={{0,4},{4,0},{8,12},{12,8},{16,20},{20,16},{24,28},{28,24},{32,36},... | collective-permute-start | bytes 811016 | tf_op jit(solution)/shard_map/ppermute | solution.py:44
  51.2 9.6 %collective-permute-start.3 = (f32[4,2,32,66]{3,2,1,0:T(8,128)S(1)}, f32[4,2,32,66]{3,2,1,0:T(8,128)S(1)}, u32[]{:S(2)}, u32[]{:S(2)}) collective-permute-start(f32[4,2,32,66]{3,2,1,0:T(8,128)S(1)} %get-tuple-element.52), channel_id=1, source_target_pairs={{0,24},{4,28},{8,0},{12,4},{16,8},{20,12},{24,16},{28,20},{32,56},... | collective-permute-start | bytes 202760 | tf_op jit(solution)/shard_map/ppermute | solution.py:44
  55.1 6.3 %collective-permute-start.2 = (f32[4,2,32,66]{3,2,1,0:T(8,128)S(1)}, f32[4,2,32,66]{3,2,1,0:T(8,128)S(1)}, u32[]{:S(2)}, u32[]{:S(2)}) collective-permute-start(f32[4,2,32,66]{3,2,1,0:T(8,128)S(1)} %get-tuple-element.53), channel_id=1, source_target_pairs={{0,16},{4,20},{8,24},{12,28},{16,0},{20,4},{24,8},{28,12},{32,48},... | collective-permute-start | bytes 202760 | tf_op jit(solution)/shard_map/ppermute | solution.py:44
  55.2 9.1 %collective-permute-start.1 = (f32[4,2,32,66]{3,2,1,0:T(8,128)S(1)}, f32[4,2,32,66]{3,2,1,0:T(8,128)S(1)}, u32[]{:S(2)}, u32[]{:S(2)}) collective-permute-start(f32[4,2,32,66]{3,2,1,0:T(8,128)S(1)} %get-tuple-element.54), channel_id=1, source_target_pairs={{0,8},{4,12},{8,16},{12,20},{16,24},{20,28},{24,0},{28,4},{32,40},... | collective-permute-start | bytes 202760 | tf_op jit(solution)/shard_map/ppermute | solution.py:44
  68.0 4.3 %collective-permute-start.5 = (f32[2,32,66]{2,1,0:T(8,128)S(1)}, f32[2,32,66]{2,1,0:T(8,128)S(1)}, u32[]{:S(2)}, u32[]{:S(2)}) collective-permute-start(f32[2,32,66]{2,1,0:T(8,128)S(1)} %get-tuple-element.68), channel_id=1, source_target_pairs={{0,64},{4,68},{8,72},{12,76},{16,80},{20,84},{24,88},{28,92},{32,9... | collective-permute-start | bytes 50696 | tf_op jit(solution)/shard_map/ppermute | solution.py:44
  74.7 6.1 %collective-permute-start.9 = (f32[8,2048]{1,0:T(8,128)S(1)}, f32[8,2048]{1,0:T(8,128)S(1)}, u32[]{:S(2)}, u32[]{:S(2)}) collective-permute-start(f32[8,2048]{1,0:T(8,128)S(1)} %fusion.99), channel_id=1, source_target_pairs={{0,1},{1,2},{2,3},{3,0},{4,5},{5,6},{6,7},{7,4},{8,9},{9,10},{10,1... | collective-permute-start | bytes 196616 | tf_op jit(solution)/shard_map/ppermute | solution.py:44
  76.0 5.0 %collective-permute-start.8 = (f32[8,2048]{1,0:T(8,128)S(1)}, f32[8,2048]{1,0:T(8,128)S(1)}, u32[]{:S(2)}, u32[]{:S(2)}) collective-permute-start(f32[8,2048]{1,0:T(8,128)S(1)} %fusion.99), channel_id=1, source_target_pairs={{0,2},{1,3},{2,0},{3,1},{4,6},{5,7},{6,4},{7,5},{8,10},{9,11},{10,... | collective-permute-start | bytes 196616 | tf_op jit(solution)/shard_map/ppermute | solution.py:44
  82.3 4.3 %collective-permute-start.11 = (bf16[8,2048]{1,0:T(8,128)(2,1)S(1)}, bf16[8,2048]{1,0:T(8,128)(2,1)S(1)}, u32[]{:S(2)}, u32[]{:S(2)}) collective-permute-start(bf16[8,2048]{1,0:T(8,128)(2,1)S(1)} %fusion.30), channel_id=1, source_target_pairs={{0,64},{4,68},{8,72},{12,76},{16,80},{20,84},{24,88},{28,92},{32,9... | collective-permute-start | bytes 98312 | tf_op jit(solution)/shard_map/ppermute | solution.py:44
  87.5 5.5 %collective-permute-start.14 = (bf16[4,8,2048]{2,1,0:T(8,128)(2,1)S(1)}, bf16[4,8,2048]{2,1,0:T(8,128)(2,1)S(1)}, u32[]{:S(2)}, u32[]{:S(2)}) collective-permute-start(bf16[4,8,2048]{2,1,0:T(8,128)(2,1)S(1)} %get-tuple-element.65), channel_id=1, source_target_pairs={{0,16},{4,20},{8,24},{12,28},{16,0},{20,4},{24,8},{28,12},{32,48},... | collective-permute-start | bytes 393224 | tf_op jit(solution)/shard_map/ppermute | solution.py:44
  88.4 5.9 %collective-permute-start.13 = (bf16[4,8,2048]{2,1,0:T(8,128)(2,1)S(1)}, bf16[4,8,2048]{2,1,0:T(8,128)(2,1)S(1)}, u32[]{:S(2)}, u32[]{:S(2)}) collective-permute-start(bf16[4,8,2048]{2,1,0:T(8,128)(2,1)S(1)} %get-tuple-element.65), channel_id=1, source_target_pairs={{0,8},{4,12},{8,16},{12,20},{16,24},{20,28},{24,0},{28,4},{32,40},... | collective-permute-start | bytes 393224 | tf_op jit(solution)/shard_map/ppermute | solution.py:44
  88.4 5.9 %collective-permute-start.15 = (bf16[4,8,2048]{2,1,0:T(8,128)(2,1)S(1)}, bf16[4,8,2048]{2,1,0:T(8,128)(2,1)S(1)}, u32[]{:S(2)}, u32[]{:S(2)}) collective-permute-start(bf16[4,8,2048]{2,1,0:T(8,128)(2,1)S(1)} %get-tuple-element.65), channel_id=1, source_target_pairs={{0,24},{4,28},{8,0},{12,4},{16,8},{20,12},{24,16},{28,20},{32,56},... | collective-permute-start | bytes 393224 | tf_op jit(solution)/shard_map/ppermute | solution.py:44
  94.4 8.1 %collective-permute-start.16 = (bf16[4,4,8,2048]{3,2,1,0:T(8,128)(2,1)S(1)}, bf16[4,4,8,2048]{3,2,1,0:T(8,128)(2,1)S(1)}, u32[]{:S(2)}, u32[]{:S(2)}) collective-permute-start(bf16[4,4,8,2048]{3,2,1,0:T(8,128)(2,1)S(1)} %pad_maximum_fusion.1), channel_id=1, source_target_pairs={{0,4},{4,0},{8,12},{12,8},{16,20},{20,16},{24,28},{28,24},{32,36},... | collective-permute-start | bytes 1572872 | tf_op jit(solution)/shard_map/ppermute | solution.py:44
  106.1 4.2 %collective-permute-start.17 = (bf16[4,4,8,2048]{3,2,1,0:T(8,128)(2,1)}, bf16[4,4,8,2048]{3,2,1,0:T(8,128)(2,1)S(1)}, u32[]{:S(2)}, u32[]{:S(2)}) collective-permute-start(bf16[4,4,8,2048]{3,2,1,0:T(8,128)(2,1)} %bitcast.171), channel_id=1, source_target_pairs={{0,4},{4,0},{8,12},{12,8},{16,20},{20,16},{24,28},{28,24},{32,36},... | collective-permute-start | bytes 1572872 | tf_op jit(solution)/shard_map/ppermute | solution.py:44
  111.7 6.2 %collective-permute-start.18 = (bf16[4,8,2048]{2,1,0:T(8,128)(2,1)S(1)}, bf16[4,8,2048]{2,1,0:T(8,128)(2,1)S(1)}, u32[]{:S(2)}, u32[]{:S(2)}) collective-permute-start(bf16[4,8,2048]{2,1,0:T(8,128)(2,1)S(1)} %get-tuple-element.48), channel_id=1, source_target_pairs={{0,8},{4,12},{8,16},{12,20},{16,24},{20,28},{24,0},{28,4},{32,40},... | collective-permute-start | bytes 393224 | tf_op jit(solution)/shard_map/ppermute | solution.py:44
  112.0 5.8 %collective-permute-start.20 = (bf16[4,8,2048]{2,1,0:T(8,128)(2,1)S(1)}, bf16[4,8,2048]{2,1,0:T(8,128)(2,1)S(1)}, u32[]{:S(2)}, u32[]{:S(2)}) collective-permute-start(bf16[4,8,2048]{2,1,0:T(8,128)(2,1)S(1)} %get-tuple-element.49), channel_id=1, source_target_pairs={{0,24},{4,28},{8,0},{12,4},{16,8},{20,12},{24,16},{28,20},{32,56},... | collective-permute-start | bytes 393224 | tf_op jit(solution)/shard_map/ppermute | solution.py:44
  114.4 6.2 %collective-permute-start.19 = (bf16[4,8,2048]{2,1,0:T(8,128)(2,1)S(1)}, bf16[4,8,2048]{2,1,0:T(8,128)(2,1)S(1)}, u32[]{:S(2)}, u32[]{:S(2)}) collective-permute-start(bf16[4,8,2048]{2,1,0:T(8,128)(2,1)S(1)} %get-tuple-element.50), channel_id=1, source_target_pairs={{0,16},{4,20},{8,24},{12,28},{16,0},{20,4},{24,8},{28,12},{32,48},... | collective-permute-start | bytes 393224 | tf_op jit(solution)/shard_map/ppermute | solution.py:44
  120.7 4.3 %collective-permute-start.21 = (bf16[8,2048]{1,0:T(8,128)(2,1)S(1)}, bf16[8,2048]{1,0:T(8,128)(2,1)S(1)}, u32[]{:S(2)}, u32[]{:S(2)}) collective-permute-start(bf16[8,2048]{1,0:T(8,128)(2,1)S(1)} %get-tuple-element.61), channel_id=1, source_target_pairs={{0,32},{4,36},{8,40},{12,44},{16,48},{20,52},{24,56},{28,60},{32,6... | collective-permute-start | bytes 98312 | tf_op jit(solution)/shard_map/ppermute | solution.py:44
  123.8 4.6 %collective-permute-start.22 = (bf16[8,2048]{1,0:T(8,128)(2,1)S(1)}, bf16[8,2048]{1,0:T(8,128)(2,1)S(1)}, u32[]{:S(2)}, u32[]{:S(2)}) collective-permute-start(bf16[8,2048]{1,0:T(8,128)(2,1)S(1)} %get-tuple-element.63), channel_id=1, source_target_pairs={{0,64},{4,68},{8,72},{12,76},{16,80},{20,84},{24,88},{28,92},{32,9... | collective-permute-start | bytes 98312 | tf_op jit(solution)/shard_map/ppermute | solution.py:44
  128.5 5.1 %collective-permute-start.25 = (bf16[8,2048]{1,0:T(8,128)(2,1)S(1)}, bf16[8,2048]{1,0:T(8,128)(2,1)S(1)}, u32[]{:S(2)}, u32[]{:S(2)}) collective-permute-start(bf16[8,2048]{1,0:T(8,128)(2,1)S(1)} %fusion.39), channel_id=1, source_target_pairs={{0,2},{1,3},{2,0},{3,1},{4,6},{5,7},{6,4},{7,5},{8,10},{9,11},{10,... | collective-permute-start | bytes 98312 | tf_op jit(solution)/shard_map/ppermute | solution.py:44
  135.9 4.4 %collective-permute-start.28 = (bf16[8,2048]{1,0:T(8,128)(2,1)S(1)}, bf16[8,2048]{1,0:T(8,128)(2,1)S(1)}, u32[]{:S(2)}, u32[]{:S(2)}) collective-permute-start(bf16[8,2048]{1,0:T(8,128)(2,1)S(1)} %fusion.31), channel_id=1, source_target_pairs={{0,64},{4,68},{8,72},{12,76},{16,80},{20,84},{24,88},{28,92},{32,9... | collective-permute-start | bytes 98312 | tf_op jit(solution)/shard_map/ppermute | solution.py:44
  135.9 4.4 %collective-permute-start.27 = (bf16[8,2048]{1,0:T(8,128)(2,1)S(1)}, bf16[8,2048]{1,0:T(8,128)(2,1)S(1)}, u32[]{:S(2)}, u32[]{:S(2)}) collective-permute-start(bf16[8,2048]{1,0:T(8,128)(2,1)S(1)} %fusion.31), channel_id=1, source_target_pairs={{0,32},{4,36},{8,40},{12,44},{16,48},{20,52},{24,56},{28,60},{32,6... | collective-permute-start | bytes 98312 | tf_op jit(solution)/shard_map/ppermute | solution.py:44
  140.4 5.6 %collective-permute-start.31 = (bf16[4,8,2048]{2,1,0:T(8,128)(2,1)S(1)}, bf16[4,8,2048]{2,1,0:T(8,128)(2,1)S(1)}, u32[]{:S(2)}, u32[]{:S(2)}) collective-permute-start(bf16[4,8,2048]{2,1,0:T(8,128)(2,1)S(1)} %get-tuple-element.60), channel_id=1, source_target_pairs={{0,16},{4,20},{8,24},{12,28},{16,0},{20,4},{24,8},{28,12},{32,48},... | collective-permute-start | bytes 393224 | tf_op jit(solution)/shard_map/ppermute | solution.py:44
  140.9 6.3 %collective-permute-start.30 = (bf16[4,8,2048]{2,1,0:T(8,128)(2,1)S(1)}, bf16[4,8,2048]{2,1,0:T(8,128)(2,1)S(1)}, u32[]{:S(2)}, u32[]{:S(2)}) collective-permute-start(bf16[4,8,2048]{2,1,0:T(8,128)(2,1)S(1)} %get-tuple-element.60), channel_id=1, source_target_pairs={{0,8},{4,12},{8,16},{12,20},{16,24},{20,28},{24,0},{28,4},{32,40},... | collective-permute-start | bytes 393224 | tf_op jit(solution)/shard_map/ppermute | solution.py:44
  147.3 9.4 %collective-permute-start.33 = (bf16[4,4,8,2048]{3,2,1,0:T(8,128)(2,1)S(1)}, bf16[4,4,8,2048]{3,2,1,0:T(8,128)(2,1)S(1)}, u32[]{:S(2)}, u32[]{:S(2)}) collective-permute-start(bf16[4,4,8,2048]{3,2,1,0:T(8,128)(2,1)S(1)} %pad_maximum_fusion.2), channel_id=1, source_target_pairs={{0,4},{4,0},{8,12},{12,8},{16,20},{20,16},{24,28},{28,24},{32,36},... | collective-permute-start | bytes 1572872 | tf_op jit(solution)/shard_map/ppermute | solution.py:44
  (25 other events, 227.0 us)

commit v5 on v2

--- a/solution.py
+++ b/solution.py
@@ -146,8 +146,9 @@
                                  preferred_element_type=jnp.float32) * attn_scale
         top = jnp.max(jnp.where(live, scores, neg_large), axis=-1, keepdims=True)
         weights = jnp.where(live, jnp.exp(scores - top), 0.0)
-        packed_ref[i, :, head_dim:head_dim + 1] = top
-        packed_ref[i, :, head_dim + 1:head_dim + 2] = jnp.sum(weights, axis=-1, keepdims=True)
+        packed_ref[i, :, head_dim:head_dim + 2] = jnp.concatenate(
+            [top, jnp.sum(weights, axis=-1, keepdims=True)], axis=-1
+        )
         mixed = jnp.dot(weights.astype(jnp.bfloat16), v_ref[i], preferred_element_type=jnp.float32)
         packed_ref[i, 0:half, 0:head_dim] = mixed[0:half, 0:head_dim]
         packed_ref[i, half:rows, 0:head_dim] = mixed[half:rows, head_dim:2 * head_dim]

time: 159 us -> 162 us (1.019)
  Pallas kernels: 20.3 us -> 23.4 us
    pallas_call x1, Pallas kernels: 20.3 us -> 23.4 us  [cache_attention(): pl.pallas_call(cache_kernel, out_shape=jax.ShapeDtypeStruct((req, rows, h...]
where the time goes in v5:
time: 162 us
  starting transfers between devices  52.4 us (32%)
  waiting for transfers between devices  39.6 us (24%)
  Pallas kernels  23.4 us (14%)
  matrix products  16.7 us (10%)
  other arithmetic  15.6 us (10%)
  local copies, waits for them, and re-layouts  12.8 us (8%)
    ppermute x34, starting transfers between devices, shifted(): return lax.ppermute(x, level[0], shift_perm(level, d))  52.4 us
    ppermute x34, waiting for transfers between devices, shifted(): return lax.ppermute(x, level[0], shift_perm(level, d))  39.6 us
    pallas_call x1, Pallas kernels, cache_attention(): pl.pallas_call(cache_kernel, out_shape=jax.ShapeDtypeStruct((req, rows, h...  23.4 us
    unnamed x33, local copies, waits for them, and re-layouts  6.88 us
    dot_general x2, matrix products, feed(): jnp.dot(hidden, w_down, preferred_element_type=jnp.float32)  5.7 us
  transfers between devices with their start and end apart: 34, of which 26 were waited for; matrix products, arithmetic and copies ran while one was open for 9% of the time, Pallas kernels for 0%

profile of v5, /device:TPU:1, one launch (start us, length us, event | category | flops | bytes accessed | tf_op | source)
XLA Modules:
  0.0 161.9 jit_solution(14216313871852766066)
XLA Ops:
  3.7 4.0 %copy.65 = bf16[2048,512]{0,1:T(8,128)(2,1)} copy(bf16[2048,512]{1,0:T(8,128)(2,1)} %param.20) | data formatting | bytes 4194304 | tf_op args[6]
  8.1 2.9 %fusion.10 = f32[4,64,8,64]{1,3,2,0:T(8,128)S(1)} fusion(bf16[8,64,2048,1]{2,1,0,3:T(8,128)(2,1)} %bitcast.160, f32[2048]{0:T(1024)S(1)} %convert_element_type.131, f32[4,64]{1,0:T(4,128)S(1)} %add_rsqrt_fusion, bf16[4,64,2048]{2,1,0:T(8,128)(2,1)S(1)} %copy-done.5), kind=kOutput, calls=%fused_computation.18 | convolution fusion | flops 538968064 | bytes 3679232 | tf_op jit(solution)/shard_map/dot_general | solution.py:217
  16.8 23.4 %shard_map.157 = f32[64,32,66]{2,1,0:T(8,128)} custom-call(s32[64]{0:T(128)} %and_select_fusion.start_ref, s32[64]{0:T(128)} %len_ref.1, bf16[64,32,128]{2,1,0:T(8,128)(2,1)} %fusion.12.q_ref, bf16[64,512,128]{2,1,0:T(8,128)(2,1)} %k_ref.1, bf16[64,512,128]{2,1,0:T(8,128)(2,1)} %v_ref.1), custom_call_target="tpu_custom_call" | custom-call | tf_op jit(solution)/shard_map/pallas_call | solution.py:163
  40.2 2.1 %dynamic-slice_bitcast_fusion.1 = (f32[4,4,2,32,66]{4,3,2,1,0:T(8,128)S(1)}, f32[4,4,2,32,66]{4,3,2,1,0:T(8,128)}) fusion(f32[2,4,4,2,32,66]{5,4,3,2,1,0:T(8,128)} %bitcast.159, s32[]{:T(128)S(6)} %select_n.441, s32[]{:T(128)S(6)} %select_n.443), kind=kLoop, calls=%fused_computation.33 | loop fusion | bytes 1081352 | tf_op jit(solution)/shard_map/jit(dynamic_index_in_dim)/squeeze | solution.py:48
  45.8 2.2 %fusion.8 = f32[4,64,2,64]{1,3,2,0:T(8,128)S(1)} fusion(bf16[2,64,2048,1]{2,1,0,3:T(8,128)(2,1)} %bitcast.170, f32[2048]{0:T(1024)S(1)} %convert_element_type.131, f32[4,64]{1,0:T(4,128)S(1)} %add_rsqrt_fusion, bf16[4,64,2048]{2,1,0:T(8,128)(2,1)} %param.14), kind=kOutput, calls=%fused_computation.17 | convolution fusion | flops 136314880 | bytes 1713152 | tf_op jit(solution)/shard_map/dot_general | solution.py:220
  54.3 3.9 %collective-permute-start.3 = (f32[4,2,32,66]{3,2,1,0:T(8,128)S(1)}, f32[4,2,32,66]{3,2,1,0:T(8,128)S(1)}, u32[]{:S(2)}, u32[]{:S(2)}) collective-permute-start(f32[4,2,32,66]{3,2,1,0:T(8,128)S(1)} %get-tuple-element.52), channel_id=1, source_target_pairs={{0,24},{4,28},{8,0},{12,4},{16,8},{20,12},{24,16},{28,20},{32,56},... | collective-permute-start | bytes 202760 | tf_op jit(solution)/shard_map/ppermute | solution.py:44
  59.5 4.4 %collective-permute-done.3 = f32[4,2,32,66]{3,2,1,0:T(8,128)S(1)} collective-permute-done((f32[4,2,32,66]{3,2,1,0:T(8,128)S(1)}, f32[4,2,32,66]{3,2,1,0:T(8,128)S(1)}, u32[]{:S(2)}, u32[]{:S(2)}) %collective-permute-start.3) | collective-permute-done | bytes 67616 | tf_op jit(solution)/shard_map/ppermute | solution.py:44
  64.5 2.8 %collective-permute-done.1 = f32[4,2,32,66]{3,2,1,0:T(8,128)S(1)} collective-permute-done((f32[4,2,32,66]{3,2,1,0:T(8,128)S(1)}, f32[4,2,32,66]{3,2,1,0:T(8,128)S(1)}, u32[]{:S(2)}, u32[]{:S(2)}) %collective-permute-start.1) | collective-permute-done | bytes 67616 | tf_op jit(solution)/shard_map/ppermute | solution.py:44
  68.5 2.5 %collective-permute-start.6 = (f32[2,32,66]{2,1,0:T(8,128)S(1)}, f32[2,32,66]{2,1,0:T(8,128)S(1)}, u32[]{:S(2)}, u32[]{:S(2)}) collective-permute-start(f32[2,32,66]{2,1,0:T(8,128)S(1)} %get-tuple-element.67), channel_id=1, source_target_pairs={{0,96},{4,100},{8,104},{12,108},{16,112},{20,116},{24,120},{28,124... | collective-permute-start | bytes 50696 | tf_op jit(solution)/shard_map/ppermute | solution.py:44
  72.2 3.1 %collective-permute-done.5 = f32[2,32,66]{2,1,0:T(8,128)S(1)} collective-permute-done((f32[2,32,66]{2,1,0:T(8,128)S(1)}, f32[2,32,66]{2,1,0:T(8,128)S(1)}, u32[]{:S(2)}, u32[]{:S(2)}) %collective-permute-start.5) | collective-permute-done | bytes 16928 | tf_op jit(solution)/shard_map/ppermute | solution.py:44
  79.1 2.6 %collective-permute-start.8 = (f32[8,2048]{1,0:T(8,128)S(1)}, f32[8,2048]{1,0:T(8,128)S(1)}, u32[]{:S(2)}, u32[]{:S(2)}) collective-permute-start(f32[8,2048]{1,0:T(8,128)S(1)} %fusion.95), channel_id=1, source_target_pairs={{0,2},{1,3},{2,0},{3,1},{4,6},{5,7},{6,4},{7,5},{8,10},{9,11},{10,... | collective-permute-start | bytes 196616 | tf_op jit(solution)/shard_map/ppermute | solution.py:44
  86.6 2.7 %collective-permute-start.12 = (bf16[8,2048]{1,0:T(8,128)(2,1)S(1)}, bf16[8,2048]{1,0:T(8,128)(2,1)S(1)}, u32[]{:S(2)}, u32[]{:S(2)}) collective-permute-start(bf16[8,2048]{1,0:T(8,128)(2,1)S(1)} %fusion.30), channel_id=1, source_target_pairs={{0,96},{4,100},{8,104},{12,108},{16,112},{20,116},{24,120},{28,124... | collective-permute-start | bytes 98312 | tf_op jit(solution)/shard_map/ppermute | solution.py:44
  91.5 2.7 %collective-permute-start.15 = (bf16[4,8,2048]{2,1,0:T(8,128)(2,1)S(1)}, bf16[4,8,2048]{2,1,0:T(8,128)(2,1)S(1)}, u32[]{:S(2)}, u32[]{:S(2)}) collective-permute-start(bf16[4,8,2048]{2,1,0:T(8,128)(2,1)S(1)} %get-tuple-element.65), channel_id=1, source_target_pairs={{0,24},{4,28},{8,0},{12,4},{16,8},{20,12},{24,16},{28,20},{32,56},... | collective-permute-start | bytes 393224 | tf_op jit(solution)/shard_map/ppermute | solution.py:44
  97.4 6.6 %collective-permute-start.16 = (bf16[4,4,8,2048]{3,2,1,0:T(8,128)(2,1)S(1)}, bf16[4,4,8,2048]{3,2,1,0:T(8,128)(2,1)S(1)}, u32[]{:S(2)}, u32[]{:S(2)}) collective-permute-start(bf16[4,4,8,2048]{3,2,1,0:T(8,128)(2,1)S(1)} %pad_maximum_fusion.1), channel_id=1, source_target_pairs={{0,4},{4,0},{8,12},{12,8},{16,20},{20,16},{24,28},{28,24},{32,36},... | collective-permute-start | bytes 1572872 | tf_op jit(solution)/shard_map/ppermute | solution.py:44
  106.5 2.9 %fusion.55 = f32[128,2048]{1,0:T(8,128)} fusion(bf16[64,2048]{1,0:T(8,128)(2,1)} %param.27, f32[128,64]{0,1:T(8,128)} %fusion.97, bf16[128,2048]{1,0:T(8,128)(2,1)S(1)} %bitcast.164, bf16[64,2048]{1,0:T(8,128)(2,1)} %param.26), kind=kOutput, calls=%fused_computation.145 | convolution fusion | flops 67158016 | bytes 2129920 | tf_op jit(solution)/shard_map/dot_general | solution.py:301
  110.0 2.8 %fusion.4 = f32[128,2048]{1,0:T(8,128)} fusion(bf16[64,2048]{1,0:T(8,128)(2,1)} %param.27, bf16[128,2048]{1,0:T(8,128)(2,1)S(1)} %bitcast.157, bf16[64,2048]{1,0:T(8,128)(2,1)} %param.26, f32[128,64]{0,1:T(8,128)S(1)} %fusion.96), kind=kOutput, calls=%fused_computation.11 | convolution fusion | flops 67158016 | bytes 2129920 | tf_op jit(solution)/shard_map/dot_general | solution.py:301
  114.9 2.4 %collective-permute-start.20 = (bf16[4,8,2048]{2,1,0:T(8,128)(2,1)S(1)}, bf16[4,8,2048]{2,1,0:T(8,128)(2,1)S(1)}, u32[]{:S(2)}, u32[]{:S(2)}) collective-permute-start(bf16[4,8,2048]{2,1,0:T(8,128)(2,1)S(1)} %get-tuple-element.49), channel_id=1, source_target_pairs={{0,24},{4,28},{8,0},{12,4},{16,8},{20,12},{24,16},{28,20},{32,56},... | collective-permute-start | bytes 393224 | tf_op jit(solution)/shard_map/ppermute | solution.py:44
  117.7 3.1 %collective-permute-done.18 = bf16[4,8,2048]{2,1,0:T(8,128)(2,1)S(1)} collective-permute-done((bf16[4,8,2048]{2,1,0:T(8,128)(2,1)S(1)}, bf16[4,8,2048]{2,1,0:T(8,128)(2,1)S(1)}, u32[]{:S(2)}, u32[]{:S(2)}) %collective-permute-start.18) | collective-permute-done | bytes 131104 | tf_op jit(solution)/shard_map/ppermute | solution.py:44
  120.8 2.7 %collective-permute-done.19 = bf16[4,8,2048]{2,1,0:T(8,128)(2,1)S(1)} collective-permute-done((bf16[4,8,2048]{2,1,0:T(8,128)(2,1)S(1)}, bf16[4,8,2048]{2,1,0:T(8,128)(2,1)S(1)}, u32[]{:S(2)}, u32[]{:S(2)}) %collective-permute-start.19) | collective-permute-done | bytes 131104 | tf_op jit(solution)/shard_map/ppermute | solution.py:44
  124.2 2.6 %collective-permute-start.23 = (bf16[8,2048]{1,0:T(8,128)(2,1)S(1)}, bf16[8,2048]{1,0:T(8,128)(2,1)S(1)}, u32[]{:S(2)}, u32[]{:S(2)}) collective-permute-start(bf16[8,2048]{1,0:T(8,128)(2,1)S(1)} %get-tuple-element.62), channel_id=1, source_target_pairs={{0,96},{4,100},{8,104},{12,108},{16,112},{20,116},{24,120},{28,124... | collective-permute-start | bytes 98312 | tf_op jit(solution)/shard_map/ppermute | solution.py:44
  127.9 3.4 %collective-permute-done.22 = bf16[8,2048]{1,0:T(8,128)(2,1)S(1)} collective-permute-done((bf16[8,2048]{1,0:T(8,128)(2,1)S(1)}, bf16[8,2048]{1,0:T(8,128)(2,1)S(1)}, u32[]{:S(2)}, u32[]{:S(2)}) %collective-permute-start.22) | collective-permute-done | bytes 32800 | tf_op jit(solution)/shard_map/ppermute | solution.py:44
  131.4 3.4 %collective-permute-start.25 = (f32[8,2048]{1,0:T(8,128)S(1)}, f32[8,2048]{1,0:T(8,128)S(1)}, u32[]{:S(2)}, u32[]{:S(2)}) collective-permute-start(f32[8,2048]{1,0:T(8,128)S(1)} %fusion.34), channel_id=1, source_target_pairs={{0,2},{1,3},{2,0},{3,1},{4,6},{5,7},{6,4},{7,5},{8,10},{9,11},{10,... | collective-permute-start | bytes 196616 | tf_op jit(solution)/shard_map/ppermute | solution.py:44
  144.3 2.7 %collective-permute-start.30 = (bf16[4,8,2048]{2,1,0:T(8,128)(2,1)S(1)}, bf16[4,8,2048]{2,1,0:T(8,128)(2,1)S(1)}, u32[]{:S(2)}, u32[]{:S(2)}) collective-permute-start(bf16[4,8,2048]{2,1,0:T(8,128)(2,1)S(1)} %get-tuple-element.60), channel_id=1, source_target_pairs={{0,8},{4,12},{8,16},{12,20},{16,24},{20,28},{24,0},{28,4},{32,40},... | collective-permute-start | bytes 393224 | tf_op jit(solution)/shard_map/ppermute | solution.py:44
  150.8 7.6 %collective-permute-start.33 = (bf16[4,4,8,2048]{3,2,1,0:T(8,128)(2,1)S(1)}, bf16[4,4,8,2048]{3,2,1,0:T(8,128)(2,1)S(1)}, u32[]{:S(2)}, u32[]{:S(2)}) collective-permute-start(bf16[4,4,8,2048]{3,2,1,0:T(8,128)(2,1)S(1)} %pad_maximum_fusion.2), channel_id=1, source_target_pairs={{0,4},{4,0},{8,12},{12,8},{16,20},{20,16},{24,28},{28,24},{32,36},... | collective-permute-start | bytes 1572872 | tf_op jit(solution)/shard_map/ppermute | solution.py:44
  (158 shorter events, 60.9 us)
Async XLA Ops:
  42.3 9.9 %collective-permute-start = (f32[4,4,2,32,66]{4,3,2,1,0:T(8,128)}, f32[4,4,2,32,66]{4,3,2,1,0:T(8,128)S(1)}, u32[]{:S(2)}, u32[]{:S(2)}) collective-permute-start(f32[4,4,2,32,66]{4,3,2,1,0:T(8,128)} %get-tuple-element.47), channel_id=1, source_target_pairs={{0,4},{4,0},{8,12},{12,8},{16,20},{20,16},{24,28},{28,24},{32,36},... | collective-permute-start | bytes 811016 | tf_op jit(solution)/shard_map/ppermute | solution.py:44
  54.3 9.6 %collective-permute-start.3 = (f32[4,2,32,66]{3,2,1,0:T(8,128)S(1)}, f32[4,2,32,66]{3,2,1,0:T(8,128)S(1)}, u32[]{:S(2)}, u32[]{:S(2)}) collective-permute-start(f32[4,2,32,66]{3,2,1,0:T(8,128)S(1)} %get-tuple-element.52), channel_id=1, source_target_pairs={{0,24},{4,28},{8,0},{12,4},{16,8},{20,12},{24,16},{28,20},{32,56},... | collective-permute-start | bytes 202760 | tf_op jit(solution)/shard_map/ppermute | solution.py:44
  58.2 6.3 %collective-permute-start.2 = (f32[4,2,32,66]{3,2,1,0:T(8,128)S(1)}, f32[4,2,32,66]{3,2,1,0:T(8,128)S(1)}, u32[]{:S(2)}, u32[]{:S(2)}) collective-permute-start(f32[4,2,32,66]{3,2,1,0:T(8,128)S(1)} %get-tuple-element.53), channel_id=1, source_target_pairs={{0,16},{4,20},{8,24},{12,28},{16,0},{20,4},{24,8},{28,12},{32,48},... | collective-permute-start | bytes 202760 | tf_op jit(solution)/shard_map/ppermute | solution.py:44
  58.2 9.1 %collective-permute-start.1 = (f32[4,2,32,66]{3,2,1,0:T(8,128)S(1)}, f32[4,2,32,66]{3,2,1,0:T(8,128)S(1)}, u32[]{:S(2)}, u32[]{:S(2)}) collective-permute-start(f32[4,2,32,66]{3,2,1,0:T(8,128)S(1)} %get-tuple-element.54), channel_id=1, source_target_pairs={{0,8},{4,12},{8,16},{12,20},{16,24},{20,28},{24,0},{28,4},{32,40},... | collective-permute-start | bytes 202760 | tf_op jit(solution)/shard_map/ppermute | solution.py:44
  71.1 4.3 %collective-permute-start.5 = (f32[2,32,66]{2,1,0:T(8,128)S(1)}, f32[2,32,66]{2,1,0:T(8,128)S(1)}, u32[]{:S(2)}, u32[]{:S(2)}) collective-permute-start(f32[2,32,66]{2,1,0:T(8,128)S(1)} %get-tuple-element.68), channel_id=1, source_target_pairs={{0,64},{4,68},{8,72},{12,76},{16,80},{20,84},{24,88},{28,92},{32,9... | collective-permute-start | bytes 50696 | tf_op jit(solution)/shard_map/ppermute | solution.py:44
  77.8 6.1 %collective-permute-start.9 = (f32[8,2048]{1,0:T(8,128)S(1)}, f32[8,2048]{1,0:T(8,128)S(1)}, u32[]{:S(2)}, u32[]{:S(2)}) collective-permute-start(f32[8,2048]{1,0:T(8,128)S(1)} %fusion.95), channel_id=1, source_target_pairs={{0,1},{1,2},{2,3},{3,0},{4,5},{5,6},{6,7},{7,4},{8,9},{9,10},{10,1... | collective-permute-start | bytes 196616 | tf_op jit(solution)/shard_map/ppermute | solution.py:44
  79.1 5.0 %collective-permute-start.8 = (f32[8,2048]{1,0:T(8,128)S(1)}, f32[8,2048]{1,0:T(8,128)S(1)}, u32[]{:S(2)}, u32[]{:S(2)}) collective-permute-start(f32[8,2048]{1,0:T(8,128)S(1)} %fusion.95), channel_id=1, source_target_pairs={{0,2},{1,3},{2,0},{3,1},{4,6},{5,7},{6,4},{7,5},{8,10},{9,11},{10,... | collective-permute-start | bytes 196616 | tf_op jit(solution)/shard_map/ppermute | solution.py:44
  85.4 4.3 %collective-permute-start.11 = (bf16[8,2048]{1,0:T(8,128)(2,1)S(1)}, bf16[8,2048]{1,0:T(8,128)(2,1)S(1)}, u32[]{:S(2)}, u32[]{:S(2)}) collective-permute-start(bf16[8,2048]{1,0:T(8,128)(2,1)S(1)} %fusion.30), channel_id=1, source_target_pairs={{0,64},{4,68},{8,72},{12,76},{16,80},{20,84},{24,88},{28,92},{32,9... | collective-permute-start | bytes 98312 | tf_op jit(solution)/shard_map/ppermute | solution.py:44
  90.6 5.5 %collective-permute-start.14 = (bf16[4,8,2048]{2,1,0:T(8,128)(2,1)S(1)}, bf16[4,8,2048]{2,1,0:T(8,128)(2,1)S(1)}, u32[]{:S(2)}, u32[]{:S(2)}) collective-permute-start(bf16[4,8,2048]{2,1,0:T(8,128)(2,1)S(1)} %get-tuple-element.65), channel_id=1, source_target_pairs={{0,16},{4,20},{8,24},{12,28},{16,0},{20,4},{24,8},{28,12},{32,48},... | collective-permute-start | bytes 393224 | tf_op jit(solution)/shard_map/ppermute | solution.py:44
  91.5 5.9 %collective-permute-start.13 = (bf16[4,8,2048]{2,1,0:T(8,128)(2,1)S(1)}, bf16[4,8,2048]{2,1,0:T(8,128)(2,1)S(1)}, u32[]{:S(2)}, u32[]{:S(2)}) collective-permute-start(bf16[4,8,2048]{2,1,0:T(8,128)(2,1)S(1)} %get-tuple-element.65), channel_id=1, source_target_pairs={{0,8},{4,12},{8,16},{12,20},{16,24},{20,28},{24,0},{28,4},{32,40},... | collective-permute-start | bytes 393224 | tf_op jit(solution)/shard_map/ppermute | solution.py:44
  91.5 5.9 %collective-permute-start.15 = (bf16[4,8,2048]{2,1,0:T(8,128)(2,1)S(1)}, bf16[4,8,2048]{2,1,0:T(8,128)(2,1)S(1)}, u32[]{:S(2)}, u32[]{:S(2)}) collective-permute-start(bf16[4,8,2048]{2,1,0:T(8,128)(2,1)S(1)} %get-tuple-element.65), channel_id=1, source_target_pairs={{0,24},{4,28},{8,0},{12,4},{16,8},{20,12},{24,16},{28,20},{32,56},... | collective-permute-start | bytes 393224 | tf_op jit(solution)/shard_map/ppermute | solution.py:44
  97.4 8.1 %collective-permute-start.16 = (bf16[4,4,8,2048]{3,2,1,0:T(8,128)(2,1)S(1)}, bf16[4,4,8,2048]{3,2,1,0:T(8,128)(2,1)S(1)}, u32[]{:S(2)}, u32[]{:S(2)}) collective-permute-start(bf16[4,4,8,2048]{3,2,1,0:T(8,128)(2,1)S(1)} %pad_maximum_fusion.1), channel_id=1, source_target_pairs={{0,4},{4,0},{8,12},{12,8},{16,20},{20,16},{24,28},{28,24},{32,36},... | collective-permute-start | bytes 1572872 | tf_op jit(solution)/shard_map/ppermute | solution.py:44
  114.6 6.2 %collective-permute-start.18 = (bf16[4,8,2048]{2,1,0:T(8,128)(2,1)S(1)}, bf16[4,8,2048]{2,1,0:T(8,128)(2,1)S(1)}, u32[]{:S(2)}, u32[]{:S(2)}) collective-permute-start(bf16[4,8,2048]{2,1,0:T(8,128)(2,1)S(1)} %get-tuple-element.48), channel_id=1, source_target_pairs={{0,8},{4,12},{8,16},{12,20},{16,24},{20,28},{24,0},{28,4},{32,40},... | collective-permute-start | bytes 393224 | tf_op jit(solution)/shard_map/ppermute | solution.py:44
  114.9 5.8 %collective-permute-start.20 = (bf16[4,8,2048]{2,1,0:T(8,128)(2,1)S(1)}, bf16[4,8,2048]{2,1,0:T(8,128)(2,1)S(1)}, u32[]{:S(2)}, u32[]{:S(2)}) collective-permute-start(bf16[4,8,2048]{2,1,0:T(8,128)(2,1)S(1)} %get-tuple-element.49), channel_id=1, source_target_pairs={{0,24},{4,28},{8,0},{12,4},{16,8},{20,12},{24,16},{28,20},{32,56},... | collective-permute-start | bytes 393224 | tf_op jit(solution)/shard_map/ppermute | solution.py:44
  117.3 6.2 %collective-permute-start.19 = (bf16[4,8,2048]{2,1,0:T(8,128)(2,1)S(1)}, bf16[4,8,2048]{2,1,0:T(8,128)(2,1)S(1)}, u32[]{:S(2)}, u32[]{:S(2)}) collective-permute-start(bf16[4,8,2048]{2,1,0:T(8,128)(2,1)S(1)} %get-tuple-element.50), channel_id=1, source_target_pairs={{0,16},{4,20},{8,24},{12,28},{16,0},{20,4},{24,8},{28,12},{32,48},... | collective-permute-start | bytes 393224 | tf_op jit(solution)/shard_map/ppermute | solution.py:44
  123.6 4.3 %collective-permute-start.21 = (bf16[8,2048]{1,0:T(8,128)(2,1)S(1)}, bf16[8,2048]{1,0:T(8,128)(2,1)S(1)}, u32[]{:S(2)}, u32[]{:S(2)}) collective-permute-start(bf16[8,2048]{1,0:T(8,128)(2,1)S(1)} %get-tuple-element.61), channel_id=1, source_target_pairs={{0,32},{4,36},{8,40},{12,44},{16,48},{20,52},{24,56},{28,60},{32,6... | collective-permute-start | bytes 98312 | tf_op jit(solution)/shard_map/ppermute | solution.py:44
  126.7 4.6 %collective-permute-start.22 = (bf16[8,2048]{1,0:T(8,128)(2,1)S(1)}, bf16[8,2048]{1,0:T(8,128)(2,1)S(1)}, u32[]{:S(2)}, u32[]{:S(2)}) collective-permute-start(bf16[8,2048]{1,0:T(8,128)(2,1)S(1)} %get-tuple-element.63), channel_id=1, source_target_pairs={{0,64},{4,68},{8,72},{12,76},{16,80},{20,84},{24,88},{28,92},{32,9... | collective-permute-start | bytes 98312 | tf_op jit(solution)/shard_map/ppermute | solution.py:44
  131.3 4.4 %collective-permute-start.26 = (f32[8,2048]{1,0:T(8,128)S(1)}, f32[8,2048]{1,0:T(8,128)S(1)}, u32[]{:S(2)}, u32[]{:S(2)}) collective-permute-start(f32[8,2048]{1,0:T(8,128)S(1)} %fusion.34), channel_id=1, source_target_pairs={{0,1},{1,2},{2,3},{3,0},{4,5},{5,6},{6,7},{7,4},{8,9},{9,10},{10,1... | collective-permute-start | bytes 196616 | tf_op jit(solution)/shard_map/ppermute | solution.py:44
  131.4 5.8 %collective-permute-start.25 = (f32[8,2048]{1,0:T(8,128)S(1)}, f32[8,2048]{1,0:T(8,128)S(1)}, u32[]{:S(2)}, u32[]{:S(2)}) collective-permute-start(f32[8,2048]{1,0:T(8,128)S(1)} %fusion.34), channel_id=1, source_target_pairs={{0,2},{1,3},{2,0},{3,1},{4,6},{5,7},{6,4},{7,5},{8,10},{9,11},{10,... | collective-permute-start | bytes 196616 | tf_op jit(solution)/shard_map/ppermute | solution.py:44
  139.2 4.3 %collective-permute-start.28 = (bf16[8,2048]{1,0:T(8,128)(2,1)S(1)}, bf16[8,2048]{1,0:T(8,128)(2,1)S(1)}, u32[]{:S(2)}, u32[]{:S(2)}) collective-permute-start(bf16[8,2048]{1,0:T(8,128)(2,1)S(1)} %fusion.31), channel_id=1, source_target_pairs={{0,64},{4,68},{8,72},{12,76},{16,80},{20,84},{24,88},{28,92},{32,9... | collective-permute-start | bytes 98312 | tf_op jit(solution)/shard_map/ppermute | solution.py:44
  139.2 4.6 %collective-permute-start.27 = (bf16[8,2048]{1,0:T(8,128)(2,1)S(1)}, bf16[8,2048]{1,0:T(8,128)(2,1)S(1)}, u32[]{:S(2)}, u32[]{:S(2)}) collective-permute-start(bf16[8,2048]{1,0:T(8,128)(2,1)S(1)} %fusion.31), channel_id=1, source_target_pairs={{0,32},{4,36},{8,40},{12,44},{16,48},{20,52},{24,56},{28,60},{32,6... | collective-permute-start | bytes 98312 | tf_op jit(solution)/shard_map/ppermute | solution.py:44
  143.8 5.5 %collective-permute-start.31 = (bf16[4,8,2048]{2,1,0:T(8,128)(2,1)S(1)}, bf16[4,8,2048]{2,1,0:T(8,128)(2,1)S(1)}, u32[]{:S(2)}, u32[]{:S(2)}) collective-permute-start(bf16[4,8,2048]{2,1,0:T(8,128)(2,1)S(1)} %get-tuple-element.60), channel_id=1, source_target_pairs={{0,16},{4,20},{8,24},{12,28},{16,0},{20,4},{24,8},{28,12},{32,48},... | collective-permute-start | bytes 393224 | tf_op jit(solution)/shard_map/ppermute | solution.py:44
  144.3 6.4 %collective-permute-start.30 = (bf16[4,8,2048]{2,1,0:T(8,128)(2,1)S(1)}, bf16[4,8,2048]{2,1,0:T(8,128)(2,1)S(1)}, u32[]{:S(2)}, u32[]{:S(2)}) collective-permute-start(bf16[4,8,2048]{2,1,0:T(8,128)(2,1)S(1)} %get-tuple-element.60), channel_id=1, source_target_pairs={{0,8},{4,12},{8,16},{12,20},{16,24},{20,28},{24,0},{28,4},{32,40},... | collective-permute-start | bytes 393224 | tf_op jit(solution)/shard_map/ppermute | solution.py:44
  150.8 9.1 %collective-permute-start.33 = (bf16[4,4,8,2048]{3,2,1,0:T(8,128)(2,1)S(1)}, bf16[4,4,8,2048]{3,2,1,0:T(8,128)(2,1)S(1)}, u32[]{:S(2)}, u32[]{:S(2)}) collective-permute-start(bf16[4,4,8,2048]{3,2,1,0:T(8,128)(2,1)S(1)} %pad_maximum_fusion.2), channel_id=1, source_target_pairs={{0,4},{4,0},{8,12},{12,8},{16,20},{20,16},{24,28},{28,24},{32,36},... | collective-permute-start | bytes 1572872 | tf_op jit(solution)/shard_map/ppermute | solution.py:44
  (25 other events, 231.4 us)

commit v6 on v2

--- a/solution.py
+++ b/solution.py
@@ -127,7 +127,7 @@
     )
 
 
-BLOCK_REQ = 16
+BLOCK_REQ = 4
 
 
 def cache_kernel(start_ref, len_ref, q_ref, k_ref, v_ref, packed_ref):

time: 159 us -> 161 us (1.013)
  transfers between devices with their start and end apart: 34 -> 34, of which waited for: 26 -> 25; matrix products, arithmetic and copies ran while one was open for 9% -> 9% of each run, Pallas kernels for 0% -> 0%
where the time goes in v6:
time: 161 us; the launch traced here: 160 us
  starting transfers between devices  52.9 us (33%)
  waiting for transfers between devices  39.1 us (24%)
  Pallas kernels  21.8 us (14%)
  matrix products  16.7 us (10%)
  other arithmetic  15.6 us (10%)
  local copies, waits for them, and re-layouts  12.8 us (8%)
    ppermute x34, starting transfers between devices, shifted(): return lax.ppermute(x, level[0], shift_perm(level, d))  52.9 us
    ppermute x34, waiting for transfers between devices, shifted(): return lax.ppermute(x, level[0], shift_perm(level, d))  39.1 us
    pallas_call x1, Pallas kernels, cache_attention(): pl.pallas_call(cache_kernel, out_shape=jax.ShapeDtypeStruct((req, rows, h...  21.8 us
    unnamed x33, local copies, waits for them, and re-layouts  6.88 us
    dot_general x2, matrix products, feed(): jnp.dot(hidden, w_down, preferred_element_type=jnp.float32)  5.7 us
  transfers between devices with their start and end apart: 34, of which 25 were waited for; matrix products, arithmetic and copies ran while one was open for 9% of the time, Pallas kernels for 0%

profile of v6, /device:TPU:1, one launch (start us, length us, event | category | flops | bytes accessed | tf_op | source)
XLA Modules:
  0.0 160.4 jit_solution(10047091631484673411)
XLA Ops:
  3.7 4.0 %copy.65 = bf16[2048,512]{0,1:T(8,128)(2,1)} copy(bf16[2048,512]{1,0:T(8,128)(2,1)} %param.20) | data formatting | bytes 4194304 | tf_op args[6]
  8.1 2.9 %fusion.10 = f32[4,64,8,64]{1,3,2,0:T(8,128)S(1)} fusion(bf16[8,64,2048,1]{2,1,0,3:T(8,128)(2,1)} %bitcast.160, f32[2048]{0:T(1024)S(1)} %convert_element_type.131, f32[4,64]{1,0:T(4,128)S(1)} %add_rsqrt_fusion, bf16[4,64,2048]{2,1,0:T(8,128)(2,1)S(1)} %copy-done.5), kind=kOutput, calls=%fused_computation.18 | convolution fusion | flops 538968064 | bytes 3679232 | tf_op jit(solution)/shard_map/dot_general | solution.py:216
  16.8 21.8 %shard_map.157 = f32[64,32,66]{2,1,0:T(8,128)} custom-call(s32[64]{0:T(128)} %and_select_fusion.start_ref, s32[64]{0:T(128)} %len_ref.1, bf16[64,32,128]{2,1,0:T(8,128)(2,1)} %fusion.12.q_ref, bf16[64,512,128]{2,1,0:T(8,128)(2,1)} %k_ref.1, bf16[64,512,128]{2,1,0:T(8,128)(2,1)} %v_ref.1), custom_call_target="tpu_custom_call" | custom-call | tf_op jit(solution)/shard_map/pallas_call | solution.py:162
  52.7 3.9 %collective-permute-start.3 = (f32[4,2,32,66]{3,2,1,0:T(8,128)S(1)}, f32[4,2,32,66]{3,2,1,0:T(8,128)S(1)}, u32[]{:S(2)}, u32[]{:S(2)}) collective-permute-start(f32[4,2,32,66]{3,2,1,0:T(8,128)S(1)} %get-tuple-element.52), channel_id=1, source_target_pairs={{0,24},{4,28},{8,0},{12,4},{16,8},{20,12},{24,16},{28,20},{32,56},... | collective-permute-start | bytes 202760 | tf_op jit(solution)/shard_map/ppermute | solution.py:44
  57.9 4.4 %collective-permute-done.3 = f32[4,2,32,66]{3,2,1,0:T(8,128)S(1)} collective-permute-done((f32[4,2,32,66]{3,2,1,0:T(8,128)S(1)}, f32[4,2,32,66]{3,2,1,0:T(8,128)S(1)}, u32[]{:S(2)}, u32[]{:S(2)}) %collective-permute-start.3) | collective-permute-done | bytes 67616 | tf_op jit(solution)/shard_map/ppermute | solution.py:44
  63.0 2.8 %collective-permute-done.1 = f32[4,2,32,66]{3,2,1,0:T(8,128)S(1)} collective-permute-done((f32[4,2,32,66]{3,2,1,0:T(8,128)S(1)}, f32[4,2,32,66]{3,2,1,0:T(8,128)S(1)}, u32[]{:S(2)}, u32[]{:S(2)}) %collective-permute-start.1) | collective-permute-done | bytes 67616 | tf_op jit(solution)/shard_map/ppermute | solution.py:44
  67.0 2.5 %collective-permute-start.6 = (f32[2,32,66]{2,1,0:T(8,128)S(1)}, f32[2,32,66]{2,1,0:T(8,128)S(1)}, u32[]{:S(2)}, u32[]{:S(2)}) collective-permute-start(f32[2,32,66]{2,1,0:T(8,128)S(1)} %get-tuple-element.67), channel_id=1, source_target_pairs={{0,96},{4,100},{8,104},{12,108},{16,112},{20,116},{24,120},{28,124... | collective-permute-start | bytes 50696 | tf_op jit(solution)/shard_map/ppermute | solution.py:44
  70.7 3.1 %collective-permute-done.5 = f32[2,32,66]{2,1,0:T(8,128)S(1)} collective-permute-done((f32[2,32,66]{2,1,0:T(8,128)S(1)}, f32[2,32,66]{2,1,0:T(8,128)S(1)}, u32[]{:S(2)}, u32[]{:S(2)}) %collective-permute-start.5) | collective-permute-done | bytes 16928 | tf_op jit(solution)/shard_map/ppermute | solution.py:44
  77.5 2.6 %collective-permute-start.8 = (f32[8,2048]{1,0:T(8,128)S(1)}, f32[8,2048]{1,0:T(8,128)S(1)}, u32[]{:S(2)}, u32[]{:S(2)}) collective-permute-start(f32[8,2048]{1,0:T(8,128)S(1)} %fusion.95), channel_id=1, source_target_pairs={{0,2},{1,3},{2,0},{3,1},{4,6},{5,7},{6,4},{7,5},{8,10},{9,11},{10,... | collective-permute-start | bytes 196616 | tf_op jit(solution)/shard_map/ppermute | solution.py:44
  85.0 2.7 %collective-permute-start.12 = (bf16[8,2048]{1,0:T(8,128)(2,1)S(1)}, bf16[8,2048]{1,0:T(8,128)(2,1)S(1)}, u32[]{:S(2)}, u32[]{:S(2)}) collective-permute-start(bf16[8,2048]{1,0:T(8,128)(2,1)S(1)} %fusion.30), channel_id=1, source_target_pairs={{0,96},{4,100},{8,104},{12,108},{16,112},{20,116},{24,120},{28,124... | collective-permute-start | bytes 98312 | tf_op jit(solution)/shard_map/ppermute | solution.py:44
  89.9 2.7 %collective-permute-start.15 = (bf16[4,8,2048]{2,1,0:T(8,128)(2,1)S(1)}, bf16[4,8,2048]{2,1,0:T(8,128)(2,1)S(1)}, u32[]{:S(2)}, u32[]{:S(2)}) collective-permute-start(bf16[4,8,2048]{2,1,0:T(8,128)(2,1)S(1)} %get-tuple-element.65), channel_id=1, source_target_pairs={{0,24},{4,28},{8,0},{12,4},{16,8},{20,12},{24,16},{28,20},{32,56},... | collective-permute-start | bytes 393224 | tf_op jit(solution)/shard_map/ppermute | solution.py:44
  95.9 6.6 %collective-permute-start.16 = (bf16[4,4,8,2048]{3,2,1,0:T(8,128)(2,1)S(1)}, bf16[4,4,8,2048]{3,2,1,0:T(8,128)(2,1)S(1)}, u32[]{:S(2)}, u32[]{:S(2)}) collective-permute-start(bf16[4,4,8,2048]{3,2,1,0:T(8,128)(2,1)S(1)} %pad_maximum_fusion.1), channel_id=1, source_target_pairs={{0,4},{4,0},{8,12},{12,8},{16,20},{20,16},{24,28},{28,24},{32,36},... | collective-permute-start | bytes 1572872 | tf_op jit(solution)/shard_map/ppermute | solution.py:44
  104.9 2.9 %fusion.55 = f32[128,2048]{1,0:T(8,128)} fusion(bf16[64,2048]{1,0:T(8,128)(2,1)} %param.27, f32[128,64]{0,1:T(8,128)} %fusion.97, bf16[128,2048]{1,0:T(8,128)(2,1)S(1)} %bitcast.164, bf16[64,2048]{1,0:T(8,128)(2,1)} %param.26), kind=kOutput, calls=%fused_computation.145 | convolution fusion | flops 67158016 | bytes 2129920 | tf_op jit(solution)/shard_map/dot_general | solution.py:300
  108.4 2.8 %fusion.4 = f32[128,2048]{1,0:T(8,128)} fusion(bf16[64,2048]{1,0:T(8,128)(2,1)} %param.27, bf16[128,2048]{1,0:T(8,128)(2,1)S(1)} %bitcast.157, bf16[64,2048]{1,0:T(8,128)(2,1)} %param.26, f32[128,64]{0,1:T(8,128)S(1)} %fusion.96), kind=kOutput, calls=%fused_computation.11 | convolution fusion | flops 67158016 | bytes 2129920 | tf_op jit(solution)/shard_map/dot_general | solution.py:300
  113.4 2.4 %collective-permute-start.20 = (bf16[4,8,2048]{2,1,0:T(8,128)(2,1)S(1)}, bf16[4,8,2048]{2,1,0:T(8,128)(2,1)S(1)}, u32[]{:S(2)}, u32[]{:S(2)}) collective-permute-start(bf16[4,8,2048]{2,1,0:T(8,128)(2,1)S(1)} %get-tuple-element.49), channel_id=1, source_target_pairs={{0,24},{4,28},{8,0},{12,4},{16,8},{20,12},{24,16},{28,20},{32,56},... | collective-permute-start | bytes 393224 | tf_op jit(solution)/shard_map/ppermute | solution.py:44
  116.1 3.1 %collective-permute-done.18 = bf16[4,8,2048]{2,1,0:T(8,128)(2,1)S(1)} collective-permute-done((bf16[4,8,2048]{2,1,0:T(8,128)(2,1)S(1)}, bf16[4,8,2048]{2,1,0:T(8,128)(2,1)S(1)}, u32[]{:S(2)}, u32[]{:S(2)}) %collective-permute-start.18) | collective-permute-done | bytes 131104 | tf_op jit(solution)/shard_map/ppermute | solution.py:44
  119.2 2.7 %collective-permute-done.19 = bf16[4,8,2048]{2,1,0:T(8,128)(2,1)S(1)} collective-permute-done((bf16[4,8,2048]{2,1,0:T(8,128)(2,1)S(1)}, bf16[4,8,2048]{2,1,0:T(8,128)(2,1)S(1)}, u32[]{:S(2)}, u32[]{:S(2)}) %collective-permute-start.19) | collective-permute-done | bytes 131104 | tf_op jit(solution)/shard_map/ppermute | solution.py:44
  122.6 2.6 %collective-permute-start.23 = (bf16[8,2048]{1,0:T(8,128)(2,1)S(1)}, bf16[8,2048]{1,0:T(8,128)(2,1)S(1)}, u32[]{:S(2)}, u32[]{:S(2)}) collective-permute-start(bf16[8,2048]{1,0:T(8,128)(2,1)S(1)} %get-tuple-element.62), channel_id=1, source_target_pairs={{0,96},{4,100},{8,104},{12,108},{16,112},{20,116},{24,120},{28,124... | collective-permute-start | bytes 98312 | tf_op jit(solution)/shard_map/ppermute | solution.py:44
  126.4 3.4 %collective-permute-done.22 = bf16[8,2048]{1,0:T(8,128)(2,1)S(1)} collective-permute-done((bf16[8,2048]{1,0:T(8,128)(2,1)S(1)}, bf16[8,2048]{1,0:T(8,128)(2,1)S(1)}, u32[]{:S(2)}, u32[]{:S(2)}) %collective-permute-start.22) | collective-permute-done | bytes 32800 | tf_op jit(solution)/shard_map/ppermute | solution.py:44
  129.9 3.4 %collective-permute-start.25 = (f32[8,2048]{1,0:T(8,128)S(1)}, f32[8,2048]{1,0:T(8,128)S(1)}, u32[]{:S(2)}, u32[]{:S(2)}) collective-permute-start(f32[8,2048]{1,0:T(8,128)S(1)} %fusion.34), channel_id=1, source_target_pairs={{0,2},{1,3},{2,0},{3,1},{4,6},{5,7},{6,4},{7,5},{8,10},{9,11},{10,... | collective-permute-start | bytes 196616 | tf_op jit(solution)/shard_map/ppermute | solution.py:44
  139.6 2.4 %collective-permute-done.28 = bf16[8,2048]{1,0:T(8,128)(2,1)S(1)} collective-permute-done((bf16[8,2048]{1,0:T(8,128)(2,1)S(1)}, bf16[8,2048]{1,0:T(8,128)(2,1)S(1)}, u32[]{:S(2)}, u32[]{:S(2)}) %collective-permute-start.28) | collective-permute-done | bytes 32800 | tf_op jit(solution)/shard_map/ppermute | solution.py:44
  142.6 2.5 %collective-permute-start.30 = (bf16[4,8,2048]{2,1,0:T(8,128)(2,1)S(1)}, bf16[4,8,2048]{2,1,0:T(8,128)(2,1)S(1)}, u32[]{:S(2)}, u32[]{:S(2)}) collective-permute-start(bf16[4,8,2048]{2,1,0:T(8,128)(2,1)S(1)} %get-tuple-element.60), channel_id=1, source_target_pairs={{0,8},{4,12},{8,16},{12,20},{16,24},{20,28},{24,0},{28,4},{32,40},... | collective-permute-start | bytes 393224 | tf_op jit(solution)/shard_map/ppermute | solution.py:44
  145.4 2.3 %collective-permute-done.31 = bf16[4,8,2048]{2,1,0:T(8,128)(2,1)S(1)} collective-permute-done((bf16[4,8,2048]{2,1,0:T(8,128)(2,1)S(1)}, bf16[4,8,2048]{2,1,0:T(8,128)(2,1)S(1)}, u32[]{:S(2)}, u32[]{:S(2)}) %collective-permute-start.31) | collective-permute-done | bytes 131104 | tf_op jit(solution)/shard_map/ppermute | solution.py:44
  149.0 7.9 %collective-permute-start.33 = (bf16[4,4,8,2048]{3,2,1,0:T(8,128)(2,1)S(1)}, bf16[4,4,8,2048]{3,2,1,0:T(8,128)(2,1)S(1)}, u32[]{:S(2)}, u32[]{:S(2)}) collective-permute-start(bf16[4,4,8,2048]{3,2,1,0:T(8,128)(2,1)S(1)} %pad_maximum_fusion.2), channel_id=1, source_target_pairs={{0,4},{4,0},{8,12},{12,8},{16,20},{20,16},{24,28},{28,24},{32,36},... | collective-permute-start | bytes 1572872 | tf_op jit(solution)/shard_map/ppermute | solution.py:44
  (158 shorter events, 60.5 us)
Async XLA Ops:
  40.8 9.9 %collective-permute-start = (f32[4,4,2,32,66]{4,3,2,1,0:T(8,128)}, f32[4,4,2,32,66]{4,3,2,1,0:T(8,128)S(1)}, u32[]{:S(2)}, u32[]{:S(2)}) collective-permute-start(f32[4,4,2,32,66]{4,3,2,1,0:T(8,128)} %get-tuple-element.47), channel_id=1, source_target_pairs={{0,4},{4,0},{8,12},{12,8},{16,20},{20,16},{24,28},{28,24},{32,36},... | collective-permute-start | bytes 811016 | tf_op jit(solution)/shard_map/ppermute | solution.py:44
  52.7 9.6 %collective-permute-start.3 = (f32[4,2,32,66]{3,2,1,0:T(8,128)S(1)}, f32[4,2,32,66]{3,2,1,0:T(8,128)S(1)}, u32[]{:S(2)}, u32[]{:S(2)}) collective-permute-start(f32[4,2,32,66]{3,2,1,0:T(8,128)S(1)} %get-tuple-element.52), channel_id=1, source_target_pairs={{0,24},{4,28},{8,0},{12,4},{16,8},{20,12},{24,16},{28,20},{32,56},... | collective-permute-start | bytes 202760 | tf_op jit(solution)/shard_map/ppermute | solution.py:44
  56.7 6.3 %collective-permute-start.2 = (f32[4,2,32,66]{3,2,1,0:T(8,128)S(1)}, f32[4,2,32,66]{3,2,1,0:T(8,128)S(1)}, u32[]{:S(2)}, u32[]{:S(2)}) collective-permute-start(f32[4,2,32,66]{3,2,1,0:T(8,128)S(1)} %get-tuple-element.53), channel_id=1, source_target_pairs={{0,16},{4,20},{8,24},{12,28},{16,0},{20,4},{24,8},{28,12},{32,48},... | collective-permute-start | bytes 202760 | tf_op jit(solution)/shard_map/ppermute | solution.py:44
  56.7 9.1 %collective-permute-start.1 = (f32[4,2,32,66]{3,2,1,0:T(8,128)S(1)}, f32[4,2,32,66]{3,2,1,0:T(8,128)S(1)}, u32[]{:S(2)}, u32[]{:S(2)}) collective-permute-start(f32[4,2,32,66]{3,2,1,0:T(8,128)S(1)} %get-tuple-element.54), channel_id=1, source_target_pairs={{0,8},{4,12},{8,16},{12,20},{16,24},{20,28},{24,0},{28,4},{32,40},... | collective-permute-start | bytes 202760 | tf_op jit(solution)/shard_map/ppermute | solution.py:44
  69.5 4.3 %collective-permute-start.5 = (f32[2,32,66]{2,1,0:T(8,128)S(1)}, f32[2,32,66]{2,1,0:T(8,128)S(1)}, u32[]{:S(2)}, u32[]{:S(2)}) collective-permute-start(f32[2,32,66]{2,1,0:T(8,128)S(1)} %get-tuple-element.68), channel_id=1, source_target_pairs={{0,64},{4,68},{8,72},{12,76},{16,80},{20,84},{24,88},{28,92},{32,9... | collective-permute-start | bytes 50696 | tf_op jit(solution)/shard_map/ppermute | solution.py:44
  76.2 6.1 %collective-permute-start.9 = (f32[8,2048]{1,0:T(8,128)S(1)}, f32[8,2048]{1,0:T(8,128)S(1)}, u32[]{:S(2)}, u32[]{:S(2)}) collective-permute-start(f32[8,2048]{1,0:T(8,128)S(1)} %fusion.95), channel_id=1, source_target_pairs={{0,1},{1,2},{2,3},{3,0},{4,5},{5,6},{6,7},{7,4},{8,9},{9,10},{10,1... | collective-permute-start | bytes 196616 | tf_op jit(solution)/shard_map/ppermute | solution.py:44
  77.5 5.0 %collective-permute-start.8 = (f32[8,2048]{1,0:T(8,128)S(1)}, f32[8,2048]{1,0:T(8,128)S(1)}, u32[]{:S(2)}, u32[]{:S(2)}) collective-permute-start(f32[8,2048]{1,0:T(8,128)S(1)} %fusion.95), channel_id=1, source_target_pairs={{0,2},{1,3},{2,0},{3,1},{4,6},{5,7},{6,4},{7,5},{8,10},{9,11},{10,... | collective-permute-start | bytes 196616 | tf_op jit(solution)/shard_map/ppermute | solution.py:44
  83.8 4.3 %collective-permute-start.11 = (bf16[8,2048]{1,0:T(8,128)(2,1)S(1)}, bf16[8,2048]{1,0:T(8,128)(2,1)S(1)}, u32[]{:S(2)}, u32[]{:S(2)}) collective-permute-start(bf16[8,2048]{1,0:T(8,128)(2,1)S(1)} %fusion.30), channel_id=1, source_target_pairs={{0,64},{4,68},{8,72},{12,76},{16,80},{20,84},{24,88},{28,92},{32,9... | collective-permute-start | bytes 98312 | tf_op jit(solution)/shard_map/ppermute | solution.py:44
  89.0 5.5 %collective-permute-start.14 = (bf16[4,8,2048]{2,1,0:T(8,128)(2,1)S(1)}, bf16[4,8,2048]{2,1,0:T(8,128)(2,1)S(1)}, u32[]{:S(2)}, u32[]{:S(2)}) collective-permute-start(bf16[4,8,2048]{2,1,0:T(8,128)(2,1)S(1)} %get-tuple-element.65), channel_id=1, source_target_pairs={{0,16},{4,20},{8,24},{12,28},{16,0},{20,4},{24,8},{28,12},{32,48},... | collective-permute-start | bytes 393224 | tf_op jit(solution)/shard_map/ppermute | solution.py:44
  89.9 5.9 %collective-permute-start.13 = (bf16[4,8,2048]{2,1,0:T(8,128)(2,1)S(1)}, bf16[4,8,2048]{2,1,0:T(8,128)(2,1)S(1)}, u32[]{:S(2)}, u32[]{:S(2)}) collective-permute-start(bf16[4,8,2048]{2,1,0:T(8,128)(2,1)S(1)} %get-tuple-element.65), channel_id=1, source_target_pairs={{0,8},{4,12},{8,16},{12,20},{16,24},{20,28},{24,0},{28,4},{32,40},... | collective-permute-start | bytes 393224 | tf_op jit(solution)/shard_map/ppermute | solution.py:44
  89.9 5.9 %collective-permute-start.15 = (bf16[4,8,2048]{2,1,0:T(8,128)(2,1)S(1)}, bf16[4,8,2048]{2,1,0:T(8,128)(2,1)S(1)}, u32[]{:S(2)}, u32[]{:S(2)}) collective-permute-start(bf16[4,8,2048]{2,1,0:T(8,128)(2,1)S(1)} %get-tuple-element.65), channel_id=1, source_target_pairs={{0,24},{4,28},{8,0},{12,4},{16,8},{20,12},{24,16},{28,20},{32,56},... | collective-permute-start | bytes 393224 | tf_op jit(solution)/shard_map/ppermute | solution.py:44
  95.9 8.1 %collective-permute-start.16 = (bf16[4,4,8,2048]{3,2,1,0:T(8,128)(2,1)S(1)}, bf16[4,4,8,2048]{3,2,1,0:T(8,128)(2,1)S(1)}, u32[]{:S(2)}, u32[]{:S(2)}) collective-permute-start(bf16[4,4,8,2048]{3,2,1,0:T(8,128)(2,1)S(1)} %pad_maximum_fusion.1), channel_id=1, source_target_pairs={{0,4},{4,0},{8,12},{12,8},{16,20},{20,16},{24,28},{28,24},{32,36},... | collective-permute-start | bytes 1572872 | tf_op jit(solution)/shard_map/ppermute | solution.py:44
  113.0 6.2 %collective-permute-start.18 = (bf16[4,8,2048]{2,1,0:T(8,128)(2,1)S(1)}, bf16[4,8,2048]{2,1,0:T(8,128)(2,1)S(1)}, u32[]{:S(2)}, u32[]{:S(2)}) collective-permute-start(bf16[4,8,2048]{2,1,0:T(8,128)(2,1)S(1)} %get-tuple-element.48), channel_id=1, source_target_pairs={{0,8},{4,12},{8,16},{12,20},{16,24},{20,28},{24,0},{28,4},{32,40},... | collective-permute-start | bytes 393224 | tf_op jit(solution)/shard_map/ppermute | solution.py:44
  113.4 5.8 %collective-permute-start.20 = (bf16[4,8,2048]{2,1,0:T(8,128)(2,1)S(1)}, bf16[4,8,2048]{2,1,0:T(8,128)(2,1)S(1)}, u32[]{:S(2)}, u32[]{:S(2)}) collective-permute-start(bf16[4,8,2048]{2,1,0:T(8,128)(2,1)S(1)} %get-tuple-element.49), channel_id=1, source_target_pairs={{0,24},{4,28},{8,0},{12,4},{16,8},{20,12},{24,16},{28,20},{32,56},... | collective-permute-start | bytes 393224 | tf_op jit(solution)/shard_map/ppermute | solution.py:44
  115.8 6.2 %collective-permute-start.19 = (bf16[4,8,2048]{2,1,0:T(8,128)(2,1)S(1)}, bf16[4,8,2048]{2,1,0:T(8,128)(2,1)S(1)}, u32[]{:S(2)}, u32[]{:S(2)}) collective-permute-start(bf16[4,8,2048]{2,1,0:T(8,128)(2,1)S(1)} %get-tuple-element.50), channel_id=1, source_target_pairs={{0,16},{4,20},{8,24},{12,28},{16,0},{20,4},{24,8},{28,12},{32,48},... | collective-permute-start | bytes 393224 | tf_op jit(solution)/shard_map/ppermute | solution.py:44
  122.1 4.3 %collective-permute-start.21 = (bf16[8,2048]{1,0:T(8,128)(2,1)S(1)}, bf16[8,2048]{1,0:T(8,128)(2,1)S(1)}, u32[]{:S(2)}, u32[]{:S(2)}) collective-permute-start(bf16[8,2048]{1,0:T(8,128)(2,1)S(1)} %get-tuple-element.61), channel_id=1, source_target_pairs={{0,32},{4,36},{8,40},{12,44},{16,48},{20,52},{24,56},{28,60},{32,6... | collective-permute-start | bytes 98312 | tf_op jit(solution)/shard_map/ppermute | solution.py:44
  125.2 4.6 %collective-permute-start.22 = (bf16[8,2048]{1,0:T(8,128)(2,1)S(1)}, bf16[8,2048]{1,0:T(8,128)(2,1)S(1)}, u32[]{:S(2)}, u32[]{:S(2)}) collective-permute-start(bf16[8,2048]{1,0:T(8,128)(2,1)S(1)} %get-tuple-element.63), channel_id=1, source_target_pairs={{0,64},{4,68},{8,72},{12,76},{16,80},{20,84},{24,88},{28,92},{32,9... | collective-permute-start | bytes 98312 | tf_op jit(solution)/shard_map/ppermute | solution.py:44
  129.8 4.4 %collective-permute-start.26 = (f32[8,2048]{1,0:T(8,128)S(1)}, f32[8,2048]{1,0:T(8,128)S(1)}, u32[]{:S(2)}, u32[]{:S(2)}) collective-permute-start(f32[8,2048]{1,0:T(8,128)S(1)} %fusion.34), channel_id=1, source_target_pairs={{0,1},{1,2},{2,3},{3,0},{4,5},{5,6},{6,7},{7,4},{8,9},{9,10},{10,1... | collective-permute-start | bytes 196616 | tf_op jit(solution)/shard_map/ppermute | solution.py:44
  129.9 5.8 %collective-permute-start.25 = (f32[8,2048]{1,0:T(8,128)S(1)}, f32[8,2048]{1,0:T(8,128)S(1)}, u32[]{:S(2)}, u32[]{:S(2)}) collective-permute-start(f32[8,2048]{1,0:T(8,128)S(1)} %fusion.34), channel_id=1, source_target_pairs={{0,2},{1,3},{2,0},{3,1},{4,6},{5,7},{6,4},{7,5},{8,10},{9,11},{10,... | collective-permute-start | bytes 196616 | tf_op jit(solution)/shard_map/ppermute | solution.py:44
  137.6 4.4 %collective-permute-start.28 = (bf16[8,2048]{1,0:T(8,128)(2,1)S(1)}, bf16[8,2048]{1,0:T(8,128)(2,1)S(1)}, u32[]{:S(2)}, u32[]{:S(2)}) collective-permute-start(bf16[8,2048]{1,0:T(8,128)(2,1)S(1)} %fusion.31), channel_id=1, source_target_pairs={{0,64},{4,68},{8,72},{12,76},{16,80},{20,84},{24,88},{28,92},{32,9... | collective-permute-start | bytes 98312 | tf_op jit(solution)/shard_map/ppermute | solution.py:44
  137.6 4.4 %collective-permute-start.27 = (bf16[8,2048]{1,0:T(8,128)(2,1)S(1)}, bf16[8,2048]{1,0:T(8,128)(2,1)S(1)}, u32[]{:S(2)}, u32[]{:S(2)}) collective-permute-start(bf16[8,2048]{1,0:T(8,128)(2,1)S(1)} %fusion.31), channel_id=1, source_target_pairs={{0,32},{4,36},{8,40},{12,44},{16,48},{20,52},{24,56},{28,60},{32,6... | collective-permute-start | bytes 98312 | tf_op jit(solution)/shard_map/ppermute | solution.py:44
  142.1 5.6 %collective-permute-start.31 = (bf16[4,8,2048]{2,1,0:T(8,128)(2,1)S(1)}, bf16[4,8,2048]{2,1,0:T(8,128)(2,1)S(1)}, u32[]{:S(2)}, u32[]{:S(2)}) collective-permute-start(bf16[4,8,2048]{2,1,0:T(8,128)(2,1)S(1)} %get-tuple-element.60), channel_id=1, source_target_pairs={{0,16},{4,20},{8,24},{12,28},{16,0},{20,4},{24,8},{28,12},{32,48},... | collective-permute-start | bytes 393224 | tf_op jit(solution)/shard_map/ppermute | solution.py:44
  142.6 6.3 %collective-permute-start.30 = (bf16[4,8,2048]{2,1,0:T(8,128)(2,1)S(1)}, bf16[4,8,2048]{2,1,0:T(8,128)(2,1)S(1)}, u32[]{:S(2)}, u32[]{:S(2)}) collective-permute-start(bf16[4,8,2048]{2,1,0:T(8,128)(2,1)S(1)} %get-tuple-element.60), channel_id=1, source_target_pairs={{0,8},{4,12},{8,16},{12,20},{16,24},{20,28},{24,0},{28,4},{32,40},... | collective-permute-start | bytes 393224 | tf_op jit(solution)/shard_map/ppermute | solution.py:44
  149.0 9.4 %collective-permute-start.33 = (bf16[4,4,8,2048]{3,2,1,0:T(8,128)(2,1)S(1)}, bf16[4,4,8,2048]{3,2,1,0:T(8,128)(2,1)S(1)}, u32[]{:S(2)}, u32[]{:S(2)}) collective-permute-start(bf16[4,4,8,2048]{3,2,1,0:T(8,128)(2,1)S(1)} %pad_maximum_fusion.2), channel_id=1, source_target_pairs={{0,4},{4,0},{8,12},{12,8},{16,20},{20,16},{24,28},{28,24},{32,36},... | collective-permute-start | bytes 1572872 | tf_op jit(solution)/shard_map/ppermute | solution.py:44
  (25 other events, 229.2 us)
